TPU v7x, 256 devices: a whole 4x4x8 slice. The times are simulated.
256 devices in a mesh: dp: 4 (over y), ctx: 32 (over x, z_lo, core), tp: 2 (over z_hi).
Axes of the slice: x: 4, y: 4, z: 8 (z_hi: 2, z_lo: 4; z = z_hi * 4 + z_lo), core: 2. Of those that a mesh axis runs over, the one named last changes fastest.
Arguments:
- projected: bfloat16 [4, 3, 4096, 8192], P('dp', None, 'tp', 'ctx'), may hold values from -6 to 6
- cotangent: bfloat16 [4, 4096, 8192], P('dp', None, ('ctx', 'tp')), may hold values from -6 to 6
- short_filter: float32 [3, 3, 4096], P(None, None, 'tp'), may hold values from -3 to 3
- residues: float32 [4096, 16], P('tp'), may hold values from -3 to 3
- decay_rate: float32 [4096, 16], P('tp'), may hold values from 3.0517578e-05 to 0.035
- skip_gain: float32 [4096], P('tp'), may hold values from -1 to 1
Outputs:
- hyena_out: bfloat16 [4, 4096, 8192], P('dp', 'tp', 'ctx')
- input_grad: bfloat16 [4, 3, 4096, 8192], P('dp', None, 'tp', 'ctx')
- residue_grad: float32 [4096, 16], P('tp')
- skip_grad: float32 [4096], P('tp')
All inputs are finite; a program needn't handle non-finite values.
Results may differ from a plain program's by a relative error of at most 0.0076.
Values may be sent and summed in bfloat16 or wider, within the bound.
No kernel may reach another device: no remote copies, remote signals or barrier semaphores. Data moves between devices by JAX's collectives and lax.ppermute only.
A program may use at most 128 MiB of HBM per device.

v0:
```python
from functools import partial
import math

import jax
import jax.numpy as jnp
from jax import lax
from jax.sharding import PartitionSpec as P
from jax.experimental import pallas as pl
from jax.experimental.pallas import tpu as pltpu

exact_mode = lax.Precision.HIGHEST
data_mode = lax.Precision.HIGH


def from_behind(shard, axis, by):
    count = lax.axis_size(axis)
    pairs = [(i, i + by) for i in range(count) if 0 <= i + by < count]
    return lax.ppermute(shard, axis, pairs)


def causal_short(proj_rows, prev_rim, tap_weights):
    rim_width = prev_rim.shape[2]
    token_count = proj_rows.shape[2]
    extended = jnp.concatenate([prev_rim, proj_rows], axis=2).astype(jnp.float32)
    result = tap_weights[:, 0, :, None] * extended[:, :, rim_width : rim_width + token_count]
    for lag_index in range(1, rim_width + 1):
        start_at = rim_width - lag_index
        result = (
            result
            + tap_weights[:, lag_index, :, None] * extended[:, :, start_at : start_at + token_count]
        )
    return result


def anticausal_short(grad_rows, next_rim, tap_weights):
    rim_width = next_rim.shape[2]
    token_count = grad_rows.shape[2]
    extended = jnp.concatenate([grad_rows, next_rim], axis=2).astype(jnp.float32)
    result = tap_weights[:, 0, :, None] * extended[:, :, :token_count]
    for lag_index in range(1, rim_width + 1):
        result = (
            result
            + tap_weights[:, lag_index, :, None]
            * extended[:, :, lag_index : lag_index + token_count]
        )
    return result


def make_tables(rate_rows, block_len):
    offsets = jnp.arange(block_len, dtype=jnp.float32)
    fall_now = jnp.exp(-rate_rows[:, :, None] * offsets)
    rise_now = jnp.exp(rate_rows[:, :, None] * offsets)
    fall_next = jnp.exp(-rate_rows[:, :, None] * (offsets + 1.0))
    fall_tail = jnp.exp(-rate_rows[:, :, None] * (block_len - 1.0 - offsets))
    lower_mask = offsets[:, None] >= offsets[None, :]
    return (fall_now, rise_now, fall_next, fall_tail, lower_mask)


def chain_link(earlier, later):
    return (earlier[0] * later[0], later[0] * earlier[1] + later[1])


def modal_pass(signal, rate_rows, weights, incoming, tables):
    fall_now, rise_now, fall_next, fall_tail, lower_mask = tables
    block_len = fall_now.shape[2]
    chan_count, length = signal.shape
    block_count = length // block_len
    pieces = signal.reshape(chan_count, block_count, block_len)
    kernel = jnp.einsum(
        "cnt,cns->cts", weights[:, :, None] * fall_now, rise_now, precision=exact_mode
    )
    kernel = jnp.where(lower_mask[None], kernel, 0.0)
    inside = jnp.einsum("cts,cbs->cbt", kernel, pieces, precision=data_mode)
    block_ends = jnp.einsum("cns,cbs->cnb", fall_tail, pieces, precision=data_mode)
    span_decay = jnp.exp(-rate_rows * block_len)
    block_mults = jnp.broadcast_to(span_decay[:, :, None], block_ends.shape)
    _, running = lax.associative_scan(chain_link, (block_mults, block_ends), axis=2)
    block_steps = jnp.arange(block_count, dtype=jnp.float32)
    before = jnp.concatenate([jnp.zeros_like(running[:, :, :1]), running[:, :, :-1]], axis=2)
    before = (
        before + jnp.exp(-rate_rows[:, :, None] * block_len * block_steps) * incoming[:, :, None]
    )
    carry_in = jnp.einsum(
        "cnt,cnb->cbt", weights[:, :, None] * fall_next, before, precision=exact_mode
    )
    return ((inside + carry_in).reshape(chan_count, length), before)


def mode_products(signal, adjoint, before, tables):
    fall_now, rise_now, fall_next, fall_tail, lower_mask = tables
    block_len = fall_now.shape[2]
    chan_count, length = signal.shape
    block_count = length // block_len
    pieces = signal.reshape(chan_count, block_count, block_len)
    dual_pieces = adjoint.reshape(chan_count, block_count, block_len)
    crossed = jnp.einsum("cbt,cbs->cts", dual_pieces, pieces, precision=data_mode)
    crossed = jnp.where(lower_mask[None], crossed, 0.0)
    weighted = jnp.einsum("cts,cnt->cns", crossed, fall_now, precision=exact_mode)
    inside = jnp.sum(weighted * rise_now, axis=2)
    carried = jnp.einsum("cbt,cnt->cnb", dual_pieces, fall_next, precision=data_mode)
    return inside + jnp.sum(carried * before, axis=2)


def channel_group(group_items, block_len):
    (
        forward_narrow,
        backward_narrow,
        rate_rows,
        weights,
        gain_rows,
        enter_forward,
        enter_backward,
    ) = group_items
    forward_rows = forward_narrow.astype(jnp.float32)
    backward_rows = backward_narrow.astype(jnp.float32)
    tables = make_tables(rate_rows, block_len)
    carried, before = modal_pass(forward_rows, rate_rows, weights, enter_forward, tables)
    returned, _ = modal_pass(jnp.flip(backward_rows, 1), rate_rows, weights, enter_backward, tables)
    signal = (carried + gain_rows[:, None] * forward_rows).astype(jnp.bfloat16)
    back_signal = (jnp.flip(returned, 1) + gain_rows[:, None] * backward_rows).astype(jnp.bfloat16)
    mode_raw = mode_products(forward_rows, backward_rows, before, tables)
    skip_raw = jnp.sum(backward_rows * forward_rows, axis=1)
    return (signal, back_signal, mode_raw, skip_raw)


def split_pair(values):
    high = values.astype(jnp.bfloat16)
    low = (values - high.astype(jnp.float32)).astype(jnp.bfloat16)
    return high, low


def mat_nn(a, b):
    return jnp.dot(a, b, preferred_element_type=jnp.float32)


def mat_nt(a, b):
    return lax.dot_general(a, b, (((1,), (1,)), ((), ())), preferred_element_type=jnp.float32)


def mat_tn(a, b):
    return lax.dot_general(a, b, (((0,), (0,)), ((), ())), preferred_element_type=jnp.float32)


def wide_nn(a, b_pair):
    a_high, a_low = split_pair(a)
    return mat_nn(a_high, b_pair[0]) + mat_nn(a_high, b_pair[1]) + mat_nn(a_low, b_pair[0])


def shifted(values, by, lanes_rows):
    rows = values.shape[0]
    rolled = pltpu.roll(values, by % rows, 0)
    index = lax.broadcasted_iota(jnp.int32, values.shape, 0)
    keep = (index >= by) if by > 0 else (index < rows + by)
    return jnp.where(keep, rolled, 0.0)


def long_conv_kernel(u_ref, dz_ref, tab_ref, row_ref, z_ref, du_ref, mode_ref, skip_ref):
    chans, blocks, width = u_ref.shape
    modes = tab_ref.shape[2]

    def one_channel(c, carry):
        u_narrow = u_ref[c]
        dz_narrow = dz_ref[c]
        tabs = tab_ref[c]
        rows = row_ref[c]
        fall_end = (tabs[0], tabs[1])
        fall_start = (tabs[2], tabs[3])
        gain_fwd = (tabs[4], tabs[5])
        gain_bwd = (tabs[6], tabs[7])
        gain_lag = (tabs[8], tabs[9])
        rate_row = rows[6:7, :]
        step_row = rows[5:6, :]
        gain = rows[7:8, 0:1]
        lag_ids = lax.broadcasted_iota(jnp.int32, (width, modes), 0).astype(jnp.float32)
        rise = jnp.exp(lag_ids * rate_row)
        toeplitz = wide_nn(rise, gain_lag)
        col = lax.broadcasted_iota(jnp.int32, (width, width), 1)
        row = lax.broadcasted_iota(jnp.int32, (width, width), 0)
        upper = col >= row
        toeplitz = jnp.where(upper, toeplitz, 0.0)
        t_high, t_low = split_pair(toeplitz)
        z_in = mat_nn(u_narrow, t_high) + mat_nn(u_narrow, t_low)
        du_in = mat_nt(dz_narrow, t_high) + mat_nt(dz_narrow, t_low)
        ends = mat_nt(u_narrow, fall_end[0]) + mat_nt(u_narrow, fall_end[1])
        starts = mat_nt(dz_narrow, fall_start[0]) + mat_nt(dz_narrow, fall_start[1])
        fwd_state = ends
        bwd_state = starts
        level = 0
        span = 1
        while span < blocks:
            decay = rows[level : level + 1, :]
            fwd_state = fwd_state + decay * shifted(fwd_state, span, blocks)
            bwd_state = bwd_state + decay * shifted(bwd_state, -span, blocks)
            level += 1
            span *= 2
        state_before = shifted(fwd_state, 1, blocks)
        state_after = shifted(bwd_state, -1, blocks)
        z_carry = wide_nn(state_before, gain_fwd)
        du_carry = wide_nn(state_after, gain_bwd)
        u_wide = u_narrow.astype(jnp.float32)
        dz_wide = dz_narrow.astype(jnp.float32)
        z_ref[c] = (z_in + z_carry + gain * u_wide).astype(z_ref.dtype)
        du_ref[c] = (du_in + du_carry + gain * dz_wide).astype(du_ref.dtype)
        crossed = mat_tn(u_narrow, dz_narrow)
        crossed = jnp.where(upper, crossed, 0.0)
        c_high, c_low = split_pair(crossed)
        weighted = (
            mat_nt(c_high, fall_start[0]) + mat_nt(c_high, fall_start[1]) + mat_nt(c_low, fall_start[0])
        )
        mode_in = jnp.sum(weighted * rise, axis=0, keepdims=True)
        mode_carry = jnp.sum(state_before * starts, axis=0, keepdims=True) * step_row
        mode_ref[c] = mode_in + mode_carry
        skip_ref[c] = jnp.broadcast_to(jnp.sum(u_wide * dz_wide), skip_ref.shape[1:])
        return carry

    lax.fori_loop(0, chans, one_channel, 0)


def long_conv_tables(rate_rows, weight_rows, gain_rows, width, blocks):
    offsets = jnp.arange(width, dtype=jnp.float32)
    rate = rate_rows[:, :, None]
    weight = weight_rows[:, :, None]
    fall_end = jnp.exp(-rate * (width - 1.0 - offsets))
    fall_start = jnp.exp(-rate * offsets)
    gain_fwd = weight * jnp.exp(-rate * (offsets + 1.0))
    gain_bwd = weight * jnp.exp(-rate * (width - offsets))
    gain_lag = weight * jnp.exp(-rate * offsets)
    pairs = []
    for table in (fall_end, fall_start, gain_fwd, gain_bwd, gain_lag):
        high = lax.reduce_precision(table, exponent_bits=8, mantissa_bits=7)
        pairs.extend((high.astype(jnp.bfloat16), (table - high).astype(jnp.bfloat16)))
    tabs = jnp.stack(pairs, axis=1)
    levels = []
    span = 1
    while span < blocks:
        levels.append(jnp.exp(-rate_rows * (width * span)))
        span *= 2
    chan_count, modes = rate_rows.shape
    while len(levels) < 5:
        levels.append(jnp.zeros_like(rate_rows))
    levels.append(jnp.exp(-rate_rows))
    levels.append(rate_rows)
    levels.append(jnp.broadcast_to(gain_rows[:, None], (chan_count, modes)))
    return tabs, jnp.stack(levels, axis=1)


def long_conv(u_blocks, dz_blocks, rate_rows, weight_rows, gain_rows, chans_per_step=8):
    chan_count, blocks, width = u_blocks.shape
    modes = rate_rows.shape[1]
    tabs, rows = long_conv_tables(rate_rows, weight_rows, gain_rows, width, blocks)
    step = min(chans_per_step, chan_count)
    data_spec = pl.BlockSpec((step, blocks, width), lambda i: (i, 0, 0))
    return pl.pallas_call(
        long_conv_kernel,
        grid=(chan_count // step,),
        in_specs=[
            data_spec,
            data_spec,
            pl.BlockSpec((step,) + tabs.shape[1:], lambda i: (i, 0, 0, 0)),
            pl.BlockSpec((step,) + rows.shape[1:], lambda i: (i, 0, 0)),
        ],
        out_specs=[
            data_spec,
            data_spec,
            pl.BlockSpec((step, 1, modes), lambda i: (i, 0, 0)),
            pl.BlockSpec((step, 1, 128), lambda i: (i, 0, 0)),
        ],
        out_shape=[
            jax.ShapeDtypeStruct(u_blocks.shape, jnp.bfloat16),
            jax.ShapeDtypeStruct(u_blocks.shape, jnp.bfloat16),
            jax.ShapeDtypeStruct((chan_count, 1, modes), jnp.float32),
            jax.ShapeDtypeStruct((chan_count, 1, 128), jnp.float32),
        ],
        cost_estimate=pl.CostEstimate(
            flops=chan_count * 34 * width * width * blocks, transcendentals=chan_count * width * modes,
            bytes_accessed=chan_count * blocks * width * 8 + tabs.size * 2,
        ),
    )(u_blocks, dz_blocks, tabs, rows)


def grouped(function, arrays, group_size):
    stacked = tuple(
        (
            item.reshape((item.shape[0] // group_size, group_size) + item.shape[1:])
            for item in arrays
        )
    )
    results = lax.map(function, stacked)
    return tuple(
        (item.reshape((item.shape[0] * item.shape[1],) + item.shape[2:]) for item in results)
    )


def on_device(projected, cotangent, short_filter, residues, decay_rate, skip_gain):
    proj_rows = projected[0]
    token_count = proj_rows.shape[2]
    chans_tp = proj_rows.shape[1]
    rim_width = short_filter.shape[1] - 1
    grad_out = lax.all_to_all(cotangent[0], "tp", split_axis=0, concat_axis=1, tiled=True).astype(
        jnp.float32
    )
    prev_rim = from_behind(proj_rows[:, :, token_count - rim_width :], "ctx", 1)
    featured = lax.optimization_barrier(
        causal_short(proj_rows, prev_rim, short_filter).astype(jnp.bfloat16)
    )
    query_feat = featured[0].astype(jnp.float32)
    key_feat = featured[1].astype(jnp.float32)
    value_feat = featured[2].astype(jnp.float32)
    product = (key_feat * value_feat).astype(jnp.bfloat16)
    adjoint = (grad_out * query_feat).astype(jnp.bfloat16)
    ctx_count = lax.axis_size("ctx")
    token_total = token_count * ctx_count * lax.axis_size("dp")
    weight_all = residues * jnp.sqrt(2.0 * decay_rate)
    product_all, adjoint_all = (
        lax.all_to_all(product, "ctx", split_axis=0, concat_axis=1, tiled=True),
        lax.all_to_all(adjoint, "ctx", split_axis=0, concat_axis=1, tiled=True),
    )
    chan_count = chans_tp // ctx_count
    chan_start = lax.axis_index("ctx") * chan_count
    rate_rows = lax.dynamic_slice_in_dim(decay_rate, chan_start, chan_count, 0)
    weight_rows = lax.dynamic_slice_in_dim(weight_all, chan_start, chan_count, 0)
    gain_rows = lax.dynamic_slice_in_dim(skip_gain, chan_start, chan_count, 0)
    length = product_all.shape[1]
    block_len = math.gcd(256, length)
    block_count = length // block_len
    conv_blocks, back_blocks, mode_part, skip_part = long_conv(
        product_all.reshape(chan_count, block_count, block_len),
        adjoint_all.reshape(chan_count, block_count, block_len),
        rate_rows,
        weight_rows,
        gain_rows,
    )
    conv_rows = conv_blocks.reshape(chan_count, length)
    back_rows = back_blocks.reshape(chan_count, length)
    mode_part = mode_part[:, 0, :]
    skip_part = skip_part[:, 0, 0]
    signal, back_signal = (
        lax.all_to_all(conv_rows, "ctx", split_axis=1, concat_axis=0, tiled=True),
        lax.all_to_all(back_rows, "ctx", split_axis=1, concat_axis=0, tiled=True),
    )
    grad_scale = 1.0 / math.sqrt(token_total)
    local_grads = jnp.concatenate(
        [mode_part * jnp.sqrt(2.0 * rate_rows) * grad_scale, skip_part[:, None] * grad_scale], axis=1
    )
    local_grads = lax.psum(local_grads, "dp")
    spread = jnp.broadcast_to(local_grads[None], (ctx_count,) + local_grads.shape)
    gathered = lax.all_to_all(spread, "ctx", split_axis=0, concat_axis=0, tiled=True)
    gathered = gathered.reshape(chans_tp, local_grads.shape[1])
    residue_grad = gathered[:, : mode_part.shape[1]]
    skip_grad = gathered[:, mode_part.shape[1]]
    conv_wide = signal.astype(jnp.float32)
    back_wide = back_signal.astype(jnp.float32)
    hyena_out = (query_feat * conv_wide).astype(jnp.bfloat16)
    feature_grad = jnp.stack(
        [grad_out * conv_wide, back_wide * value_feat, back_wide * key_feat]
    ).astype(jnp.bfloat16)
    next_rim = from_behind(feature_grad[:, :, :rim_width], "ctx", -1)
    input_grad = anticausal_short(feature_grad, next_rim, short_filter).astype(jnp.bfloat16)
    return (hyena_out[None], input_grad[None], residue_grad, skip_grad)


def solution(mesh):
    placed = (
        P("dp", None, "tp", "ctx"),
        P("dp", None, ("ctx", "tp")),
        P(None, None, "tp"),
        P("tp", None),
        P("tp", None),
        P("tp"),
    )
    return jax.shard_map(
        on_device,
        mesh=mesh,
        in_specs=placed,
        out_specs=(P("dp", "tp", "ctx"), P("dp", None, "tp", "ctx"), P("tp", None), P("tp")),
        check_vma=False,
    )
```

profile of v0, /device:TPU:1, one launch (start us, length us, event | category | flops | bytes accessed | tf_op | source)
XLA Modules:
  0.0 279.1 jit_solution(6335337867705288098)
XLA Ops:
  0.7 3.2 %slice.71 = bf16[3,2048,2]{2,1,0:T(8,128)(2,1)} slice(bf16[3,2048,256]{2,1,0:T(8,128)(2,1)} %bitcast.63), slice={[0:3], [0:2048], [254:256]} | slice | bytes 49152 | tf_op jit(solution)/shard_map/slice | solution.py:302
  3.9 1.7 copy.98
  5.6 4.9 %collective-permute-start = (bf16[3,2048,2]{1,2,0:T(2,128)(2,1)S(1)}, bf16[3,2048,2]{1,2,0:T(2,128)(2,1)S(1)}, u32[]{:S(2)}, u32[]{:S(2)}) collective-permute-start(bf16[3,2048,2]{1,2,0:T(2,128)(2,1)S(1)} %copy.98), channel_id=1, source_target_pairs={{0,2},{2,4},{4,6},{6,8},{8,10},{10,12},{12,14},{14,16},{16,18},{18... | collective-permute-start | bytes 73736 | tf_op jit(solution)/shard_map/ppermute | solution.py:18
  10.5 7.3 %all-to-all-start.1 = ((bf16[2,2048,128]{2,1,0:T(8,128)(2,1)}), bf16[2,2048,128]{2,1,0:T(8,128)(2,1)}, u32[]{:S(2)}, u32[]{:S(2)}) async-start(bf16[2,2048,128]{2,1,0:T(8,128)(2,1)} %bitcast.67), calls=%async_computation.1 | async-start | bytes 2097152 | tf_op jit(solution)/shard_map/all_to_all | solution.py:299
  20.5 3.3 %maximum_convert_fusion = f32[3,2048,258]{2,1,0:T(8,128)S(1)} fusion(bf16[3,2048,256]{2,1,0:T(8,128)(2,1)S(1)} %bitcast.64, bf16[3,2048,2]{2,1,0:T(8,128)(2,1)} %copy.99), kind=kLoop, calls=%fused_computation.12 | loop fusion | flops 6340608 | bytes 9510912 | tf_op jit(solution)/shard_map/convert_element_type | solution.py:24
  23.8 6.4 %fusion.4 = bf16[3,2048,256]{2,1,0:T(8,128)(2,1)S(1)} fusion(f32[3,2048,258]{2,1,0:T(8,128)S(1)} %maximum_convert_fusion, f32[3,2048]{1,0:T(4,128)S(1)} %get-tuple-element.28, f32[3,2048]{1,0:T(4,128)S(1)} %get-tuple-element.29, f32[3,2048]{1,0:T(4,128)S(1)} %bitcast.71), kind=kLoop, calls=%fused_computation.8 | loop fusion | flops 9437184 | bytes 22093824 | tf_op jit(solution)/shard_map/convert_element_type | solution.py:304
  31.5 14.9 %all-to-all-done.1 = bf16[2,2048,128]{2,1,0:T(8,128)(2,1)} async-done(((bf16[2,2048,128]{2,1,0:T(8,128)(2,1)}), bf16[2,2048,128]{2,1,0:T(8,128)(2,1)}, u32[]{:S(2)}, u32[]{:S(2)}) %all-to-all-start.1) | async-done | bytes 1048608 | tf_op jit(solution)/shard_map/all_to_all | solution.py:299
  46.4 6.3 %all-to-all-start = ((bf16[32,64,256]{2,1,0:T(8,128)(2,1)}), bf16[32,64,256]{2,1,0:T(8,128)(2,1)}, u32[]{:S(2)}, u32[]{:S(2)}) async-start(bf16[32,64,256]{2,1,0:T(8,128)(2,1)} %bitcast.65), calls=%async_computation | async-start | bytes 2097152 | tf_op jit(solution)/shard_map/all_to_all | solution.py:315
  57.8 8.6 %copy.101 = f32[2048,2,128]{2,1,0:T(2,128)} copy(f32[2048,2,128]{2,0,1:T(8,128)S(1)} %convert_bitcast_fusion) | data formatting | bytes 4194304 | tf_op jit(solution)/shard_map/convert_element_type | solution.py:299
  66.3 4.0 %reshape.221 = f32[32,64,256]{2,1,0:T(8,128)} reshape(f32[2048,2,128]{2,1,0:T(2,128)} %copy.101) | data formatting | bytes 4194304 | tf_op jit(solution)/shard_map/convert_element_type | solution.py:299
  70.3 3.5 %multiply_convert_fusion = bf16[32,64,256]{2,1,0:T(8,128)(2,1)} fusion(f32[32,64,256]{2,1,0:T(8,128)} %reshape.221, f32[32,64,256]{2,1,0:T(8,128)} %bitcast.62), kind=kLoop, calls=%fused_computation.26 | loop fusion | flops 1048576 | bytes 5242880 | tf_op jit(solution)/shard_map/convert_element_type | solution.py:310
  73.8 6.8 %all-to-all-done = bf16[32,64,256]{2,1,0:T(8,128)(2,1)} async-done(((bf16[32,64,256]{2,1,0:T(8,128)(2,1)}), bf16[32,64,256]{2,1,0:T(8,128)(2,1)}, u32[]{:S(2)}, u32[]{:S(2)}) %all-to-all-start) | async-done | bytes 1048608 | tf_op jit(solution)/shard_map/all_to_all | solution.py:315
  80.7 4.6 %all-to-all-start.2 = ((bf16[32,64,256]{2,1,0:T(8,128)(2,1)}), bf16[32,64,256]{2,1,0:T(8,128)(2,1)}, u32[]{:S(2)}, u32[]{:S(2)}) async-start(bf16[32,64,256]{2,1,0:T(8,128)(2,1)} %multiply_convert_fusion), calls=%async_computation.2 | async-start | bytes 2097152 | tf_op jit(solution)/shard_map/all_to_all | solution.py:316
  96.8 2.8 copy.132
  99.6 13.7 %all-to-all-done.2 = bf16[32,64,256]{2,1,0:T(8,128)(2,1)} async-done(((bf16[32,64,256]{2,1,0:T(8,128)(2,1)}), bf16[32,64,256]{2,1,0:T(8,128)(2,1)}, u32[]{:S(2)}, u32[]{:S(2)}) %all-to-all-start.2) | async-done | bytes 1048608 | tf_op jit(solution)/shard_map/all_to_all | solution.py:316
  113.3 2.8 copy.131
  116.0 60.7 %shard_map.93 = (bf16[64,32,256]{2,1,0:T(8,128)(2,1)}, bf16[64,32,256]{2,1,0:T(8,128)(2,1)}, f32[64,1,16]{2,1,0:T(1,128)}, f32[64,1,128]{2,1,0:T(1,128)}) custom-call(bf16[64,32,256]{2,1,0:T(8,128)(2,1)} %bitcast.68, bf16[64,32,256]{2,1,0:T(8,128)(2,1)} %bitcast.69, bf16[64,10,16,256]{3,2,1,0:T(8,128)(2,1)} %fusion.18.tab_ref, f32[64,8,16]{2,1,0:T(8,128)} %stack.52.row_ref), custom_call_target="tpu_custom_call" | custom-call | flops 4563402752 | bytes 9437184 | tf_op jit(solution)/shard_map/pallas_call | solution.py:253
  176.8 2.8 copy.112
  179.6 4.7 %all-to-all-start.3 = ((bf16[64,32,256]{2,0,1:T(8,128)(2,1)}), bf16[64,32,256]{2,0,1:T(8,128)(2,1)}, u32[]{:S(2)}, u32[]{:S(2)}) async-start(bf16[64,32,256]{2,0,1:T(8,128)(2,1)} %copy.112), calls=%async_computation.3 | async-start | bytes 2097152 | tf_op jit(solution)/shard_map/all_to_all | solution.py:338
  184.3 2.8 copy.114
  187.0 25.3 %all-to-all-done.3 = bf16[64,32,256]{2,0,1:T(8,128)(2,1)} async-done(((bf16[64,32,256]{2,0,1:T(8,128)(2,1)}), bf16[64,32,256]{2,0,1:T(8,128)(2,1)}, u32[]{:S(2)}, u32[]{:S(2)}) %all-to-all-start.3) | async-done | bytes 1048608 | tf_op jit(solution)/shard_map/all_to_all | solution.py:338
  212.3 4.6 %all-to-all-start.4 = ((bf16[64,32,256]{2,0,1:T(8,128)(2,1)}), bf16[64,32,256]{2,0,1:T(8,128)(2,1)}, u32[]{:S(2)}, u32[]{:S(2)}) async-start(bf16[64,32,256]{2,0,1:T(8,128)(2,1)} %copy.114), calls=%async_computation.4 | async-start | bytes 2097152 | tf_op jit(solution)/shard_map/all_to_all | solution.py:339
  216.9 3.9 %reshape.224 = f32[1,2048,256]{2,1,0:T(8,128)} reshape(f32[2048,2,128]{2,1,0:T(2,128)} %copy.101) | data formatting | bytes 4194304 | tf_op jit(solution)/shard_map/convert_element_type | solution.py:299
  221.4 14.9 %psum.7 = f32[64,17]{0,1:T(8,128)S(1)} all-reduce(f32[64,17]{0,1:T(8,128)S(1)} %pad_maximum_fusion.2), channel_id=1, replica_groups=mesh['dp'=4,'ctx'=32,'tp'=2] {'dp'}, use_global_device_ids=true, to_apply=%region_0.0 | all-reduce | flops 1088 | bytes 8704 | tf_op jit(solution)/shard_map/psum | solution.py:345
  237.2 7.7 %all-to-all-done.4 = bf16[64,32,256]{2,0,1:T(8,128)(2,1)} async-done(((bf16[64,32,256]{2,0,1:T(8,128)(2,1)}), bf16[64,32,256]{2,0,1:T(8,128)(2,1)}, u32[]{:S(2)}, u32[]{:S(2)}) %all-to-all-start.4) | async-done | bytes 1048608 | tf_op jit(solution)/shard_map/all_to_all | solution.py:339
  244.9 3.9 %all-to-all-start.5 = ((f32[32,1,1088]{2,1,0:T(1,128)}), f32[32,1,1088]{2,1,0:T(1,128)S(1)}, u32[]{:S(2)}, u32[]{:S(2)}) async-start(f32[32,1,1088]{2,1,0:T(1,128)} %reshape.227), calls=%async_computation.5 | async-start | bytes 294912 | tf_op jit(solution)/shard_map/all_to_all | solution.py:347
  248.8 4.1 %fusion.9 = (bf16[1,2048,256]{2,1,0:T(8,128)(2,1)S(1)}, bf16[1,2048,256]{2,1,0:T(8,128)(2,1)S(1)}, bf16[1,2048,256]{2,1,0:T(8,128)(2,1)}, bf16[1,2048,256]{2,1,0:T(8,128)(2,1)S(1)}) fusion(bf16[64,32,256]{2,0,1:T(8,128)(2,1)} %all-to-all-done.4, bf16[3,2048,256]{2,1,0:T(8,128)(2,1)S(1)} %fusion.4, bf16[64,32,256]{2,0,1:T(8,128)(2,1)} %all-to-all-done.3, ...), kind=kLoop, calls=%fused_computation.20 | loop fusion | flops 6815744 | bytes 11534336 | tf_op jit(solution)/shard_map/convert.10
  255.9 2.5 copy.115
  258.4 2.2 collective-permute-start.1
  266.9 2.3 copy.116
  269.2 2.6 maximum_convert_fusion.1
  271.9 7.3 %fusion.6 = bf16[1,3,2048,256]{3,2,1,0:T(8,128)(2,1)} fusion(f32[3,2048,258]{2,1,0:T(8,128)S(1)} %maximum_convert_fusion.1, f32[3,2048]{1,0:T(4,128)S(1)} %copy-done.8, f32[3,2048]{1,0:T(4,128)S(1)} %copy-done.10, f32[3,2048]{1,0:T(4,128)S(1)} %bitcast.72), kind=kLoop, calls=%fused_computation.14 | loop fusion | flops 9437184 | bytes 22093824 | tf_op jit(solution)/shard_map/broadcast_in_dim | solution.py:359
  (76 shorter events, 31.3 us)
Async XLA Ops:
  0.6 19.8 %copy-start.6 = (bf16[1,3,2048,256]{3,2,1,0:T(8,128)(2,1)S(1)}, bf16[1,3,2048,256]{3,2,1,0:T(8,128)(2,1)}, u32[]{:S(2)}) copy-start(bf16[1,3,2048,256]{3,2,1,0:T(8,128)(2,1)} %param.6) | copy-start | bytes 9437188
  0.6 17.2 %copy-start.13 = (f32[3,3,2048]{2,1,0:T(4,128)S(1)}, f32[3,3,2048]{2,1,0:T(4,128)}, u32[]{:S(2)}) copy-start(f32[3,3,2048]{2,1,0:T(4,128)} %param.8) | copy-start | bytes 221188
  5.6 13.3 %collective-permute-start = (bf16[3,2048,2]{1,2,0:T(2,128)(2,1)S(1)}, bf16[3,2048,2]{1,2,0:T(2,128)(2,1)S(1)}, u32[]{:S(2)}, u32[]{:S(2)}) collective-permute-start(bf16[3,2048,2]{1,2,0:T(2,128)(2,1)S(1)} %copy.98), channel_id=1, source_target_pairs={{0,2},{2,4},{4,6},{6,8},{8,10},{10,12},{12,14},{14,16},{16,18},{18... | collective-permute-start | bytes 73736 | tf_op jit(solution)/shard_map/ppermute | solution.py:18
  10.5 35.8 %all-to-all-start.1 = ((bf16[2,2048,128]{2,1,0:T(8,128)(2,1)}), bf16[2,2048,128]{2,1,0:T(8,128)(2,1)}, u32[]{:S(2)}, u32[]{:S(2)}) async-start(bf16[2,2048,128]{2,1,0:T(8,128)(2,1)} %bitcast.67), calls=%async_computation.1 | async-start | bytes 2097152 | tf_op jit(solution)/shard_map/all_to_all | solution.py:299
  17.9 5.9 %copy-start.7 = (f32[3,2048]{1,0:T(4,128)}, f32[3,2048]{1,0:T(4,128)S(1)}, u32[]{:S(2)}) copy-start(f32[3,2048]{1,0:T(4,128)S(1)} %get-tuple-element.28) | copy-start | bytes 73732
  17.9 5.9 %copy-start.9 = (f32[3,2048]{1,0:T(4,128)}, f32[3,2048]{1,0:T(4,128)S(1)}, u32[]{:S(2)}) copy-start(f32[3,2048]{1,0:T(4,128)S(1)} %get-tuple-element.29) | copy-start | bytes 73732
  18.9 4.9 %copy-start.11 = (f32[3,1,2048]{2,0,1:T(4,128)}, f32[3,1,2048]{2,0,1:T(4,128)S(1)}, u32[]{:S(2)}) copy-start(f32[3,1,2048]{2,0,1:T(4,128)S(1)} %copy.133) | copy-start | bytes 73732
  46.4 34.3 %all-to-all-start = ((bf16[32,64,256]{2,1,0:T(8,128)(2,1)}), bf16[32,64,256]{2,1,0:T(8,128)(2,1)}, u32[]{:S(2)}, u32[]{:S(2)}) async-start(bf16[32,64,256]{2,1,0:T(8,128)(2,1)} %bitcast.65), calls=%async_computation | async-start | bytes 2097152 | tf_op jit(solution)/shard_map/all_to_all | solution.py:315
  80.7 32.6 %all-to-all-start.2 = ((bf16[32,64,256]{2,1,0:T(8,128)(2,1)}), bf16[32,64,256]{2,1,0:T(8,128)(2,1)}, u32[]{:S(2)}, u32[]{:S(2)}) async-start(bf16[32,64,256]{2,1,0:T(8,128)(2,1)} %multiply_convert_fusion), calls=%async_computation.2 | async-start | bytes 2097152 | tf_op jit(solution)/shard_map/all_to_all | solution.py:316
  179.6 41.2 %copy-start.14 = (f32[64,1,16]{2,1,0:T(1,128)S(1)}, f32[64,1,16]{2,1,0:T(1,128)}, u32[]{:S(2)}) copy-start(f32[64,1,16]{2,1,0:T(1,128)} %get-tuple-element.10) | copy-start | bytes 12292
  179.6 41.3 %copy-start.15 = (f32[64,1,128]{2,1,0:T(1,128)S(1)}, f32[64,1,128]{2,1,0:T(1,128)}, u32[]{:S(2)}) copy-start(f32[64,1,128]{2,1,0:T(1,128)} %get-tuple-element.11) | copy-start | bytes 98308
  179.6 32.7 %all-to-all-start.3 = ((bf16[64,32,256]{2,0,1:T(8,128)(2,1)}), bf16[64,32,256]{2,0,1:T(8,128)(2,1)}, u32[]{:S(2)}, u32[]{:S(2)}) async-start(bf16[64,32,256]{2,0,1:T(8,128)(2,1)} %copy.112), calls=%async_computation.3 | async-start | bytes 2097152 | tf_op jit(solution)/shard_map/all_to_all | solution.py:338
  212.3 32.6 %all-to-all-start.4 = ((bf16[64,32,256]{2,0,1:T(8,128)(2,1)}), bf16[64,32,256]{2,0,1:T(8,128)(2,1)}, u32[]{:S(2)}, u32[]{:S(2)}) async-start(bf16[64,32,256]{2,0,1:T(8,128)(2,1)} %copy.114), calls=%async_computation.4 | async-start | bytes 2097152 | tf_op jit(solution)/shard_map/all_to_all | solution.py:339
  244.9 15.7 %all-to-all-start.5 = ((f32[32,1,1088]{2,1,0:T(1,128)}), f32[32,1,1088]{2,1,0:T(1,128)S(1)}, u32[]{:S(2)}, u32[]{:S(2)}) async-start(f32[32,1,1088]{2,1,0:T(1,128)} %reshape.227), calls=%async_computation.5 | async-start | bytes 294912 | tf_op jit(solution)/shard_map/all_to_all | solution.py:347
  252.8 0.9 copy-start
  252.8 1.3 copy-start.2
  252.8 1.6 copy-start.4
  255.9 13.3 %copy-start.1 = (bf16[1,2048,256]{2,1,0:T(8,128)(2,1)S(1)}, bf16[1,2048,256]{2,1,0:T(8,128)(2,1)}, u32[]{:S(2)}) copy-start(bf16[1,2048,256]{2,1,0:T(8,128)(2,1)} %copy-done) | copy-start | bytes 3145732
  255.9 13.3 %copy-start.3 = (bf16[1,2048,256]{2,1,0:T(8,128)(2,1)S(1)}, bf16[1,2048,256]{2,1,0:T(8,128)(2,1)}, u32[]{:S(2)}) copy-start(bf16[1,2048,256]{2,1,0:T(8,128)(2,1)} %copy-done.2) | copy-start | bytes 3145732
  255.9 13.3 %copy-start.5 = (bf16[1,2048,256]{2,1,0:T(8,128)(2,1)S(1)}, bf16[1,2048,256]{2,1,0:T(8,128)(2,1)}, u32[]{:S(2)}) copy-start(bf16[1,2048,256]{2,1,0:T(8,128)(2,1)} %copy-done.4) | copy-start | bytes 3145732
  258.4 8.5 %collective-permute-start.1 = (bf16[3,2048,2]{1,2,0:T(2,128)(2,1)}, bf16[3,2048,2]{1,2,0:T(2,128)(2,1)}, u32[]{:S(2)}, u32[]{:S(2)}) collective-permute-start(bf16[3,2048,2]{1,2,0:T(2,128)(2,1)} %copy.115), channel_id=1, source_target_pairs={{2,0},{4,2},{6,4},{8,6},{10,8},{12,10},{14,12},{16,14},{18,16},{20... | collective-permute-start | bytes 73736 | tf_op jit(solution)/shard_map/ppermute | solution.py:18
  269.2 2.6 copy-start.8
  269.2 2.6 copy-start.10
  269.2 2.6 copy-start.12
where the time goes:
time: 283 us; the launch traced here: 279 us
  waiting for transfers between devices  68.4 us (24%)
  Pallas kernels  60.7 us (21%)
  local copies, waits for them, and re-layouts  48.3 us (17%)
  other arithmetic  47.3 us (17%)
  starting transfers between devices  38.5 us (14%)
  blocking collectives  14.9 us (5%)
    pallas_call x1, Pallas kernels, long_conv(): pl.pallas_call(long_conv_kernel, grid=(chan_count // step,), in_specs=[da...  60.7 us
    all_to_all x1, waiting for transfers between devices, on_device(): lax.all_to_all(conv_rows, 'ctx', split_axis=1, concat_axis=0, tiled=True)  25.3 us
    convert_element_type x3, local copies, waits for them, and re-layouts, on_device(): lax.all_to_all(cotangent[0], 'tp', split_axis=0, concat_axis=1, tiled=True)  16.4 us
    psum x1, blocking collectives, on_device(): local_grads = lax.psum(local_grads, 'dp')  14.9 us
    all_to_all x1, waiting for transfers between devices, on_device(): lax.all_to_all(cotangent[0], 'tp', split_axis=0, concat_axis=1, tiled=True)  14.9 us
    all_to_all x1, waiting for transfers between devices, on_device(): lax.all_to_all(adjoint, 'ctx', split_axis=0, concat_axis=1, tiled=True)  13.7 us
    unnamed x9, other arithmetic  10.3 us
    all_to_all x1, waiting for transfers between devices, on_device(): lax.all_to_all(back_rows, 'ctx', split_axis=1, concat_axis=0, tiled=True)  7.67 us
  transfers between devices with their start and end apart: 8, of which 5 were waited for; matrix products, arithmetic and copies ran while one was open for 26% of the time, Pallas kernels for 0%

commit v1 on v0

--- a/solution.py
+++ b/solution.py
@@ -311,10 +311,10 @@
     ctx_count = lax.axis_size("ctx")
     token_total = token_count * ctx_count * lax.axis_size("dp")
     weight_all = residues * jnp.sqrt(2.0 * decay_rate)
-    product_all, adjoint_all = (
-        lax.all_to_all(product, "ctx", split_axis=0, concat_axis=1, tiled=True),
-        lax.all_to_all(adjoint, "ctx", split_axis=0, concat_axis=1, tiled=True),
-    )
+    both_all = lax.all_to_all(
+        jnp.stack([product, adjoint]), "ctx", split_axis=1, concat_axis=2, tiled=True
+    )
+    product_all, adjoint_all = both_all[0], both_all[1]
     chan_count = chans_tp // ctx_count
     chan_start = lax.axis_index("ctx") * chan_count
     rate_rows = lax.dynamic_slice_in_dim(decay_rate, chan_start, chan_count, 0)
@@ -334,18 +334,25 @@
     back_rows = back_blocks.reshape(chan_count, length)
     mode_part = mode_part[:, 0, :]
     skip_part = skip_part[:, 0, 0]
-    signal, back_signal = (
-        lax.all_to_all(conv_rows, "ctx", split_axis=1, concat_axis=0, tiled=True),
-        lax.all_to_all(back_rows, "ctx", split_axis=1, concat_axis=0, tiled=True),
-    )
+    both_back = lax.all_to_all(
+        jnp.stack([conv_rows, back_rows]), "ctx", split_axis=2, concat_axis=1, tiled=True
+    )
+    signal, back_signal = both_back[0], both_back[1]
     grad_scale = 1.0 / math.sqrt(token_total)
     local_grads = jnp.concatenate(
         [mode_part * jnp.sqrt(2.0 * rate_rows) * grad_scale, skip_part[:, None] * grad_scale], axis=1
     )
-    local_grads = lax.psum(local_grads, "dp")
-    spread = jnp.broadcast_to(local_grads[None], (ctx_count,) + local_grads.shape)
+    dp_count = lax.axis_size("dp")
+    grad_cols = local_grads.shape[1]
+    pieces = local_grads.reshape(dp_count, chan_count // dp_count, grad_cols)
+    pieces = lax.all_to_all(pieces, "dp", split_axis=0, concat_axis=0, tiled=True)
+    summed = jnp.sum(pieces, axis=0)
+    spread = jnp.broadcast_to(summed[None], (ctx_count,) + summed.shape)
     gathered = lax.all_to_all(spread, "ctx", split_axis=0, concat_axis=0, tiled=True)
-    gathered = gathered.reshape(chans_tp, local_grads.shape[1])
+    spread = jnp.broadcast_to(gathered[None], (dp_count,) + gathered.shape)
+    gathered = lax.all_to_all(spread, "dp", split_axis=0, concat_axis=0, tiled=True)
+    gathered = gathered.reshape(dp_count, ctx_count, chan_count // dp_count, grad_cols)
+    gathered = jnp.swapaxes(gathered, 0, 1).reshape(chans_tp, grad_cols)
     residue_grad = gathered[:, : mode_part.shape[1]]
     skip_grad = gathered[:, mode_part.shape[1]]
     conv_wide = signal.astype(jnp.float32)

time: 283 us -> 380 us (1.34)
  local copies, waits for them, and re-layouts: 48.3 us -> 111 us
  waiting for transfers between devices: 68.4 us -> 100 us
  other arithmetic: 47.3 us -> 58.2 us
  blocking collectives: 14.9 us -> 8.14 us
    another operation x0 -> x6, local copies, waits for them, and re-layouts: none -> 38.7 us  [the longest x4 23.1 us: on_device(): jnp.stack([conv_rows, back_rows])]
    all_to_all x4 -> x3, waiting for transfers between devices: 53.4 us -> 83.1 us  [the longest x1 47.8 us: on_device(): lax.all_to_all(jnp.stack([conv_rows, back_rows]), 'ctx', split_axis=2, co...]
    unnamed x38 -> x42, local copies, waits for them, and re-layouts: 3.73 us -> 26.4 us
    psum x1 -> x0, blocking collectives: 14.9 us -> none  [on_device(): local_grads = lax.psum(local_grads, 'dp')]
    unnamed x9 -> x10, other arithmetic: 10.3 us -> 23.7 us
    all_to_all x0 -> x1, blocking collectives: none -> 8.14 us  [on_device(): lax.all_to_all(pieces, 'dp', split_axis=0, concat_axis=0, tiled=True)]
    pallas_call x2 -> x0, local copies, waits for them, and re-layouts: 5.55 us -> none  [long_conv(): pl.pallas_call(long_conv_kernel, grid=(chan_count // step,), in_specs=[da...]
    all_to_all x2 -> x3, local copies, waits for them, and re-layouts: 5.55 us -> 10.6 us  [the longest x1 7.33 us: on_device(): lax.all_to_all(jnp.stack([conv_rows, back_rows]), 'ctx', split_axis=2, co...]
  transfers between devices with their start and end apart: 8 -> 7, of which waited for: 5 -> 3; matrix products, arithmetic and copies ran while one was open for 26% -> 22% of each run, Pallas kernels for 0% -> 0%
where the time goes in v1:
time: 380 us; the launch traced here: 378 us
  local copies, waits for them, and re-layouts  111 us (29%)
  waiting for transfers between devices  100 us (26%)
  Pallas kernels  60.8 us (16%)
  other arithmetic  58.2 us (15%)
  starting transfers between devices  38.9 us (10%)
  blocking collectives  8.14 us (2%)
    pallas_call x1, Pallas kernels, long_conv(): pl.pallas_call(long_conv_kernel, grid=(chan_count // step,), in_specs=[da...  60.8 us
    all_to_all x1, waiting for transfers between devices, on_device(): lax.all_to_all(jnp.stack([conv_rows, back_rows]), 'ctx', split_axis=2, co...  47.8 us
    all_to_all x1, waiting for transfers between devices, on_device(): lax.all_to_all(jnp.stack([product, adjoint]), 'ctx', split_axis=1, concat...  35.3 us
    unnamed x42, local copies, waits for them, and re-layouts  26.4 us
    unnamed x10, other arithmetic  23.7 us
    another operation x4, local copies, waits for them, and re-layouts, on_device(): jnp.stack([conv_rows, back_rows])  23.1 us
    all_to_all x1, waiting for transfers between devices, on_device(): lax.all_to_all(cotangent[0], 'tp', split_axis=0, concat_axis=1, tiled=True)  17.1 us
    another operation x1, local copies, waits for them, and re-layouts, on_device(): jnp.stack([product, adjoint])  14.2 us
  transfers between devices with their start and end apart: 7, of which 3 were waited for; matrix products, arithmetic and copies ran while one was open for 22% of the time, Pallas kernels for 0%

profile of v1, /device:TPU:1, one launch (start us, length us, event | category | flops | bytes accessed | tf_op | source)
XLA Modules:
  0.0 377.9 jit_solution(10842363660852969470)
XLA Ops:
  0.7 3.2 slice.91
  5.6 4.9 %collective-permute-start = (bf16[3,2048,2]{1,2,0:T(2,128)(2,1)S(1)}, bf16[3,2048,2]{1,2,0:T(2,128)(2,1)S(1)}, u32[]{:S(2)}, u32[]{:S(2)}) collective-permute-start(bf16[3,2048,2]{1,2,0:T(2,128)(2,1)S(1)} %copy.102), channel_id=1, source_target_pairs={{0,2},{2,4},{4,6},{6,8},{8,10},{10,12},{12,14},{14,16},{16,18},{18... | collective-permute-start | bytes 73736 | tf_op jit(solution)/shard_map/ppermute | solution.py:18
  10.5 7.3 %all-to-all-start = ((bf16[2,2048,128]{2,1,0:T(8,128)(2,1)}), bf16[2,2048,128]{2,1,0:T(8,128)(2,1)}, u32[]{:S(2)}, u32[]{:S(2)}) async-start(bf16[2,2048,128]{2,1,0:T(8,128)(2,1)} %bitcast.70), calls=%async_computation | async-start | bytes 2097152 | tf_op jit(solution)/shard_map/all_to_all | solution.py:299
  19.6 3.3 maximum_convert_fusion
  22.9 6.4 %fusion.4 = bf16[3,2048,256]{2,1,0:T(8,128)(2,1)S(1)} fusion(f32[3,2048,258]{2,1,0:T(8,128)S(1)} %maximum_convert_fusion, f32[3,2048]{1,0:T(4,128)S(1)} %get-tuple-element.38, f32[3,2048]{1,0:T(4,128)S(1)} %get-tuple-element.39, f32[3,2048]{1,0:T(4,128)S(1)} %bitcast.72), kind=kLoop, calls=%fused_computation.8 | loop fusion | flops 9437184 | bytes 22093824 | tf_op jit(solution)/shard_map/convert_element_type | solution.py:304
  29.3 17.1 %all-to-all-done = bf16[2,2048,128]{2,1,0:T(8,128)(2,1)} async-done(((bf16[2,2048,128]{2,1,0:T(8,128)(2,1)}), bf16[2,2048,128]{2,1,0:T(8,128)(2,1)}, u32[]{:S(2)}, u32[]{:S(2)}) %all-to-all-start) | async-done | bytes 1048608 | tf_op jit(solution)/shard_map/all_to_all | solution.py:299
  47.7 8.6 %copy.104 = f32[2048,2,128]{2,1,0:T(2,128)} copy(f32[2048,2,128]{2,0,1:T(8,128)S(1)} %convert_bitcast_fusion) | data formatting | bytes 4194304 | tf_op jit(solution)/shard_map/convert_element_type | solution.py:299
  56.3 3.9 %reshape.206 = f32[1,2048,256]{2,1,0:T(8,128)} reshape(f32[2048,2,128]{2,1,0:T(2,128)} %copy.104) | data formatting | bytes 4194304 | tf_op jit(solution)/shard_map/convert_element_type | solution.py:299
  60.2 2.0 fusion.10
  62.4 14.2 %copy.105 = bf16[2,2048,256]{2,0,1:T(2,128)(2,1)} copy(bf16[2,2048,256]{2,1,0:T(8,128)(2,1)S(1)} %pad_maximum_fusion.1) | data formatting | bytes 4194304 | tf_op jit(solution)/shard_map/stack | solution.py:315
  76.6 6.3 %all-to-all-start.1 = ((bf16[2,2048,256]{2,0,1:T(2,128)(2,1)}), bf16[2,2048,256]{2,0,1:T(2,128)(2,1)}, u32[]{:S(2)}, u32[]{:S(2)}) async-start(bf16[2,2048,256]{2,0,1:T(2,128)(2,1)} %copy.105), calls=%async_computation.1 | async-start | bytes 4194304 | tf_op jit(solution)/shard_map/all_to_all | solution.py:314
  97.5 35.3 %all-to-all-done.1 = bf16[2,2048,256]{2,0,1:T(2,128)(2,1)} async-done(((bf16[2,2048,256]{2,0,1:T(2,128)(2,1)}), bf16[2,2048,256]{2,0,1:T(2,128)(2,1)}, u32[]{:S(2)}, u32[]{:S(2)}) %all-to-all-start.1) | async-done | bytes 2097184 | tf_op jit(solution)/shard_map/all_to_all | solution.py:314
  132.8 2.8 copy.140
  137.0 60.8 %shard_map.93 = (bf16[64,32,256]{2,1,0:T(8,128)(2,1)}, bf16[64,32,256]{2,1,0:T(8,128)(2,1)}, f32[64,1,16]{2,1,0:T(1,128)}, f32[64,1,128]{2,1,0:T(1,128)}) custom-call(bf16[64,32,256]{2,1,0:T(8,128)(2,1)} %get-tuple-element.25.u_ref, bf16[64,32,256]{2,1,0:T(8,128)(2,1)} %get-tuple-element.24.dz_ref, bf16[64,10,16,256]{3,2,1,0:T(8,128)(2,1)} %fusion.19.tab_ref, ...), custom_call_target="tpu_custom_call" | custom-call | flops 4563402752 | bytes 9437184 | tf_op jit(solution)/shard_map/pallas_call | solution.py:253
  199.6 8.1 %all_to_all.58 = f32[4,1,272]{2,1,0:T(1,128)S(1)} all-to-all(f32[4,1,272]{2,1,0:T(1,128)S(1)} %reshape.211), channel_id=1, replica_groups=mesh['dp'=4,'ctx'=32,'tp'=2] {'dp'}, dimensions={0} | all-to-all | bytes 8704 | tf_op jit(solution)/shard_map/all_to_all | solution.py:348
  209.8 5.9 %all-to-all-start.4 = ((f32[32,1,272]{2,1,0:T(1,128)}), f32[32,1,272]{2,1,0:T(1,128)S(1)}, u32[]{:S(2)}, u32[]{:S(2)}) async-start(f32[32,1,272]{2,1,0:T(1,128)} %reshape.213), calls=%async_computation.4 | async-start | bytes 98304 | tf_op jit(solution)/shard_map/all_to_all | solution.py:351
  215.8 2.3 stack_reshape.6
  218.1 9.2 %copy.117 = bf16[1,64,8192]{1,0,2:T(2,128)(2,1)} copy(bf16[1,64,8192]{2,1,0:T(8,128)(2,1)} %stack_reshape.6) | data formatting | bytes 2097152 | tf_op jit(solution)/shard_map/stack;reshape | solution.py:338
  227.3 2.3 stack_reshape.7
  229.7 9.2 %copy.118 = bf16[1,64,8192]{1,0,2:T(2,128)(2,1)} copy(bf16[1,64,8192]{2,1,0:T(8,128)(2,1)} %stack_reshape.7) | data formatting | bytes 2097152 | tf_op jit(solution)/shard_map/stack;reshape | solution.py:338
  242.8 3.5 all-to-all-start.5
  246.4 13.3 %fusion.30 = bf16[8192,2,64]{2,1,0:T(2,128)(2,1)} fusion(bf16[1,64,8192]{1,0,2:T(2,128)(2,1)} %copy.118, bf16[1,64,8192]{1,0,2:T(2,128)(2,1)} %copy.117), kind=kLoop, calls=%fused_computation.85 | loop fusion | flops 4194304 | bytes 4194304
  259.7 9.8 %reshape.209 = bf16[32,2,16384]{2,1,0:T(2,128)(2,1)} reshape(bf16[8192,2,64]{2,1,0:T(2,128)(2,1)} %fusion.30) | data formatting | bytes 4194304
  269.6 7.8 %all-to-all-start.2 = ((bf16[32,2,16384]{2,1,0:T(2,128)(2,1)}), bf16[32,2,16384]{2,1,0:T(2,128)(2,1)}, u32[]{:S(2)}, u32[]{:S(2)}) async-start(bf16[32,2,16384]{2,1,0:T(2,128)(2,1)} %reshape.209), calls=%async_computation.2 | async-start | bytes 4194304 | tf_op jit(solution)/shard_map/all_to_all | solution.py:337
  279.4 47.8 %all-to-all-done.2 = bf16[32,2,16384]{2,1,0:T(2,128)(2,1)} async-done(((bf16[32,2,16384]{2,1,0:T(2,128)(2,1)}), bf16[32,2,16384]{2,1,0:T(2,128)(2,1)}, u32[]{:S(2)}, u32[]{:S(2)}) %all-to-all-start.2) | async-done | bytes 2097184 | tf_op jit(solution)/shard_map/all_to_all | solution.py:337
  327.2 9.8 %reshape.210 = bf16[8192,2,64]{2,1,0:T(2,128)(2,1)} reshape(bf16[32,2,16384]{2,1,0:T(2,128)(2,1)} %all-to-all-done.2) | data formatting | bytes 4194304
  336.9 7.3 %copy.131 = bf16[2,64,32,256]{3,2,1,0:T(8,128)(2,1)} copy(bf16[2,64,32,256]{1,0,3,2:T(2,128)(2,1)} %bitcast.65) | data formatting | bytes 4194304 | tf_op jit(solution)/shard_map/all_to_all | solution.py:337
  355.5 3.1 collective-permute-start.1
  360.4 2.4 copy.126
  362.9 2.2 reshape.205
  368.0 2.6 maximum_convert_fusion.1
  370.6 7.3 %fusion.6 = bf16[1,3,2048,256]{3,2,1,0:T(8,128)(2,1)} fusion(f32[3,2048,258]{2,1,0:T(8,128)S(1)} %maximum_convert_fusion.1, f32[3,2048]{1,0:T(4,128)S(1)} %copy-done.9, f32[3,2048]{1,0:T(4,128)S(1)} %copy-done.11, f32[3,2048]{1,0:T(4,128)S(1)} %bitcast.73), kind=kLoop, calls=%fused_computation.15 | loop fusion | flops 9437184 | bytes 22093824 | tf_op jit(solution)/shard_map/broadcast_in_dim | solution.py:366
  (89 shorter events, 46.7 us)
Async XLA Ops:
  0.6 18.9 %copy-start.7 = (bf16[1,3,2048,256]{3,2,1,0:T(8,128)(2,1)S(1)}, bf16[1,3,2048,256]{3,2,1,0:T(8,128)(2,1)}, u32[]{:S(2)}) copy-start(bf16[1,3,2048,256]{3,2,1,0:T(8,128)(2,1)} %param.6) | copy-start | bytes 9437188
  0.6 17.2 %copy-start.14 = (f32[3,3,2048]{2,1,0:T(4,128)S(1)}, f32[3,3,2048]{2,1,0:T(4,128)}, u32[]{:S(2)}) copy-start(f32[3,3,2048]{2,1,0:T(4,128)} %param.8) | copy-start | bytes 221188
  5.6 12.4 %collective-permute-start = (bf16[3,2048,2]{1,2,0:T(2,128)(2,1)S(1)}, bf16[3,2048,2]{1,2,0:T(2,128)(2,1)S(1)}, u32[]{:S(2)}, u32[]{:S(2)}) collective-permute-start(bf16[3,2048,2]{1,2,0:T(2,128)(2,1)S(1)} %copy.102), channel_id=1, source_target_pairs={{0,2},{2,4},{4,6},{6,8},{8,10},{10,12},{12,14},{14,16},{16,18},{18... | collective-permute-start | bytes 73736 | tf_op jit(solution)/shard_map/ppermute | solution.py:18
  10.5 35.8 %all-to-all-start = ((bf16[2,2048,128]{2,1,0:T(8,128)(2,1)}), bf16[2,2048,128]{2,1,0:T(8,128)(2,1)}, u32[]{:S(2)}, u32[]{:S(2)}) async-start(bf16[2,2048,128]{2,1,0:T(8,128)(2,1)} %bitcast.70), calls=%async_computation | async-start | bytes 2097152 | tf_op jit(solution)/shard_map/all_to_all | solution.py:299
  17.9 5.0 %copy-start.8 = (f32[3,2048]{1,0:T(4,128)}, f32[3,2048]{1,0:T(4,128)S(1)}, u32[]{:S(2)}) copy-start(f32[3,2048]{1,0:T(4,128)S(1)} %get-tuple-element.38) | copy-start | bytes 73732
  17.9 5.0 %copy-start.10 = (f32[3,2048]{1,0:T(4,128)}, f32[3,2048]{1,0:T(4,128)S(1)}, u32[]{:S(2)}) copy-start(f32[3,2048]{1,0:T(4,128)S(1)} %get-tuple-element.39) | copy-start | bytes 73732
  18.0 4.9 %copy-start.12 = (f32[3,1,2048]{2,0,1:T(4,128)}, f32[3,1,2048]{2,0,1:T(4,128)S(1)}, u32[]{:S(2)}) copy-start(f32[3,1,2048]{2,0,1:T(4,128)S(1)} %copy.141) | copy-start | bytes 73732
  76.6 56.2 %all-to-all-start.1 = ((bf16[2,2048,256]{2,0,1:T(2,128)(2,1)}), bf16[2,2048,256]{2,0,1:T(2,128)(2,1)}, u32[]{:S(2)}, u32[]{:S(2)}) async-start(bf16[2,2048,256]{2,0,1:T(2,128)(2,1)} %copy.105), calls=%async_computation.1 | async-start | bytes 4194304 | tf_op jit(solution)/shard_map/all_to_all | solution.py:314
  209.8 29.0 %all-to-all-start.4 = ((f32[32,1,272]{2,1,0:T(1,128)}), f32[32,1,272]{2,1,0:T(1,128)S(1)}, u32[]{:S(2)}, u32[]{:S(2)}) async-start(f32[32,1,272]{2,1,0:T(1,128)} %reshape.213), calls=%async_computation.4 | async-start | bytes 98304 | tf_op jit(solution)/shard_map/all_to_all | solution.py:351
  242.8 26.7 %all-to-all-start.5 = ((f32[4,1,8704]{2,1,0:T(1,128)}), f32[4,1,8704]{2,1,0:T(1,128)S(1)}, u32[]{:S(2)}, u32[]{:S(2)}) async-start(f32[4,1,8704]{2,1,0:T(1,128)} %reshape.215), calls=%async_computation.5 | async-start | bytes 278528 | tf_op jit(solution)/shard_map/all_to_all | solution.py:353
  269.6 57.6 %all-to-all-start.2 = ((bf16[32,2,16384]{2,1,0:T(2,128)(2,1)}), bf16[32,2,16384]{2,1,0:T(2,128)(2,1)}, u32[]{:S(2)}, u32[]{:S(2)}) async-start(bf16[32,2,16384]{2,1,0:T(2,128)(2,1)} %reshape.209), calls=%async_computation.2 | async-start | bytes 4194304 | tf_op jit(solution)/shard_map/all_to_all | solution.py:337
  346.3 2.5 copy-start
  350.5 1.0 copy-start.1
  350.5 1.3 copy-start.3
  350.5 1.6 copy-start.5
  353.6 14.4 %copy-start.2 = (bf16[1,2048,256]{2,1,0:T(8,128)(2,1)S(1)}, bf16[1,2048,256]{2,1,0:T(8,128)(2,1)}, u32[]{:S(2)}) copy-start(bf16[1,2048,256]{2,1,0:T(8,128)(2,1)} %copy-done.1) | copy-start | bytes 3145732
  353.6 14.4 %copy-start.4 = (bf16[1,2048,256]{2,1,0:T(8,128)(2,1)S(1)}, bf16[1,2048,256]{2,1,0:T(8,128)(2,1)}, u32[]{:S(2)}) copy-start(bf16[1,2048,256]{2,1,0:T(8,128)(2,1)} %copy-done.3) | copy-start | bytes 3145732
  353.6 14.4 %copy-start.6 = (bf16[1,2048,256]{2,1,0:T(8,128)(2,1)S(1)}, bf16[1,2048,256]{2,1,0:T(8,128)(2,1)}, u32[]{:S(2)}) copy-start(bf16[1,2048,256]{2,1,0:T(8,128)(2,1)} %copy-done.5) | copy-start | bytes 3145732
  355.5 10.9 %collective-permute-start.1 = (bf16[3,2048,2]{1,2,0:T(2,128)(2,1)S(1)}, bf16[3,2048,2]{1,2,0:T(2,128)(2,1)S(1)}, u32[]{:S(2)}, u32[]{:S(2)}) collective-permute-start(bf16[3,2048,2]{1,2,0:T(2,128)(2,1)S(1)} %copy.122), channel_id=1, source_target_pairs={{2,0},{4,2},{6,4},{8,6},{10,8},{12,10},{14,12},{16,14},{18,16},{20... | collective-permute-start | bytes 73736 | tf_op jit(solution)/shard_map/ppermute | solution.py:18
  368.0 2.6 copy-start.9
  368.0 2.6 copy-start.11
  368.0 2.6 copy-start.13

commit v2 on v0

--- a/solution.py
+++ b/solution.py
@@ -154,33 +154,40 @@
     return jnp.where(keep, rolled, 0.0)
 
 
-def long_conv_kernel(u_ref, dz_ref, tab_ref, row_ref, z_ref, du_ref, mode_ref, skip_ref):
+def long_conv_kernel(u_ref, dz_ref, krow_ref, tab_ref, row_ref, z_ref, du_ref, mode_ref, skip_ref):
     chans, blocks, width = u_ref.shape
     modes = tab_ref.shape[2]
+    col = lax.broadcasted_iota(jnp.int32, (width, width), 1)
+    row = lax.broadcasted_iota(jnp.int32, (width, width), 0)
+    upper = col >= row
+    lower = col <= row
+    lag_ids = lax.broadcasted_iota(jnp.int32, (width, modes), 0).astype(jnp.float32)
 
     def one_channel(c, carry):
         u_narrow = u_ref[c]
         dz_narrow = dz_ref[c]
         tabs = tab_ref[c]
         rows = row_ref[c]
+        krow = krow_ref[c]
         fall_end = (tabs[0], tabs[1])
         fall_start = (tabs[2], tabs[3])
         gain_fwd = (tabs[4], tabs[5])
         gain_bwd = (tabs[6], tabs[7])
-        gain_lag = (tabs[8], tabs[9])
         rate_row = rows[6:7, :]
         step_row = rows[5:6, :]
         gain = rows[7:8, 0:1]
-        lag_ids = lax.broadcasted_iota(jnp.int32, (width, modes), 0).astype(jnp.float32)
-        rise = jnp.exp(lag_ids * rate_row)
-        toeplitz = wide_nn(rise, gain_lag)
-        col = lax.broadcasted_iota(jnp.int32, (width, width), 1)
-        row = lax.broadcasted_iota(jnp.int32, (width, width), 0)
-        upper = col >= row
-        toeplitz = jnp.where(upper, toeplitz, 0.0)
-        t_high, t_low = split_pair(toeplitz)
-        z_in = mat_nn(u_narrow, t_high) + mat_nn(u_narrow, t_low)
-        du_in = mat_nt(dz_narrow, t_high) + mat_nt(dz_narrow, t_low)
+        ahead = pltpu.roll(jnp.broadcast_to(krow[0:1, :], (width, width)), 0, 1, stride=1, stride_axis=0)
+        ahead = jnp.where(upper, ahead, 0.0)
+        behind = pltpu.roll(jnp.broadcast_to(krow[1:2, :], (width, width)), 1, 1, stride=1, stride_axis=0)
+        behind = jnp.where(lower, behind, 0.0)
+        a_high, a_low = split_pair(ahead)
+        b_high, b_low = split_pair(behind)
+        z_in = mat_nn(
+            jnp.concatenate([u_narrow, u_narrow], axis=1), jnp.concatenate([a_high, a_low], axis=0)
+        )
+        du_in = mat_nn(
+            jnp.concatenate([dz_narrow, dz_narrow], axis=1), jnp.concatenate([b_high, b_low], axis=0)
+        )
         ends = mat_nt(u_narrow, fall_end[0]) + mat_nt(u_narrow, fall_end[1])
         starts = mat_nt(dz_narrow, fall_start[0]) + mat_nt(dz_narrow, fall_start[1])
         fwd_state = ends
@@ -201,6 +208,7 @@
         dz_wide = dz_narrow.astype(jnp.float32)
         z_ref[c] = (z_in + z_carry + gain * u_wide).astype(z_ref.dtype)
         du_ref[c] = (du_in + du_carry + gain * dz_wide).astype(du_ref.dtype)
+        rise = jnp.exp(lag_ids * rate_row)
         crossed = mat_tn(u_narrow, dz_narrow)
         crossed = jnp.where(upper, crossed, 0.0)
         c_high, c_low = split_pair(crossed)
@@ -213,7 +221,7 @@
         skip_ref[c] = jnp.broadcast_to(jnp.sum(u_wide * dz_wide), skip_ref.shape[1:])
         return carry
 
-    lax.fori_loop(0, chans, one_channel, 0)
+    lax.fori_loop(0, chans, one_channel, 0, unroll=8)
 
 
 def long_conv_tables(rate_rows, weight_rows, gain_rows, width, blocks):
@@ -224,9 +232,8 @@
     fall_start = jnp.exp(-rate * offsets)
     gain_fwd = weight * jnp.exp(-rate * (offsets + 1.0))
     gain_bwd = weight * jnp.exp(-rate * (width - offsets))
-    gain_lag = weight * jnp.exp(-rate * offsets)
     pairs = []
-    for table in (fall_end, fall_start, gain_fwd, gain_bwd, gain_lag):
+    for table in (fall_end, fall_start, gain_fwd, gain_bwd):
         high = lax.reduce_precision(table, exponent_bits=8, mantissa_bits=7)
         pairs.extend((high.astype(jnp.bfloat16), (table - high).astype(jnp.bfloat16)))
     tabs = jnp.stack(pairs, axis=1)
@@ -241,13 +248,15 @@
     levels.append(jnp.exp(-rate_rows))
     levels.append(rate_rows)
     levels.append(jnp.broadcast_to(gain_rows[:, None], (chan_count, modes)))
-    return tabs, jnp.stack(levels, axis=1)
+    lag_kernel = jnp.sum(weight * fall_start, axis=1)
+    krow = jnp.stack([lag_kernel, jnp.flip(lag_kernel, axis=1)], axis=1)
+    return tabs, jnp.stack(levels, axis=1), krow
 
 
 def long_conv(u_blocks, dz_blocks, rate_rows, weight_rows, gain_rows, chans_per_step=8):
     chan_count, blocks, width = u_blocks.shape
     modes = rate_rows.shape[1]
-    tabs, rows = long_conv_tables(rate_rows, weight_rows, gain_rows, width, blocks)
+    tabs, rows, krow = long_conv_tables(rate_rows, weight_rows, gain_rows, width, blocks)
     step = min(chans_per_step, chan_count)
     data_spec = pl.BlockSpec((step, blocks, width), lambda i: (i, 0, 0))
     return pl.pallas_call(
@@ -256,6 +265,7 @@
         in_specs=[
             data_spec,
             data_spec,
+            pl.BlockSpec((step,) + krow.shape[1:], lambda i: (i, 0, 0)),
             pl.BlockSpec((step,) + tabs.shape[1:], lambda i: (i, 0, 0, 0)),
             pl.BlockSpec((step,) + rows.shape[1:], lambda i: (i, 0, 0)),
         ],
@@ -275,7 +285,7 @@
             flops=chan_count * 34 * width * width * blocks, transcendentals=chan_count * width * modes,
             bytes_accessed=chan_count * blocks * width * 8 + tabs.size * 2,
         ),
-    )(u_blocks, dz_blocks, tabs, rows)
+    )(u_blocks, dz_blocks, krow, tabs, rows)
 
 
 def grouped(function, arrays, group_size):

time: 283 us -> 250 us (0.88)
  Pallas kernels: 60.7 us -> 28.2 us
    pallas_call x1, Pallas kernels: 60.7 us -> 28.2 us  [long_conv(): pl.pallas_call(long_conv_kernel, grid=(chan_count // step,), in_specs=[da...]
    all_to_all x1, waiting for transfers between devices: 25.3 us -> 7.66 us  [on_device(): lax.all_to_all(conv_rows, 'ctx', split_axis=1, concat_axis=0, tiled=True)]
    all_to_all x1, waiting for transfers between devices: 7.67 us -> 25.2 us  [on_device(): lax.all_to_all(back_rows, 'ctx', split_axis=1, concat_axis=0, tiled=True)]
    unnamed x9 -> x7, other arithmetic: 10.3 us -> 7.91 us
  transfers between devices with their start and end apart: 8 -> 8, of which waited for: 5 -> 5; matrix products, arithmetic and copies ran while one was open for 26% -> 29% of each run, Pallas kernels for 0% -> 0%
where the time goes in v2:
time: 250 us; the launch traced here: 247 us
  waiting for transfers between devices  67.9 us (27%)
  local copies, waits for them, and re-layouts  49.3 us (20%)
  other arithmetic  46.7 us (19%)
  starting transfers between devices  38.7 us (15%)
  Pallas kernels  28.2 us (11%)
  blocking collectives  14.9 us (6%)
    pallas_call x1, Pallas kernels, long_conv(): pl.pallas_call(long_conv_kernel, grid=(chan_count // step,), in_specs=[da...  28.2 us
    all_to_all x1, waiting for transfers between devices, on_device(): lax.all_to_all(back_rows, 'ctx', split_axis=1, concat_axis=0, tiled=True)  25.2 us
    convert_element_type x3, local copies, waits for them, and re-layouts, on_device(): lax.all_to_all(cotangent[0], 'tp', split_axis=0, concat_axis=1, tiled=True)  16.3 us
    all_to_all x1, waiting for transfers between devices, on_device(): lax.all_to_all(cotangent[0], 'tp', split_axis=0, concat_axis=1, tiled=True)  15.8 us
    psum x1, blocking collectives, on_device(): local_grads = lax.psum(local_grads, 'dp')  14.9 us
    all_to_all x1, waiting for transfers between devices, on_device(): lax.all_to_all(adjoint, 'ctx', split_axis=0, concat_axis=1, tiled=True)  12.3 us
    unnamed x7, other arithmetic  7.91 us
    all_to_all x1, waiting for transfers between devices, on_device(): lax.all_to_all(conv_rows, 'ctx', split_axis=1, concat_axis=0, tiled=True)  7.66 us
  transfers between devices with their start and end apart: 8, of which 5 were waited for; matrix products, arithmetic and copies ran while one was open for 29% of the time, Pallas kernels for 0%

profile of v2, /device:TPU:1, one launch (start us, length us, event | category | flops | bytes accessed | tf_op | source)
XLA Modules:
  0.0 246.7 jit_solution(12211641710646303532)
XLA Ops:
  0.7 3.2 %slice.71 = bf16[3,2048,2]{2,1,0:T(8,128)(2,1)} slice(bf16[3,2048,256]{2,1,0:T(8,128)(2,1)} %bitcast.63), slice={[0:3], [0:2048], [254:256]} | slice | bytes 49152 | tf_op jit(solution)/shard_map/slice | solution.py:312
  5.6 4.9 %collective-permute-start = (bf16[3,2048,2]{1,2,0:T(2,128)(2,1)S(1)}, bf16[3,2048,2]{1,2,0:T(2,128)(2,1)S(1)}, u32[]{:S(2)}, u32[]{:S(2)}) collective-permute-start(bf16[3,2048,2]{1,2,0:T(2,128)(2,1)S(1)} %copy.107), channel_id=1, source_target_pairs={{0,2},{2,4},{4,6},{6,8},{8,10},{10,12},{12,14},{14,16},{16,18},{18... | collective-permute-start | bytes 73736 | tf_op jit(solution)/shard_map/ppermute | solution.py:18
  10.5 7.3 %all-to-all-start.1 = ((bf16[2,2048,128]{2,1,0:T(8,128)(2,1)}), bf16[2,2048,128]{2,1,0:T(8,128)(2,1)}, u32[]{:S(2)}, u32[]{:S(2)}) async-start(bf16[2,2048,128]{2,1,0:T(8,128)(2,1)} %bitcast.67), calls=%async_computation.1 | async-start | bytes 2097152 | tf_op jit(solution)/shard_map/all_to_all | solution.py:309
  19.6 3.3 %maximum_convert_fusion = f32[3,2048,258]{2,1,0:T(8,128)S(1)} fusion(bf16[3,2048,256]{2,1,0:T(8,128)(2,1)S(1)} %bitcast.64, bf16[3,2048,2]{2,1,0:T(8,128)(2,1)} %copy.108), kind=kLoop, calls=%fused_computation.12 | loop fusion | flops 6340608 | bytes 9510912 | tf_op jit(solution)/shard_map/convert_element_type | solution.py:24
  22.9 6.4 %fusion.4 = bf16[3,2048,256]{2,1,0:T(8,128)(2,1)S(1)} fusion(f32[3,2048,258]{2,1,0:T(8,128)S(1)} %maximum_convert_fusion, f32[3,2048]{1,0:T(4,128)S(1)} %get-tuple-element.28, f32[3,2048]{1,0:T(4,128)S(1)} %get-tuple-element.29, f32[3,2048]{1,0:T(4,128)S(1)} %bitcast.71), kind=kLoop, calls=%fused_computation.8 | loop fusion | flops 9437184 | bytes 22093824 | tf_op jit(solution)/shard_map/convert_element_type | solution.py:314
  30.6 15.8 %all-to-all-done.1 = bf16[2,2048,128]{2,1,0:T(8,128)(2,1)} async-done(((bf16[2,2048,128]{2,1,0:T(8,128)(2,1)}), bf16[2,2048,128]{2,1,0:T(8,128)(2,1)}, u32[]{:S(2)}, u32[]{:S(2)}) %all-to-all-start.1) | async-done | bytes 1048608 | tf_op jit(solution)/shard_map/all_to_all | solution.py:309
  46.4 6.3 %all-to-all-start = ((bf16[32,64,256]{2,1,0:T(8,128)(2,1)}), bf16[32,64,256]{2,1,0:T(8,128)(2,1)}, u32[]{:S(2)}, u32[]{:S(2)}) async-start(bf16[32,64,256]{2,1,0:T(8,128)(2,1)} %bitcast.65), calls=%async_computation | async-start | bytes 2097152 | tf_op jit(solution)/shard_map/all_to_all | solution.py:325
  57.7 8.6 %copy.110 = f32[2048,2,128]{2,1,0:T(2,128)} copy(f32[2048,2,128]{2,0,1:T(8,128)S(1)} %convert_bitcast_fusion) | data formatting | bytes 4194304 | tf_op jit(solution)/shard_map/convert_element_type | solution.py:309
  66.2 3.9 %reshape.206 = f32[32,64,256]{2,1,0:T(8,128)} reshape(f32[2048,2,128]{2,1,0:T(2,128)} %copy.110) | data formatting | bytes 4194304 | tf_op jit(solution)/shard_map/convert_element_type | solution.py:309
  70.1 3.5 %multiply_convert_fusion = bf16[32,64,256]{2,1,0:T(8,128)(2,1)} fusion(f32[32,64,256]{2,1,0:T(8,128)} %reshape.206, f32[32,64,256]{2,1,0:T(8,128)} %bitcast.62), kind=kLoop, calls=%fused_computation.26 | loop fusion | flops 1048576 | bytes 5242880 | tf_op jit(solution)/shard_map/convert_element_type | solution.py:320
  73.6 7.0 %all-to-all-done = bf16[32,64,256]{2,1,0:T(8,128)(2,1)} async-done(((bf16[32,64,256]{2,1,0:T(8,128)(2,1)}), bf16[32,64,256]{2,1,0:T(8,128)(2,1)}, u32[]{:S(2)}, u32[]{:S(2)}) %all-to-all-start) | async-done | bytes 1048608 | tf_op jit(solution)/shard_map/all_to_all | solution.py:325
  80.6 4.6 %all-to-all-start.2 = ((bf16[32,64,256]{2,1,0:T(8,128)(2,1)}), bf16[32,64,256]{2,1,0:T(8,128)(2,1)}, u32[]{:S(2)}, u32[]{:S(2)}) async-start(bf16[32,64,256]{2,1,0:T(8,128)(2,1)} %multiply_convert_fusion), calls=%async_computation.2 | async-start | bytes 2097152 | tf_op jit(solution)/shard_map/all_to_all | solution.py:326
  86.5 1.8 stack.62.row_ref
  98.2 2.8 %copy.142 = bf16[32,64,256]{2,0,1:T(8,128)(2,1)} copy(bf16[32,64,256]{2,1,0:T(8,128)(2,1)} %all-to-all-done) | data formatting | bytes 2097152 | tf_op jit(solution)/shard_map/all_to_all | solution.py:325
  101.0 12.3 %all-to-all-done.2 = bf16[32,64,256]{2,1,0:T(8,128)(2,1)} async-done(((bf16[32,64,256]{2,1,0:T(8,128)(2,1)}), bf16[32,64,256]{2,1,0:T(8,128)(2,1)}, u32[]{:S(2)}, u32[]{:S(2)}) %all-to-all-start.2) | async-done | bytes 1048608 | tf_op jit(solution)/shard_map/all_to_all | solution.py:326
  113.2 2.8 %copy.141 = bf16[32,64,256]{2,0,1:T(8,128)(2,1)} copy(bf16[32,64,256]{2,1,0:T(8,128)(2,1)} %all-to-all-done.2) | data formatting | bytes 2097152 | tf_op jit(solution)/shard_map/all_to_all | solution.py:326
  116.0 28.2 %shard_map.93 = (bf16[64,32,256]{2,1,0:T(8,128)(2,1)}, bf16[64,32,256]{2,1,0:T(8,128)(2,1)}, f32[64,1,16]{2,1,0:T(1,128)}, f32[64,1,128]{2,1,0:T(1,128)}) custom-call(bf16[64,32,256]{2,1,0:T(8,128)(2,1)} %bitcast.68, bf16[64,32,256]{2,1,0:T(8,128)(2,1)} %bitcast.69, f32[64,2,256]{2,1,0:T(2,128)} %pad_maximum_fusion.2.krow_ref, ...), custom_call_target="tpu_custom_call" | custom-call | flops 4563402752 | bytes 8388608 | tf_op jit(solution)/shard_map/pallas_call | solution.py:262
  144.2 2.8 %copy.124 = bf16[64,32,256]{2,0,1:T(8,128)(2,1)} copy(bf16[64,32,256]{2,1,0:T(8,128)(2,1)} %get-tuple-element.9) | data formatting | bytes 2097152 | tf_op jit(solution)/shard_map/pallas_call | solution.py:262
  147.0 4.6 %all-to-all-start.4 = ((bf16[64,32,256]{2,0,1:T(8,128)(2,1)}), bf16[64,32,256]{2,0,1:T(8,128)(2,1)}, u32[]{:S(2)}, u32[]{:S(2)}) async-start(bf16[64,32,256]{2,0,1:T(8,128)(2,1)} %copy.124), calls=%async_computation.4 | async-start | bytes 2097152 | tf_op jit(solution)/shard_map/all_to_all | solution.py:349
  151.6 2.8 %copy.122 = bf16[64,32,256]{2,0,1:T(8,128)(2,1)} copy(bf16[64,32,256]{2,1,0:T(8,128)(2,1)} %get-tuple-element.8) | data formatting | bytes 2097152 | tf_op jit(solution)/shard_map/pallas_call | solution.py:262
  154.4 25.2 %all-to-all-done.4 = bf16[64,32,256]{2,0,1:T(8,128)(2,1)} async-done(((bf16[64,32,256]{2,0,1:T(8,128)(2,1)}), bf16[64,32,256]{2,0,1:T(8,128)(2,1)}, u32[]{:S(2)}, u32[]{:S(2)}) %all-to-all-start.4) | async-done | bytes 1048608 | tf_op jit(solution)/shard_map/all_to_all | solution.py:349
  179.6 4.6 %all-to-all-start.3 = ((bf16[64,32,256]{2,0,1:T(8,128)(2,1)}), bf16[64,32,256]{2,0,1:T(8,128)(2,1)}, u32[]{:S(2)}, u32[]{:S(2)}) async-start(bf16[64,32,256]{2,0,1:T(8,128)(2,1)} %copy.122), calls=%async_computation.3 | async-start | bytes 2097152 | tf_op jit(solution)/shard_map/all_to_all | solution.py:348
  184.2 3.9 %reshape.209 = f32[1,2048,256]{2,1,0:T(8,128)} reshape(f32[2048,2,128]{2,1,0:T(2,128)} %copy.110) | data formatting | bytes 4194304 | tf_op jit(solution)/shard_map/convert_element_type | solution.py:309
  188.8 14.9 %psum.7 = f32[64,17]{0,1:T(8,128)S(1)} all-reduce(f32[64,17]{0,1:T(8,128)S(1)} %pad_maximum_fusion.3), channel_id=1, replica_groups=mesh['dp'=4,'ctx'=32,'tp'=2] {'dp'}, use_global_device_ids=true, to_apply=%region_1.2 | all-reduce | flops 1088 | bytes 8704 | tf_op jit(solution)/shard_map/psum | solution.py:355
  204.6 7.7 %all-to-all-done.3 = bf16[64,32,256]{2,0,1:T(8,128)(2,1)} async-done(((bf16[64,32,256]{2,0,1:T(8,128)(2,1)}), bf16[64,32,256]{2,0,1:T(8,128)(2,1)}, u32[]{:S(2)}, u32[]{:S(2)}) %all-to-all-start.3) | async-done | bytes 1048608 | tf_op jit(solution)/shard_map/all_to_all | solution.py:348
  212.2 3.9 %all-to-all-start.5 = ((f32[32,1,1088]{2,1,0:T(1,128)}), f32[32,1,1088]{2,1,0:T(1,128)S(1)}, u32[]{:S(2)}, u32[]{:S(2)}) async-start(f32[32,1,1088]{2,1,0:T(1,128)} %reshape.212), calls=%async_computation.5 | async-start | bytes 294912 | tf_op jit(solution)/shard_map/all_to_all | solution.py:357
  216.1 4.1 %fusion.9 = (bf16[1,2048,256]{2,1,0:T(8,128)(2,1)S(1)}, bf16[1,2048,256]{2,1,0:T(8,128)(2,1)S(1)}, bf16[1,2048,256]{2,1,0:T(8,128)(2,1)}, bf16[1,2048,256]{2,1,0:T(8,128)(2,1)S(1)}) fusion(bf16[64,32,256]{2,0,1:T(8,128)(2,1)} %all-to-all-done.4, bf16[3,2048,256]{2,1,0:T(8,128)(2,1)S(1)} %fusion.4, bf16[64,32,256]{2,0,1:T(8,128)(2,1)} %all-to-all-done.3, ...), kind=kLoop, calls=%fused_computation.20 | loop fusion | flops 6815744 | bytes 11534336 | tf_op jit(solution)/shard_map/convert.10
  223.3 2.5 %copy.125 = bf16[3,2048,2]{1,2,0:T(2,128)(2,1)} copy(bf16[3,2048,2]{2,1,0:T(8,128)(2,1)} %pad_maximum_fusion) | data formatting | bytes 49152 | tf_op jit(solution)/shard_map/slice | solution.py:367
  225.8 2.4 collective-permute-start.1
  234.5 2.3 copy.126
  236.8 2.6 %maximum_convert_fusion.1 = f32[3,2048,258]{2,1,0:T(8,128)S(1)} fusion(bf16[3,2048,2]{2,1,0:T(8,128)(2,1)} %copy.126, bf16[1,2048,256]{2,1,0:T(8,128)(2,1)S(1)} %copy-done.3, bf16[1,2048,256]{2,1,0:T(8,128)(2,1)S(1)} %copy-done.1, bf16[1,2048,256]{2,1,0:T(8,128)(2,1)S(1)} %copy-done.5), kind=kLoop, calls=%fused_computation.13 | loop fusion | flops 12681216 | bytes 9510912 | tf_op jit(solution)/shard_map/convert_element_type | solution.py:38
  239.5 7.3 %fusion.6 = bf16[1,3,2048,256]{3,2,1,0:T(8,128)(2,1)} fusion(f32[3,2048,258]{2,1,0:T(8,128)S(1)} %maximum_convert_fusion.1, f32[3,2048]{1,0:T(4,128)S(1)} %copy-done.8, f32[3,2048]{1,0:T(4,128)S(1)} %copy-done.10, f32[3,2048]{1,0:T(4,128)S(1)} %bitcast.72), kind=kLoop, calls=%fused_computation.14 | loop fusion | flops 9437184 | bytes 22093824 | tf_op jit(solution)/shard_map/broadcast_in_dim | solution.py:369
  (79 shorter events, 31.6 us)
Async XLA Ops:
  0.6 17.2 %copy-start.13 = (f32[3,3,2048]{2,1,0:T(4,128)S(1)}, f32[3,3,2048]{2,1,0:T(4,128)}, u32[]{:S(2)}) copy-start(f32[3,3,2048]{2,1,0:T(4,128)} %param.8) | copy-start | bytes 221188
  0.6 18.9 %copy-start.6 = (bf16[1,3,2048,256]{3,2,1,0:T(8,128)(2,1)S(1)}, bf16[1,3,2048,256]{3,2,1,0:T(8,128)(2,1)}, u32[]{:S(2)}) copy-start(bf16[1,3,2048,256]{3,2,1,0:T(8,128)(2,1)} %param.6) | copy-start | bytes 9437188
  5.6 12.4 %collective-permute-start = (bf16[3,2048,2]{1,2,0:T(2,128)(2,1)S(1)}, bf16[3,2048,2]{1,2,0:T(2,128)(2,1)S(1)}, u32[]{:S(2)}, u32[]{:S(2)}) collective-permute-start(bf16[3,2048,2]{1,2,0:T(2,128)(2,1)S(1)} %copy.107), channel_id=1, source_target_pairs={{0,2},{2,4},{4,6},{6,8},{8,10},{10,12},{12,14},{14,16},{16,18},{18... | collective-permute-start | bytes 73736 | tf_op jit(solution)/shard_map/ppermute | solution.py:18
  10.5 35.8 %all-to-all-start.1 = ((bf16[2,2048,128]{2,1,0:T(8,128)(2,1)}), bf16[2,2048,128]{2,1,0:T(8,128)(2,1)}, u32[]{:S(2)}, u32[]{:S(2)}) async-start(bf16[2,2048,128]{2,1,0:T(8,128)(2,1)} %bitcast.67), calls=%async_computation.1 | async-start | bytes 2097152 | tf_op jit(solution)/shard_map/all_to_all | solution.py:309
  17.9 5.0 %copy-start.7 = (f32[3,2048]{1,0:T(4,128)}, f32[3,2048]{1,0:T(4,128)S(1)}, u32[]{:S(2)}) copy-start(f32[3,2048]{1,0:T(4,128)S(1)} %get-tuple-element.28) | copy-start | bytes 73732
  17.9 5.0 %copy-start.9 = (f32[3,2048]{1,0:T(4,128)}, f32[3,2048]{1,0:T(4,128)S(1)}, u32[]{:S(2)}) copy-start(f32[3,2048]{1,0:T(4,128)S(1)} %get-tuple-element.29) | copy-start | bytes 73732
  17.9 4.9 %copy-start.11 = (f32[3,1,2048]{2,0,1:T(4,128)}, f32[3,1,2048]{2,0,1:T(4,128)S(1)}, u32[]{:S(2)}) copy-start(f32[3,1,2048]{2,0,1:T(4,128)S(1)} %copy.143) | copy-start | bytes 73732
  46.4 34.3 %all-to-all-start = ((bf16[32,64,256]{2,1,0:T(8,128)(2,1)}), bf16[32,64,256]{2,1,0:T(8,128)(2,1)}, u32[]{:S(2)}, u32[]{:S(2)}) async-start(bf16[32,64,256]{2,1,0:T(8,128)(2,1)} %bitcast.65), calls=%async_computation | async-start | bytes 2097152 | tf_op jit(solution)/shard_map/all_to_all | solution.py:325
  80.6 32.6 %all-to-all-start.2 = ((bf16[32,64,256]{2,1,0:T(8,128)(2,1)}), bf16[32,64,256]{2,1,0:T(8,128)(2,1)}, u32[]{:S(2)}, u32[]{:S(2)}) async-start(bf16[32,64,256]{2,1,0:T(8,128)(2,1)} %multiply_convert_fusion), calls=%async_computation.2 | async-start | bytes 2097152 | tf_op jit(solution)/shard_map/all_to_all | solution.py:326
  147.0 32.6 %all-to-all-start.4 = ((bf16[64,32,256]{2,0,1:T(8,128)(2,1)}), bf16[64,32,256]{2,0,1:T(8,128)(2,1)}, u32[]{:S(2)}, u32[]{:S(2)}) async-start(bf16[64,32,256]{2,0,1:T(8,128)(2,1)} %copy.124), calls=%async_computation.4 | async-start | bytes 2097152 | tf_op jit(solution)/shard_map/all_to_all | solution.py:349
  151.6 36.5 %copy-start.14 = (f32[64,1,16]{2,1,0:T(1,128)S(1)}, f32[64,1,16]{2,1,0:T(1,128)}, u32[]{:S(2)}) copy-start(f32[64,1,16]{2,1,0:T(1,128)} %get-tuple-element.10) | copy-start | bytes 12292
  151.6 36.6 %copy-start.15 = (f32[64,1,128]{2,1,0:T(1,128)S(1)}, f32[64,1,128]{2,1,0:T(1,128)}, u32[]{:S(2)}) copy-start(f32[64,1,128]{2,1,0:T(1,128)} %get-tuple-element.11) | copy-start | bytes 98308
  179.6 32.6 %all-to-all-start.3 = ((bf16[64,32,256]{2,0,1:T(8,128)(2,1)}), bf16[64,32,256]{2,0,1:T(8,128)(2,1)}, u32[]{:S(2)}, u32[]{:S(2)}) async-start(bf16[64,32,256]{2,0,1:T(8,128)(2,1)} %copy.122), calls=%async_computation.3 | async-start | bytes 2097152 | tf_op jit(solution)/shard_map/all_to_all | solution.py:348
  212.2 16.0 %all-to-all-start.5 = ((f32[32,1,1088]{2,1,0:T(1,128)}), f32[32,1,1088]{2,1,0:T(1,128)S(1)}, u32[]{:S(2)}, u32[]{:S(2)}) async-start(f32[32,1,1088]{2,1,0:T(1,128)} %reshape.212), calls=%async_computation.5 | async-start | bytes 294912 | tf_op jit(solution)/shard_map/all_to_all | solution.py:357
  220.2 1.0 copy-start
  220.2 1.3 copy-start.2
  220.2 1.6 copy-start.4
  223.3 13.5 %copy-start.1 = (bf16[1,2048,256]{2,1,0:T(8,128)(2,1)S(1)}, bf16[1,2048,256]{2,1,0:T(8,128)(2,1)}, u32[]{:S(2)}) copy-start(bf16[1,2048,256]{2,1,0:T(8,128)(2,1)} %copy-done) | copy-start | bytes 3145732
  223.3 13.5 %copy-start.3 = (bf16[1,2048,256]{2,1,0:T(8,128)(2,1)S(1)}, bf16[1,2048,256]{2,1,0:T(8,128)(2,1)}, u32[]{:S(2)}) copy-start(bf16[1,2048,256]{2,1,0:T(8,128)(2,1)} %copy-done.2) | copy-start | bytes 3145732
  223.3 13.5 %copy-start.5 = (bf16[1,2048,256]{2,1,0:T(8,128)(2,1)S(1)}, bf16[1,2048,256]{2,1,0:T(8,128)(2,1)}, u32[]{:S(2)}) copy-start(bf16[1,2048,256]{2,1,0:T(8,128)(2,1)} %copy-done.4) | copy-start | bytes 3145732
  225.8 8.7 %collective-permute-start.1 = (bf16[3,2048,2]{1,2,0:T(2,128)(2,1)}, bf16[3,2048,2]{1,2,0:T(2,128)(2,1)}, u32[]{:S(2)}, u32[]{:S(2)}) collective-permute-start(bf16[3,2048,2]{1,2,0:T(2,128)(2,1)} %copy.125), channel_id=1, source_target_pairs={{2,0},{4,2},{6,4},{8,6},{10,8},{12,10},{14,12},{16,14},{18,16},{20... | collective-permute-start | bytes 73736 | tf_op jit(solution)/shard_map/ppermute | solution.py:18
  236.8 2.6 %copy-start.8 = (f32[3,2048]{1,0:T(4,128)S(1)}, f32[3,2048]{1,0:T(4,128)}, u32[]{:S(2)}) copy-start(f32[3,2048]{1,0:T(4,128)} %copy-done.7) | copy-start | bytes 73732
  236.8 2.6 %copy-start.10 = (f32[3,2048]{1,0:T(4,128)S(1)}, f32[3,2048]{1,0:T(4,128)}, u32[]{:S(2)}) copy-start(f32[3,2048]{1,0:T(4,128)} %copy-done.9) | copy-start | bytes 73732
  236.8 2.6 %copy-start.12 = (f32[3,1,2048]{2,0,1:T(4,128)S(1)}, f32[3,1,2048]{2,0,1:T(4,128)}, u32[]{:S(2)}) copy-start(f32[3,1,2048]{2,0,1:T(4,128)} %copy-done.11) | copy-start | bytes 73732

commit v3 on v2

--- a/solution.py
+++ b/solution.py
@@ -352,7 +352,15 @@
     local_grads = jnp.concatenate(
         [mode_part * jnp.sqrt(2.0 * rate_rows) * grad_scale, skip_part[:, None] * grad_scale], axis=1
     )
-    local_grads = lax.psum(local_grads, "dp")
+    dp_count = lax.axis_size("dp")
+    if dp_count & (dp_count - 1) == 0:
+        hop = 1
+        while hop < dp_count:
+            partners = [(i, i ^ hop) for i in range(dp_count)]
+            local_grads = local_grads + lax.ppermute(local_grads, "dp", partners)
+            hop *= 2
+    else:
+        local_grads = lax.psum(local_grads, "dp")
     spread = jnp.broadcast_to(local_grads[None], (ctx_count,) + local_grads.shape)
     gathered = lax.all_to_all(spread, "ctx", split_axis=0, concat_axis=0, tiled=True)
     gathered = gathered.reshape(chans_tp, local_grads.shape[1])

time: 250 us -> 250 us (level)
  blocking collectives: 14.9 us -> 0 us
  waiting for transfers between devices: 67.9 us -> 78.7 us
  starting transfers between devices: 38.7 us -> 42.9 us
    psum x1 -> x0, blocking collectives: 14.9 us -> none  [on_device(): local_grads = lax.psum(local_grads, 'dp')]
    all_to_all x1, waiting for transfers between devices: 7.66 us -> 16.6 us  [on_device(): lax.all_to_all(conv_rows, 'ctx', split_axis=1, concat_axis=0, tiled=True)]
    ppermute x0 -> x2, starting transfers between devices: none -> 4.29 us  [on_device(): local_grads = local_grads + lax.ppermute(local_grads, 'dp', partners)]
  transfers between devices with their start and end apart: 8 -> 10, of which waited for: 5 -> 6; matrix products, arithmetic and copies ran while one was open for 29% -> 29% of each run, Pallas kernels for 0% -> 0%
where the time goes in v3:
time: 250 us; the launch traced here: 247 us
  waiting for transfers between devices  78.7 us (31%)
  local copies, waits for them, and re-layouts  49.2 us (20%)
  other arithmetic  46.7 us (19%)
  starting transfers between devices  42.9 us (17%)
  Pallas kernels  28.2 us (11%)
    pallas_call x1, Pallas kernels, long_conv(): pl.pallas_call(long_conv_kernel, grid=(chan_count // step,), in_specs=[da...  28.2 us
    all_to_all x1, waiting for transfers between devices, on_device(): lax.all_to_all(back_rows, 'ctx', split_axis=1, concat_axis=0, tiled=True)  25.2 us
    all_to_all x1, waiting for transfers between devices, on_device(): lax.all_to_all(conv_rows, 'ctx', split_axis=1, concat_axis=0, tiled=True)  16.6 us
    convert_element_type x3, local copies, waits for them, and re-layouts, on_device(): lax.all_to_all(cotangent[0], 'tp', split_axis=0, concat_axis=1, tiled=True)  16.3 us
    all_to_all x1, waiting for transfers between devices, on_device(): lax.all_to_all(cotangent[0], 'tp', split_axis=0, concat_axis=1, tiled=True)  15.8 us
    all_to_all x1, waiting for transfers between devices, on_device(): lax.all_to_all(adjoint, 'ctx', split_axis=0, concat_axis=1, tiled=True)  12.3 us
    unnamed x7, other arithmetic  7.82 us
    all_to_all x1, starting transfers between devices, on_device(): lax.all_to_all(cotangent[0], 'tp', split_axis=0, concat_axis=1, tiled=True)  7.29 us
  transfers between devices with their start and end apart: 10, of which 6 were waited for; matrix products, arithmetic and copies ran while one was open for 29% of the time, Pallas kernels for 0%

profile of v3, /device:TPU:1, one launch (start us, length us, event | category | flops | bytes accessed | tf_op | source)
XLA Modules:
  0.0 246.7 jit_solution(866737029426156920)
XLA Ops:
  0.7 3.2 %slice.71 = bf16[3,2048,2]{2,1,0:T(8,128)(2,1)} slice(bf16[3,2048,256]{2,1,0:T(8,128)(2,1)} %bitcast.63), slice={[0:3], [0:2048], [254:256]} | slice | bytes 49152 | tf_op jit(solution)/shard_map/slice | solution.py:312
  5.6 4.9 %collective-permute-start = (bf16[3,2048,2]{1,2,0:T(2,128)(2,1)S(1)}, bf16[3,2048,2]{1,2,0:T(2,128)(2,1)S(1)}, u32[]{:S(2)}, u32[]{:S(2)}) collective-permute-start(bf16[3,2048,2]{1,2,0:T(2,128)(2,1)S(1)} %copy.107), channel_id=1, source_target_pairs={{0,2},{2,4},{4,6},{6,8},{8,10},{10,12},{12,14},{14,16},{16,18},{18... | collective-permute-start | bytes 73736 | tf_op jit(solution)/shard_map/ppermute | solution.py:18
  10.5 7.3 %all-to-all-start.1 = ((bf16[2,2048,128]{2,1,0:T(8,128)(2,1)}), bf16[2,2048,128]{2,1,0:T(8,128)(2,1)}, u32[]{:S(2)}, u32[]{:S(2)}) async-start(bf16[2,2048,128]{2,1,0:T(8,128)(2,1)} %bitcast.67), calls=%async_computation.1 | async-start | bytes 2097152 | tf_op jit(solution)/shard_map/all_to_all | solution.py:309
  19.6 3.3 %maximum_convert_fusion = f32[3,2048,258]{2,1,0:T(8,128)S(1)} fusion(bf16[3,2048,256]{2,1,0:T(8,128)(2,1)S(1)} %bitcast.64, bf16[3,2048,2]{2,1,0:T(8,128)(2,1)} %copy.108), kind=kLoop, calls=%fused_computation.12 | loop fusion | flops 6340608 | bytes 9510912 | tf_op jit(solution)/shard_map/convert_element_type | solution.py:24
  22.9 6.4 %fusion.4 = bf16[3,2048,256]{2,1,0:T(8,128)(2,1)S(1)} fusion(f32[3,2048,258]{2,1,0:T(8,128)S(1)} %maximum_convert_fusion, f32[3,2048]{1,0:T(4,128)S(1)} %get-tuple-element.28, f32[3,2048]{1,0:T(4,128)S(1)} %get-tuple-element.29, f32[3,2048]{1,0:T(4,128)S(1)} %bitcast.71), kind=kLoop, calls=%fused_computation.8 | loop fusion | flops 9437184 | bytes 22093824 | tf_op jit(solution)/shard_map/convert_element_type | solution.py:314
  30.6 15.8 %all-to-all-done.1 = bf16[2,2048,128]{2,1,0:T(8,128)(2,1)} async-done(((bf16[2,2048,128]{2,1,0:T(8,128)(2,1)}), bf16[2,2048,128]{2,1,0:T(8,128)(2,1)}, u32[]{:S(2)}, u32[]{:S(2)}) %all-to-all-start.1) | async-done | bytes 1048608 | tf_op jit(solution)/shard_map/all_to_all | solution.py:309
  46.4 6.3 %all-to-all-start = ((bf16[32,64,256]{2,1,0:T(8,128)(2,1)}), bf16[32,64,256]{2,1,0:T(8,128)(2,1)}, u32[]{:S(2)}, u32[]{:S(2)}) async-start(bf16[32,64,256]{2,1,0:T(8,128)(2,1)} %bitcast.65), calls=%async_computation | async-start | bytes 2097152 | tf_op jit(solution)/shard_map/all_to_all | solution.py:325
  57.7 8.6 %copy.110 = f32[2048,2,128]{2,1,0:T(2,128)} copy(f32[2048,2,128]{2,0,1:T(8,128)S(1)} %convert_bitcast_fusion) | data formatting | bytes 4194304 | tf_op jit(solution)/shard_map/convert_element_type | solution.py:309
  66.2 3.9 %reshape.206 = f32[32,64,256]{2,1,0:T(8,128)} reshape(f32[2048,2,128]{2,1,0:T(2,128)} %copy.110) | data formatting | bytes 4194304 | tf_op jit(solution)/shard_map/convert_element_type | solution.py:309
  70.1 3.5 %multiply_convert_fusion = bf16[32,64,256]{2,1,0:T(8,128)(2,1)} fusion(f32[32,64,256]{2,1,0:T(8,128)} %reshape.206, f32[32,64,256]{2,1,0:T(8,128)} %bitcast.62), kind=kLoop, calls=%fused_computation.26 | loop fusion | flops 1048576 | bytes 5242880 | tf_op jit(solution)/shard_map/convert_element_type | solution.py:320
  73.6 7.0 %all-to-all-done = bf16[32,64,256]{2,1,0:T(8,128)(2,1)} async-done(((bf16[32,64,256]{2,1,0:T(8,128)(2,1)}), bf16[32,64,256]{2,1,0:T(8,128)(2,1)}, u32[]{:S(2)}, u32[]{:S(2)}) %all-to-all-start) | async-done | bytes 1048608 | tf_op jit(solution)/shard_map/all_to_all | solution.py:325
  80.6 4.6 %all-to-all-start.2 = ((bf16[32,64,256]{2,1,0:T(8,128)(2,1)}), bf16[32,64,256]{2,1,0:T(8,128)(2,1)}, u32[]{:S(2)}, u32[]{:S(2)}) async-start(bf16[32,64,256]{2,1,0:T(8,128)(2,1)} %multiply_convert_fusion), calls=%async_computation.2 | async-start | bytes 2097152 | tf_op jit(solution)/shard_map/all_to_all | solution.py:326
  86.5 1.8 stack.62.row_ref
  98.2 2.8 %copy.142 = bf16[32,64,256]{2,0,1:T(8,128)(2,1)} copy(bf16[32,64,256]{2,1,0:T(8,128)(2,1)} %all-to-all-done) | data formatting | bytes 2097152 | tf_op jit(solution)/shard_map/all_to_all | solution.py:325
  100.9 12.3 %all-to-all-done.2 = bf16[32,64,256]{2,1,0:T(8,128)(2,1)} async-done(((bf16[32,64,256]{2,1,0:T(8,128)(2,1)}), bf16[32,64,256]{2,1,0:T(8,128)(2,1)}, u32[]{:S(2)}, u32[]{:S(2)}) %all-to-all-start.2) | async-done | bytes 1048608 | tf_op jit(solution)/shard_map/all_to_all | solution.py:326
  113.2 2.8 %copy.141 = bf16[32,64,256]{2,0,1:T(8,128)(2,1)} copy(bf16[32,64,256]{2,1,0:T(8,128)(2,1)} %all-to-all-done.2) | data formatting | bytes 2097152 | tf_op jit(solution)/shard_map/all_to_all | solution.py:326
  116.0 28.2 %shard_map.93 = (bf16[64,32,256]{2,1,0:T(8,128)(2,1)}, bf16[64,32,256]{2,1,0:T(8,128)(2,1)}, f32[64,1,16]{2,1,0:T(1,128)}, f32[64,1,128]{2,1,0:T(1,128)}) custom-call(bf16[64,32,256]{2,1,0:T(8,128)(2,1)} %bitcast.68, bf16[64,32,256]{2,1,0:T(8,128)(2,1)} %bitcast.69, f32[64,2,256]{2,1,0:T(2,128)} %pad_maximum_fusion.2.krow_ref, ...), custom_call_target="tpu_custom_call" | custom-call | flops 4563402752 | bytes 8388608 | tf_op jit(solution)/shard_map/pallas_call | solution.py:262
  144.2 2.8 %copy.124 = bf16[64,32,256]{2,0,1:T(8,128)(2,1)} copy(bf16[64,32,256]{2,1,0:T(8,128)(2,1)} %get-tuple-element.9) | data formatting | bytes 2097152 | tf_op jit(solution)/shard_map/pallas_call | solution.py:262
  147.0 4.6 %all-to-all-start.4 = ((bf16[64,32,256]{2,0,1:T(8,128)(2,1)}), bf16[64,32,256]{2,0,1:T(8,128)(2,1)}, u32[]{:S(2)}, u32[]{:S(2)}) async-start(bf16[64,32,256]{2,0,1:T(8,128)(2,1)} %copy.124), calls=%async_computation.4 | async-start | bytes 2097152 | tf_op jit(solution)/shard_map/all_to_all | solution.py:349
  151.6 2.8 %copy.122 = bf16[64,32,256]{2,0,1:T(8,128)(2,1)} copy(bf16[64,32,256]{2,1,0:T(8,128)(2,1)} %get-tuple-element.8) | data formatting | bytes 2097152 | tf_op jit(solution)/shard_map/pallas_call | solution.py:262
  154.4 25.2 %all-to-all-done.4 = bf16[64,32,256]{2,0,1:T(8,128)(2,1)} async-done(((bf16[64,32,256]{2,0,1:T(8,128)(2,1)}), bf16[64,32,256]{2,0,1:T(8,128)(2,1)}, u32[]{:S(2)}, u32[]{:S(2)}) %all-to-all-start.4) | async-done | bytes 1048608 | tf_op jit(solution)/shard_map/all_to_all | solution.py:349
  179.6 4.6 %all-to-all-start.3 = ((bf16[64,32,256]{2,0,1:T(8,128)(2,1)}), bf16[64,32,256]{2,0,1:T(8,128)(2,1)}, u32[]{:S(2)}, u32[]{:S(2)}) async-start(bf16[64,32,256]{2,0,1:T(8,128)(2,1)} %copy.122), calls=%async_computation.3 | async-start | bytes 2097152 | tf_op jit(solution)/shard_map/all_to_all | solution.py:348
  187.9 2.9 %collective-permute-start.3 = (f32[64,17]{0,1:T(8,128)S(1)}, f32[64,17]{0,1:T(8,128)S(1)}, u32[]{:S(2)}, u32[]{:S(2)}) collective-permute-start(f32[64,17]{0,1:T(8,128)S(1)} %fusion.24), channel_id=1, source_target_pairs={{0,128},{64,192},{128,0},{192,64},{1,129},{65,193},{129,1},{193,65... | collective-permute-start | bytes 13064 | tf_op jit(solution)/shard_map/ppermute | solution.py:360
  190.8 3.9 %reshape.209 = f32[1,2048,256]{2,1,0:T(8,128)} reshape(f32[2048,2,128]{2,1,0:T(2,128)} %copy.110) | data formatting | bytes 4194304 | tf_op jit(solution)/shard_map/convert_element_type | solution.py:309
  195.6 16.6 %all-to-all-done.3 = bf16[64,32,256]{2,0,1:T(8,128)(2,1)} async-done(((bf16[64,32,256]{2,0,1:T(8,128)(2,1)}), bf16[64,32,256]{2,0,1:T(8,128)(2,1)}, u32[]{:S(2)}, u32[]{:S(2)}) %all-to-all-start.3) | async-done | bytes 1048608 | tf_op jit(solution)/shard_map/all_to_all | solution.py:348
  212.3 4.1 %all-to-all-start.5 = ((f32[32,1,1088]{2,1,0:T(1,128)}), f32[32,1,1088]{2,1,0:T(1,128)S(1)}, u32[]{:S(2)}, u32[]{:S(2)}) async-start(f32[32,1,1088]{2,1,0:T(1,128)} %reshape.212), calls=%async_computation.5 | async-start | bytes 294912 | tf_op jit(solution)/shard_map/all_to_all | solution.py:365
  216.3 4.1 %fusion.9 = (bf16[1,2048,256]{2,1,0:T(8,128)(2,1)S(1)}, bf16[1,2048,256]{2,1,0:T(8,128)(2,1)S(1)}, bf16[1,2048,256]{2,1,0:T(8,128)(2,1)}, bf16[1,2048,256]{2,1,0:T(8,128)(2,1)S(1)}) fusion(bf16[64,32,256]{2,0,1:T(8,128)(2,1)} %all-to-all-done.4, bf16[3,2048,256]{2,1,0:T(8,128)(2,1)S(1)} %fusion.4, bf16[64,32,256]{2,0,1:T(8,128)(2,1)} %all-to-all-done.3, ...), kind=kLoop, calls=%fused_computation.20 | loop fusion | flops 6815744 | bytes 11534336 | tf_op jit(solution)/shard_map/convert.10
  223.5 2.5 %copy.125 = bf16[3,2048,2]{1,2,0:T(2,128)(2,1)} copy(bf16[3,2048,2]{2,1,0:T(8,128)(2,1)} %pad_maximum_fusion) | data formatting | bytes 49152 | tf_op jit(solution)/shard_map/slice | solution.py:375
  226.0 2.2 collective-permute-start.1
  234.5 2.3 copy.126
  236.8 2.6 %maximum_convert_fusion.1 = f32[3,2048,258]{2,1,0:T(8,128)S(1)} fusion(bf16[3,2048,2]{2,1,0:T(8,128)(2,1)} %copy.126, bf16[1,2048,256]{2,1,0:T(8,128)(2,1)S(1)} %copy-done.3, bf16[1,2048,256]{2,1,0:T(8,128)(2,1)S(1)} %copy-done.1, bf16[1,2048,256]{2,1,0:T(8,128)(2,1)S(1)} %copy-done.5), kind=kLoop, calls=%fused_computation.13 | loop fusion | flops 12681216 | bytes 9510912 | tf_op jit(solution)/shard_map/convert_element_type | solution.py:38
  239.4 7.3 %fusion.6 = bf16[1,3,2048,256]{3,2,1,0:T(8,128)(2,1)} fusion(f32[3,2048,258]{2,1,0:T(8,128)S(1)} %maximum_convert_fusion.1, f32[3,2048]{1,0:T(4,128)S(1)} %copy-done.8, f32[3,2048]{1,0:T(4,128)S(1)} %copy-done.10, f32[3,2048]{1,0:T(4,128)S(1)} %bitcast.72), kind=kLoop, calls=%fused_computation.14 | loop fusion | flops 9437184 | bytes 22093824 | tf_op jit(solution)/shard_map/broadcast_in_dim | solution.py:377
  (84 shorter events, 34.6 us)
Async XLA Ops:
  0.6 17.2 %copy-start.13 = (f32[3,3,2048]{2,1,0:T(4,128)S(1)}, f32[3,3,2048]{2,1,0:T(4,128)}, u32[]{:S(2)}) copy-start(f32[3,3,2048]{2,1,0:T(4,128)} %param.8) | copy-start | bytes 221188
  0.6 18.9 %copy-start.6 = (bf16[1,3,2048,256]{3,2,1,0:T(8,128)(2,1)S(1)}, bf16[1,3,2048,256]{3,2,1,0:T(8,128)(2,1)}, u32[]{:S(2)}) copy-start(bf16[1,3,2048,256]{3,2,1,0:T(8,128)(2,1)} %param.6) | copy-start | bytes 9437188
  5.6 12.4 %collective-permute-start = (bf16[3,2048,2]{1,2,0:T(2,128)(2,1)S(1)}, bf16[3,2048,2]{1,2,0:T(2,128)(2,1)S(1)}, u32[]{:S(2)}, u32[]{:S(2)}) collective-permute-start(bf16[3,2048,2]{1,2,0:T(2,128)(2,1)S(1)} %copy.107), channel_id=1, source_target_pairs={{0,2},{2,4},{4,6},{6,8},{8,10},{10,12},{12,14},{14,16},{16,18},{18... | collective-permute-start | bytes 73736 | tf_op jit(solution)/shard_map/ppermute | solution.py:18
  10.5 35.8 %all-to-all-start.1 = ((bf16[2,2048,128]{2,1,0:T(8,128)(2,1)}), bf16[2,2048,128]{2,1,0:T(8,128)(2,1)}, u32[]{:S(2)}, u32[]{:S(2)}) async-start(bf16[2,2048,128]{2,1,0:T(8,128)(2,1)} %bitcast.67), calls=%async_computation.1 | async-start | bytes 2097152 | tf_op jit(solution)/shard_map/all_to_all | solution.py:309
  17.9 5.0 %copy-start.7 = (f32[3,2048]{1,0:T(4,128)}, f32[3,2048]{1,0:T(4,128)S(1)}, u32[]{:S(2)}) copy-start(f32[3,2048]{1,0:T(4,128)S(1)} %get-tuple-element.28) | copy-start | bytes 73732
  17.9 5.0 %copy-start.9 = (f32[3,2048]{1,0:T(4,128)}, f32[3,2048]{1,0:T(4,128)S(1)}, u32[]{:S(2)}) copy-start(f32[3,2048]{1,0:T(4,128)S(1)} %get-tuple-element.29) | copy-start | bytes 73732
  17.9 4.9 %copy-start.11 = (f32[3,1,2048]{2,0,1:T(4,128)}, f32[3,1,2048]{2,0,1:T(4,128)S(1)}, u32[]{:S(2)}) copy-start(f32[3,1,2048]{2,0,1:T(4,128)S(1)} %copy.143) | copy-start | bytes 73732
  46.4 34.3 %all-to-all-start = ((bf16[32,64,256]{2,1,0:T(8,128)(2,1)}), bf16[32,64,256]{2,1,0:T(8,128)(2,1)}, u32[]{:S(2)}, u32[]{:S(2)}) async-start(bf16[32,64,256]{2,1,0:T(8,128)(2,1)} %bitcast.65), calls=%async_computation | async-start | bytes 2097152 | tf_op jit(solution)/shard_map/all_to_all | solution.py:325
  80.6 32.6 %all-to-all-start.2 = ((bf16[32,64,256]{2,1,0:T(8,128)(2,1)}), bf16[32,64,256]{2,1,0:T(8,128)(2,1)}, u32[]{:S(2)}, u32[]{:S(2)}) async-start(bf16[32,64,256]{2,1,0:T(8,128)(2,1)} %multiply_convert_fusion), calls=%async_computation.2 | async-start | bytes 2097152 | tf_op jit(solution)/shard_map/all_to_all | solution.py:326
  144.2 40.0 %copy-start.14 = (f32[64,1,16]{2,1,0:T(1,128)S(1)}, f32[64,1,16]{2,1,0:T(1,128)}, u32[]{:S(2)}) copy-start(f32[64,1,16]{2,1,0:T(1,128)} %get-tuple-element.10) | copy-start | bytes 12292
  144.2 40.1 %copy-start.15 = (f32[64,1,128]{2,1,0:T(1,128)S(1)}, f32[64,1,128]{2,1,0:T(1,128)}, u32[]{:S(2)}) copy-start(f32[64,1,128]{2,1,0:T(1,128)} %get-tuple-element.11) | copy-start | bytes 98308
  147.0 32.6 %all-to-all-start.4 = ((bf16[64,32,256]{2,0,1:T(8,128)(2,1)}), bf16[64,32,256]{2,0,1:T(8,128)(2,1)}, u32[]{:S(2)}, u32[]{:S(2)}) async-start(bf16[64,32,256]{2,0,1:T(8,128)(2,1)} %copy.124), calls=%async_computation.4 | async-start | bytes 2097152 | tf_op jit(solution)/shard_map/all_to_all | solution.py:349
  179.6 32.6 %all-to-all-start.3 = ((bf16[64,32,256]{2,0,1:T(8,128)(2,1)}), bf16[64,32,256]{2,0,1:T(8,128)(2,1)}, u32[]{:S(2)}, u32[]{:S(2)}) async-start(bf16[64,32,256]{2,0,1:T(8,128)(2,1)} %copy.122), calls=%async_computation.3 | async-start | bytes 2097152 | tf_op jit(solution)/shard_map/all_to_all | solution.py:348
  184.9 3.0 %collective-permute-start.2 = (f32[64,17]{0,1:T(8,128)S(1)}, f32[64,17]{0,1:T(8,128)S(1)}, u32[]{:S(2)}, u32[]{:S(2)}) collective-permute-start(f32[64,17]{0,1:T(8,128)S(1)} %pad_maximum_fusion.3), channel_id=1, source_target_pairs={{0,64},{64,0},{128,192},{192,128},{1,65},{65,1},{129,193},{193,129... | collective-permute-start | bytes 13064 | tf_op jit(solution)/shard_map/ppermute | solution.py:360
  187.9 6.8 %collective-permute-start.3 = (f32[64,17]{0,1:T(8,128)S(1)}, f32[64,17]{0,1:T(8,128)S(1)}, u32[]{:S(2)}, u32[]{:S(2)}) collective-permute-start(f32[64,17]{0,1:T(8,128)S(1)} %fusion.24), channel_id=1, source_target_pairs={{0,128},{64,192},{128,0},{192,64},{1,129},{65,193},{129,1},{193,65... | collective-permute-start | bytes 13064 | tf_op jit(solution)/shard_map/ppermute | solution.py:360
  212.3 15.9 %all-to-all-start.5 = ((f32[32,1,1088]{2,1,0:T(1,128)}), f32[32,1,1088]{2,1,0:T(1,128)S(1)}, u32[]{:S(2)}, u32[]{:S(2)}) async-start(f32[32,1,1088]{2,1,0:T(1,128)} %reshape.212), calls=%async_computation.5 | async-start | bytes 294912 | tf_op jit(solution)/shard_map/all_to_all | solution.py:365
  220.4 1.0 copy-start
  220.4 1.3 copy-start.2
  220.4 1.6 copy-start.4
  223.5 13.3 %copy-start.1 = (bf16[1,2048,256]{2,1,0:T(8,128)(2,1)S(1)}, bf16[1,2048,256]{2,1,0:T(8,128)(2,1)}, u32[]{:S(2)}) copy-start(bf16[1,2048,256]{2,1,0:T(8,128)(2,1)} %copy-done) | copy-start | bytes 3145732
  223.5 13.3 %copy-start.3 = (bf16[1,2048,256]{2,1,0:T(8,128)(2,1)S(1)}, bf16[1,2048,256]{2,1,0:T(8,128)(2,1)}, u32[]{:S(2)}) copy-start(bf16[1,2048,256]{2,1,0:T(8,128)(2,1)} %copy-done.2) | copy-start | bytes 3145732
  223.5 13.3 %copy-start.5 = (bf16[1,2048,256]{2,1,0:T(8,128)(2,1)S(1)}, bf16[1,2048,256]{2,1,0:T(8,128)(2,1)}, u32[]{:S(2)}) copy-start(bf16[1,2048,256]{2,1,0:T(8,128)(2,1)} %copy-done.4) | copy-start | bytes 3145732
  226.0 8.5 %collective-permute-start.1 = (bf16[3,2048,2]{1,2,0:T(2,128)(2,1)}, bf16[3,2048,2]{1,2,0:T(2,128)(2,1)}, u32[]{:S(2)}, u32[]{:S(2)}) collective-permute-start(bf16[3,2048,2]{1,2,0:T(2,128)(2,1)} %copy.125), channel_id=1, source_target_pairs={{2,0},{4,2},{6,4},{8,6},{10,8},{12,10},{14,12},{16,14},{18,16},{20... | collective-permute-start | bytes 73736 | tf_op jit(solution)/shard_map/ppermute | solution.py:18
  236.8 2.6 %copy-start.8 = (f32[3,2048]{1,0:T(4,128)S(1)}, f32[3,2048]{1,0:T(4,128)}, u32[]{:S(2)}) copy-start(f32[3,2048]{1,0:T(4,128)} %copy-done.7) | copy-start | bytes 73732
  236.8 2.6 %copy-start.10 = (f32[3,2048]{1,0:T(4,128)S(1)}, f32[3,2048]{1,0:T(4,128)}, u32[]{:S(2)}) copy-start(f32[3,2048]{1,0:T(4,128)} %copy-done.9) | copy-start | bytes 73732
  236.8 2.6 %copy-start.12 = (f32[3,1,2048]{2,0,1:T(4,128)S(1)}, f32[3,1,2048]{2,0,1:T(4,128)}, u32[]{:S(2)}) copy-start(f32[3,1,2048]{2,0,1:T(4,128)} %copy-done.11) | copy-start | bytes 73732

commit v4 on v3

--- a/solution.py
+++ b/solution.py
@@ -282,7 +282,7 @@
             jax.ShapeDtypeStruct((chan_count, 1, 128), jnp.float32),
         ],
         cost_estimate=pl.CostEstimate(
-            flops=chan_count * 34 * width * width * blocks, transcendentals=chan_count * width * modes,
+            flops=chan_count * 800 * width * width * blocks, transcendentals=chan_count * width * modes,
             bytes_accessed=chan_count * blocks * width * 8 + tabs.size * 2,
         ),
     )(u_blocks, dz_blocks, krow, tabs, rows)
@@ -301,7 +301,7 @@
     )
 
 
-def on_device(projected, cotangent, short_filter, residues, decay_rate, skip_gain):
+def on_device(projected, cotangent, short_filter, residues, decay_rate, skip_gain, halves=2):
     proj_rows = projected[0]
     token_count = proj_rows.shape[2]
     chans_tp = proj_rows.shape[1]
@@ -321,37 +321,56 @@
     ctx_count = lax.axis_size("ctx")
     token_total = token_count * ctx_count * lax.axis_size("dp")
     weight_all = residues * jnp.sqrt(2.0 * decay_rate)
-    product_all, adjoint_all = (
-        lax.all_to_all(product, "ctx", split_axis=0, concat_axis=1, tiled=True),
-        lax.all_to_all(adjoint, "ctx", split_axis=0, concat_axis=1, tiled=True),
-    )
-    chan_count = chans_tp // ctx_count
-    chan_start = lax.axis_index("ctx") * chan_count
-    rate_rows = lax.dynamic_slice_in_dim(decay_rate, chan_start, chan_count, 0)
-    weight_rows = lax.dynamic_slice_in_dim(weight_all, chan_start, chan_count, 0)
-    gain_rows = lax.dynamic_slice_in_dim(skip_gain, chan_start, chan_count, 0)
-    length = product_all.shape[1]
-    block_len = math.gcd(256, length)
-    block_count = length // block_len
-    conv_blocks, back_blocks, mode_part, skip_part = long_conv(
-        product_all.reshape(chan_count, block_count, block_len),
-        adjoint_all.reshape(chan_count, block_count, block_len),
-        rate_rows,
-        weight_rows,
-        gain_rows,
-    )
-    conv_rows = conv_blocks.reshape(chan_count, length)
-    back_rows = back_blocks.reshape(chan_count, length)
-    mode_part = mode_part[:, 0, :]
-    skip_part = skip_part[:, 0, 0]
-    signal, back_signal = (
-        lax.all_to_all(conv_rows, "ctx", split_axis=1, concat_axis=0, tiled=True),
-        lax.all_to_all(back_rows, "ctx", split_axis=1, concat_axis=0, tiled=True),
-    )
+    part = chans_tp // halves
+    chan_count = part // ctx_count
     grad_scale = 1.0 / math.sqrt(token_total)
-    local_grads = jnp.concatenate(
-        [mode_part * jnp.sqrt(2.0 * rate_rows) * grad_scale, skip_part[:, None] * grad_scale], axis=1
-    )
+    outs, grads_out, grad_parts = [], [], []
+    for half in range(halves):
+        chans = slice(half * part, (half + 1) * part)
+        product_all = lax.all_to_all(product[chans], "ctx", split_axis=0, concat_axis=1, tiled=True)
+        adjoint_all = lax.all_to_all(adjoint[chans], "ctx", split_axis=0, concat_axis=1, tiled=True)
+        chan_start = half * part + lax.axis_index("ctx") * chan_count
+        rate_rows = lax.dynamic_slice_in_dim(decay_rate, chan_start, chan_count, 0)
+        weight_rows = lax.dynamic_slice_in_dim(weight_all, chan_start, chan_count, 0)
+        gain_rows = lax.dynamic_slice_in_dim(skip_gain, chan_start, chan_count, 0)
+        length = product_all.shape[1]
+        block_len = math.gcd(256, length)
+        block_count = length // block_len
+        conv_blocks, back_blocks, mode_part, skip_part = long_conv(
+            product_all.reshape(chan_count, block_count, block_len),
+            adjoint_all.reshape(chan_count, block_count, block_len),
+            rate_rows,
+            weight_rows,
+            gain_rows,
+        )
+        mode_part = mode_part[:, 0, :]
+        skip_part = skip_part[:, 0, 0]
+        grad_parts.append(
+            jnp.concatenate(
+                [mode_part * jnp.sqrt(2.0 * rate_rows) * grad_scale, skip_part[:, None] * grad_scale],
+                axis=1,
+            )
+        )
+        signal = lax.all_to_all(
+            conv_blocks.reshape(chan_count, length), "ctx", split_axis=1, concat_axis=0, tiled=True
+        )
+        back_signal = lax.all_to_all(
+            back_blocks.reshape(chan_count, length), "ctx", split_axis=1, concat_axis=0, tiled=True
+        )
+        conv_wide = signal.astype(jnp.float32)
+        back_wide = back_signal.astype(jnp.float32)
+        outs.append((query_feat[chans] * conv_wide).astype(jnp.bfloat16))
+        feature_grad = jnp.stack(
+            [grad_out[chans] * conv_wide, back_wide * value_feat[chans], back_wide * key_feat[chans]]
+        ).astype(jnp.bfloat16)
+        next_rim = from_behind(feature_grad[:, :, :rim_width], "ctx", -1)
+        grads_out.append(
+            anticausal_short(feature_grad, next_rim, short_filter[:, :, chans]).astype(jnp.bfloat16)
+        )
+    hyena_out = jnp.concatenate(outs, axis=0)
+    input_grad = jnp.concatenate(grads_out, axis=1)
+    local_grads = jnp.concatenate(grad_parts, axis=0)
+    grad_cols = local_grads.shape[1]
     dp_count = lax.axis_size("dp")
     if dp_count & (dp_count - 1) == 0:
         hop = 1
@@ -363,17 +382,10 @@
         local_grads = lax.psum(local_grads, "dp")
     spread = jnp.broadcast_to(local_grads[None], (ctx_count,) + local_grads.shape)
     gathered = lax.all_to_all(spread, "ctx", split_axis=0, concat_axis=0, tiled=True)
-    gathered = gathered.reshape(chans_tp, local_grads.shape[1])
-    residue_grad = gathered[:, : mode_part.shape[1]]
-    skip_grad = gathered[:, mode_part.shape[1]]
-    conv_wide = signal.astype(jnp.float32)
-    back_wide = back_signal.astype(jnp.float32)
-    hyena_out = (query_feat * conv_wide).astype(jnp.bfloat16)
-    feature_grad = jnp.stack(
-        [grad_out * conv_wide, back_wide * value_feat, back_wide * key_feat]
-    ).astype(jnp.bfloat16)
-    next_rim = from_behind(feature_grad[:, :, :rim_width], "ctx", -1)
-    input_grad = anticausal_short(feature_grad, next_rim, short_filter).astype(jnp.bfloat16)
+    gathered = gathered.reshape(ctx_count, halves, chan_count, grad_cols)
+    gathered = jnp.swapaxes(gathered, 0, 1).reshape(chans_tp, grad_cols)
+    residue_grad = gathered[:, : grad_cols - 1]
+    skip_grad = gathered[:, grad_cols - 1]
     return (hyena_out[None], input_grad[None], residue_grad, skip_grad)
 
 

time: 250 us -> 318 us (1.27)
  starting transfers between devices: 42.9 us -> 72.1 us
  waiting for transfers between devices: 78.7 us -> 107 us
  other arithmetic: 46.7 us -> 61.3 us
  local copies, waits for them, and re-layouts: 49.2 us -> 43.7 us
    all_to_all x4 -> x8, waiting for transfers between devices: 61.2 us -> 82.6 us  [the longest x2 29.6 us: on_device(): lax.all_to_all(back_blocks.reshape(chan_count, length), 'ctx', split_axis...]
    all_to_all x4 -> x8, starting transfers between devices: 20.1 us -> 41.3 us  [the longest x2 14.3 us: on_device(): lax.all_to_all(product[chans], 'ctx', split_axis=0, concat_axis=1, tiled=...]
    convert_element_type x3 -> x0, local copies, waits for them, and re-layouts: 16.3 us -> none  [on_device(): lax.all_to_all(cotangent[0], 'tp', split_axis=0, concat_axis=1, tiled=True)]
    convert_element_type x1 -> x4, other arithmetic: 1.5 us -> 12.9 us  [the longest x2 6.58 us: on_device(): anticausal_short(feature_grad, next_rim, short_filter[:, :, chans])]
    all_to_all x1, waiting for transfers between devices: 0.01 us -> 6.8 us  [on_device(): lax.all_to_all(spread, 'ctx', split_axis=0, concat_axis=0, tiled=True)]
    all_to_all x1, starting transfers between devices: 4.08 us -> 9.87 us  [on_device(): lax.all_to_all(spread, 'ctx', split_axis=0, concat_axis=0, tiled=True)]
    unnamed x7 -> x17, other arithmetic: 7.82 us -> 11.6 us
    convert_element_type x1, other arithmetic: 3.53 us -> 0.31 us  [on_device(): adjoint = (grad_out * query_feat).astype(jnp.bfloat16)]
  transfers between devices with their start and end apart: 10 -> 15, of which waited for: 6 -> 11; matrix products, arithmetic and copies ran while one was open for 29% -> 21% of each run, Pallas kernels for 0% -> 5%
where the time goes in v4:
time: 318 us; the launch traced here: 315 us
  waiting for transfers between devices  107 us (34%)
  starting transfers between devices  72.1 us (23%)
  other arithmetic  61.3 us (19%)
  local copies, waits for them, and re-layouts  43.7 us (14%)
  Pallas kernels  29.9 us (9%)
    pallas_call x2, Pallas kernels, long_conv(): pl.pallas_call(long_conv_kernel, grid=(chan_count // step,), in_specs=[da...  29.9 us
    all_to_all x2, waiting for transfers between devices, on_device(): lax.all_to_all(back_blocks.reshape(chan_count, length), 'ctx', split_axis...  29.6 us
    all_to_all x2, waiting for transfers between devices, on_device(): lax.all_to_all(product[chans], 'ctx', split_axis=0, concat_axis=1, tiled=...  25.1 us
    all_to_all x2, waiting for transfers between devices, on_device(): lax.all_to_all(conv_blocks.reshape(chan_count, length), 'ctx', split_axis...  19.3 us
    all_to_all x1, waiting for transfers between devices, on_device(): lax.all_to_all(cotangent[0], 'tp', split_axis=0, concat_axis=1, tiled=True)  15.6 us
    all_to_all x2, starting transfers between devices, on_device(): lax.all_to_all(product[chans], 'ctx', split_axis=0, concat_axis=1, tiled=...  14.3 us
    unnamed x17, other arithmetic  11.6 us
    all_to_all x1, starting transfers between devices, on_device(): lax.all_to_all(spread, 'ctx', split_axis=0, concat_axis=0, tiled=True)  9.87 us
  transfers between devices with their start and end apart: 15, of which 11 were waited for; matrix products, arithmetic and copies ran while one was open for 21% of the time, Pallas kernels for 5%

profile of v4, /device:TPU:1, one launch (start us, length us, event | category | flops | bytes accessed | tf_op | source)
XLA Modules:
  0.0 315.4 jit_solution(10641561350301959983)
XLA Ops:
  3.9 5.2 %collective-permute-start = (bf16[3,2048,2]{1,2,0:T(2,128)(2,1)}, bf16[3,2048,2]{1,2,0:T(2,128)(2,1)}, u32[]{:S(2)}, u32[]{:S(2)}) collective-permute-start(bf16[3,2048,2]{1,2,0:T(2,128)(2,1)} %copy.117), channel_id=1, source_target_pairs={{0,2},{2,4},{4,6},{6,8},{8,10},{10,12},{12,14},{14,16},{16,18},{18... | collective-permute-start | bytes 73736 | tf_op jit(solution)/shard_map/ppermute | solution.py:18
  18.6 3.3 %maximum_convert_fusion = f32[3,2048,258]{2,1,0:T(8,128)S(1)} fusion(bf16[3,2048,256]{2,1,0:T(8,128)(2,1)S(1)} %bitcast.172, bf16[3,2048,2]{2,1,0:T(8,128)(2,1)} %copy.118), kind=kLoop, calls=%fused_computation.6 | loop fusion | flops 6340608 | bytes 9510912 | tf_op jit(solution)/shard_map/convert_element_type | solution.py:24
  21.9 6.4 %fusion.1 = bf16[3,2048,256]{2,1,0:T(8,128)(2,1)S(1)} fusion(f32[3,2048,258]{2,1,0:T(8,128)S(1)} %maximum_convert_fusion, f32[3,2048]{1,0:T(4,128)S(1)} %get-tuple-element.69, f32[3,2048]{1,0:T(4,128)S(1)} %get-tuple-element.70, f32[3,2048]{1,0:T(4,128)S(1)} %bitcast.197), kind=kLoop, calls=%fused_computation.2 | loop fusion | flops 9437184 | bytes 22093824 | tf_op jit(solution)/shard_map/convert_element_type | solution.py:314
  29.7 7.3 %all-to-all-start = ((bf16[32,32,256]{2,1,0:T(8,128)(2,1)}), bf16[32,32,256]{2,1,0:T(8,128)(2,1)}, u32[]{:S(2)}, u32[]{:S(2)}) async-start(bf16[32,32,256]{2,1,0:T(8,128)(2,1)} %bitcast.189), calls=%async_computation | async-start | bytes 1048576 | tf_op jit(solution)/shard_map/all_to_all | solution.py:330
  41.5 12.4 %all-to-all-done = bf16[32,32,256]{2,1,0:T(8,128)(2,1)} async-done(((bf16[32,32,256]{2,1,0:T(8,128)(2,1)}), bf16[32,32,256]{2,1,0:T(8,128)(2,1)}, u32[]{:S(2)}, u32[]{:S(2)}) %all-to-all-start) | async-done | bytes 524320 | tf_op jit(solution)/shard_map/all_to_all | solution.py:330
  53.9 7.4 %all-to-all-start.1 = ((bf16[2,2048,128]{2,1,0:T(8,128)(2,1)}), bf16[2,2048,128]{2,1,0:T(8,128)(2,1)}, u32[]{:S(2)}, u32[]{:S(2)}) async-start(bf16[2,2048,128]{2,1,0:T(8,128)(2,1)} %bitcast.191), calls=%async_computation.1 | async-start | bytes 2097152 | tf_op jit(solution)/shard_map/all_to_all | solution.py:309
  71.1 15.6 %all-to-all-done.1 = bf16[2,2048,128]{2,1,0:T(8,128)(2,1)} async-done(((bf16[2,2048,128]{2,1,0:T(8,128)(2,1)}), bf16[2,2048,128]{2,1,0:T(8,128)(2,1)}, u32[]{:S(2)}, u32[]{:S(2)}) %all-to-all-start.1) | async-done | bytes 1048608 | tf_op jit(solution)/shard_map/all_to_all | solution.py:309
  86.7 7.0 %all-to-all-start.4 = ((bf16[32,32,256]{2,1,0:T(8,128)(2,1)}), bf16[32,32,256]{2,1,0:T(8,128)(2,1)}, u32[]{:S(2)}, u32[]{:S(2)}) async-start(bf16[32,32,256]{2,1,0:T(8,128)(2,1)} %bitcast.186), calls=%async_computation.4 | async-start | bytes 1048576 | tf_op jit(solution)/shard_map/all_to_all | solution.py:330
  93.6 2.8 convert_bitcast_fusion.1
  97.9 12.6 %all-to-all-done.4 = bf16[32,32,256]{2,1,0:T(8,128)(2,1)} async-done(((bf16[32,32,256]{2,1,0:T(8,128)(2,1)}), bf16[32,32,256]{2,1,0:T(8,128)(2,1)}, u32[]{:S(2)}, u32[]{:S(2)}) %all-to-all-start.4) | async-done | bytes 524320 | tf_op jit(solution)/shard_map/all_to_all | solution.py:330
  110.5 4.4 %all-to-all-start.2 = ((bf16[32,32,256]{2,1,0:T(8,128)(2,1)}), bf16[32,32,256]{2,1,0:T(8,128)(2,1)}, u32[]{:S(2)}, u32[]{:S(2)}) async-start(bf16[32,32,256]{2,1,0:T(8,128)(2,1)} %bitcast.188), calls=%async_computation.2 | async-start | bytes 1048576 | tf_op jit(solution)/shard_map/all_to_all | solution.py:331
  123.1 8.7 %all-to-all-done.2 = bf16[32,32,256]{2,1,0:T(8,128)(2,1)} async-done(((bf16[32,32,256]{2,1,0:T(8,128)(2,1)}), bf16[32,32,256]{2,1,0:T(8,128)(2,1)}, u32[]{:S(2)}, u32[]{:S(2)}) %all-to-all-start.2) | async-done | bytes 524320 | tf_op jit(solution)/shard_map/all_to_all | solution.py:331
  131.8 4.6 %all-to-all-start.5 = ((bf16[32,32,256]{2,1,0:T(8,128)(2,1)}), bf16[32,32,256]{2,1,0:T(8,128)(2,1)}, u32[]{:S(2)}, u32[]{:S(2)}) async-start(bf16[32,32,256]{2,1,0:T(8,128)(2,1)} %bitcast.187), calls=%async_computation.5 | async-start | bytes 1048576 | tf_op jit(solution)/shard_map/all_to_all | solution.py:331
  138.5 14.9 %shard_map.93 = (bf16[32,32,256]{2,1,0:T(8,128)(2,1)}, bf16[32,32,256]{2,1,0:T(8,128)(2,1)}, f32[32,1,16]{2,1,0:T(1,128)}, f32[32,1,128]{2,1,0:T(1,128)}) custom-call(bf16[32,32,256]{2,1,0:T(8,128)(2,1)} %bitcast.193, bf16[32,32,256]{2,1,0:T(8,128)(2,1)} %bitcast.194, f32[32,2,256]{2,1,0:T(2,128)} %pad_maximum_fusion.4.krow_ref, ...), custom_call_target="tpu_custom_call" | custom-call | flops 53687091200 | bytes 4194304 | tf_op jit(solution)/shard_map/pallas_call | solution.py:262
  157.3 15.0 %shard_map.94 = (bf16[32,32,256]{2,1,0:T(8,128)(2,1)}, bf16[32,32,256]{2,1,0:T(8,128)(2,1)}, f32[32,1,16]{2,1,0:T(1,128)}, f32[32,1,128]{2,1,0:T(1,128)}) custom-call(bf16[32,32,256]{2,1,0:T(8,128)(2,1)} %bitcast.192, bf16[32,32,256]{2,1,0:T(8,128)(2,1)} %bitcast.195, f32[32,2,256]{2,1,0:T(2,128)} %pad_maximum_fusion.5.krow_ref, ...), custom_call_target="tpu_custom_call" | custom-call | flops 53687091200 | bytes 4194304 | tf_op jit(solution)/shard_map/pallas_call | solution.py:262
  176.6 2.9 collective-permute-start.4
  181.5 9.9 %all-to-all-start.9 = ((f32[32,1,1088]{2,1,0:T(1,128)}), f32[32,1,1088]{2,1,0:T(1,128)S(1)}, u32[]{:S(2)}, u32[]{:S(2)}) async-start(f32[32,1,1088]{2,1,0:T(1,128)} %reshape.308), calls=%async_computation.9 | async-start | bytes 294912 | tf_op jit(solution)/shard_map/all_to_all | solution.py:384
  193.5 6.8 %all-to-all-done.9 = f32[32,1,1088]{2,1,0:T(1,128)S(1)} async-done(((f32[32,1,1088]{2,1,0:T(1,128)}), f32[32,1,1088]{2,1,0:T(1,128)S(1)}, u32[]{:S(2)}, u32[]{:S(2)}) %all-to-all-start.9) | async-done | bytes 139296 | tf_op jit(solution)/shard_map/all_to_all | solution.py:384
  200.3 4.6 %all-to-all-start.8 = ((bf16[32,32,256]{2,0,1:T(8,128)(2,1)}), bf16[32,32,256]{2,0,1:T(8,128)(2,1)}, u32[]{:S(2)}, u32[]{:S(2)}) async-start(bf16[32,32,256]{2,0,1:T(8,128)(2,1)} %copy.143), calls=%async_computation.8 | async-start | bytes 1048576 | tf_op jit(solution)/shard_map/all_to_all | solution.py:357
  207.1 14.8 %all-to-all-done.8 = bf16[32,32,256]{2,0,1:T(8,128)(2,1)} async-done(((bf16[32,32,256]{2,0,1:T(8,128)(2,1)}), bf16[32,32,256]{2,0,1:T(8,128)(2,1)}, u32[]{:S(2)}, u32[]{:S(2)}) %all-to-all-start.8) | async-done | bytes 524320 | tf_op jit(solution)/shard_map/all_to_all | solution.py:357
  221.9 4.4 %all-to-all-start.7 = ((bf16[32,32,256]{2,0,1:T(8,128)(2,1)}), bf16[32,32,256]{2,0,1:T(8,128)(2,1)}, u32[]{:S(2)}, u32[]{:S(2)}) async-start(bf16[32,32,256]{2,0,1:T(8,128)(2,1)} %copy.139), calls=%async_computation.7 | async-start | bytes 1048576 | tf_op jit(solution)/shard_map/all_to_all | solution.py:357
  228.5 14.8 %all-to-all-done.7 = bf16[32,32,256]{2,0,1:T(8,128)(2,1)} async-done(((bf16[32,32,256]{2,0,1:T(8,128)(2,1)}), bf16[32,32,256]{2,0,1:T(8,128)(2,1)}, u32[]{:S(2)}, u32[]{:S(2)}) %all-to-all-start.7) | async-done | bytes 524320 | tf_op jit(solution)/shard_map/all_to_all | solution.py:357
  243.2 4.4 %all-to-all-start.6 = ((bf16[32,32,256]{2,0,1:T(8,128)(2,1)}), bf16[32,32,256]{2,0,1:T(8,128)(2,1)}, u32[]{:S(2)}, u32[]{:S(2)}) async-start(bf16[32,32,256]{2,0,1:T(8,128)(2,1)} %copy.137), calls=%async_computation.6 | async-start | bytes 1048576 | tf_op jit(solution)/shard_map/all_to_all | solution.py:354
  249.9 14.6 %all-to-all-done.6 = bf16[32,32,256]{2,0,1:T(8,128)(2,1)} async-done(((bf16[32,32,256]{2,0,1:T(8,128)(2,1)}), bf16[32,32,256]{2,0,1:T(8,128)(2,1)}, u32[]{:S(2)}, u32[]{:S(2)}) %all-to-all-start.6) | async-done | bytes 524320 | tf_op jit(solution)/shard_map/all_to_all | solution.py:354
  264.6 4.6 %all-to-all-start.3 = ((bf16[32,32,256]{2,0,1:T(8,128)(2,1)}), bf16[32,32,256]{2,0,1:T(8,128)(2,1)}, u32[]{:S(2)}, u32[]{:S(2)}) async-start(bf16[32,32,256]{2,0,1:T(8,128)(2,1)} %copy.126), calls=%async_computation.3 | async-start | bytes 1048576 | tf_op jit(solution)/shard_map/all_to_all | solution.py:354
  269.2 2.9 slice_convert_fusion
  277.2 4.0 %fusion.17 = (bf16[1024,256]{1,0:T(8,128)(2,1)}, bf16[1024,256]{1,0:T(8,128)(2,1)S(1)}, bf16[1024,256]{1,0:T(8,128)(2,1)S(1)}, bf16[1024,256]{1,0:T(8,128)(2,1)}) fusion(f32[1,2048,256]{2,1,0:T(8,128)} %get-tuple-element.21, bf16[32,32,256]{2,0,1:T(8,128)(2,1)} %all-to-all-done.7, bf16[32,32,256]{2,0,1:T(8,128)(2,1)} %all-to-all-done.8, ...), kind=kLoop, calls=%fused_computation.40 | loop fusion | flops 2621440 | bytes 7340032 | tf_op jit(solution)/shard_map/convert.18
  281.3 4.6 %all-to-all-done.3 = bf16[32,32,256]{2,0,1:T(8,128)(2,1)} async-done(((bf16[32,32,256]{2,0,1:T(8,128)(2,1)}), bf16[32,32,256]{2,0,1:T(8,128)(2,1)}, u32[]{:S(2)}, u32[]{:S(2)}) %all-to-all-start.3) | async-done | bytes 524320 | tf_op jit(solution)/shard_map/all_to_all | solution.py:354
  285.9 3.4 %fusion.23 = (bf16[1024,256]{1,0:T(8,128)(2,1)}, bf16[1024,256]{1,0:T(8,128)(2,1)}, bf16[1024,256]{1,0:T(8,128)(2,1)}, bf16[1024,256]{1,0:T(8,128)(2,1)S(1)}) fusion(f32[1,2048,256]{2,1,0:T(8,128)S(1)} %copy-done.2, bf16[32,32,256]{2,0,1:T(8,128)(2,1)} %all-to-all-done.3, bf16[32,32,256]{2,0,1:T(8,128)(2,1)} %all-to-all-done.6, ...), kind=kLoop, calls=%fused_computation.52 | loop fusion | flops 2621440 | bytes 7340032 | tf_op jit(solution)/shard_map/convert_element_type | solution.py:362
  300.5 3.7 %maximum_convert_fusion.1 = f32[3,1024,258]{2,1,0:T(8,128)} fusion(bf16[3,1024,2]{2,1,0:T(8,128)(2,1)} %copy.141, bf16[1,1024,256]{2,1,0:T(8,128)(2,1)S(1)} %bitcast.178, bf16[1,1024,256]{2,1,0:T(8,128)(2,1)S(1)} %bitcast.180, bf16[1,1024,256]{2,1,0:T(8,128)(2,1)S(1)} %bitcast.184), kind=kLoop, calls=%fused_computation.22 | loop fusion | flops 6340608 | bytes 4755456 | tf_op jit(solution)/shard_map/convert_element_type | solution.py:38
  307.0 3.3 %fusion.7 = bf16[3,1024,256]{2,1,0:T(8,128)(2,1)S(1)} fusion(f32[3,1024,258]{2,1,0:T(8,128)S(1)} %copy-done, f32[3,1024]{1,0:T(4,128)S(1)} %get-tuple-element.76, f32[3,1024]{1,0:T(4,128)S(1)} %get-tuple-element.77, f32[3,1024]{1,0:T(4,128)S(1)} %get-tuple-element.78), kind=kLoop, calls=%fused_computation.15 | loop fusion | flops 4718592 | bytes 11046912 | tf_op jit(solution)/shard_map/convert_element_type | solution.py:368
  310.3 3.3 %fusion.4 = bf16[3,1024,256]{2,1,0:T(8,128)(2,1)S(1)} fusion(f32[3,1024,258]{2,1,0:T(8,128)S(1)} %maximum_convert_fusion.2, f32[3,1024]{1,0:T(4,128)S(1)} %get-tuple-element.73, f32[3,1024]{1,0:T(4,128)S(1)} %get-tuple-element.74, f32[3,1024]{1,0:T(4,128)S(1)} %get-tuple-element.75), kind=kLoop, calls=%fused_computation.9 | loop fusion | flops 4718592 | bytes 11046912 | tf_op jit(solution)/shard_map/convert_element_type | solution.py:368
  (149 shorter events, 79.5 us)
Async XLA Ops:
  0.6 8.5 %copy-start.13 = (f32[2048,16]{0,1:T(8,128)S(1)}, f32[2048,16]{0,1:T(8,128)}, u32[]{:S(2)}) copy-start(f32[2048,16]{0,1:T(8,128)} %param.10) | copy-start | bytes 393220
  2.6 11.2 %copy-start.11 = (f32[3,3,2048]{2,1,0:T(4,128)S(1)}, f32[3,3,2048]{2,1,0:T(4,128)}, u32[]{:S(2)}) copy-start(f32[3,3,2048]{2,1,0:T(4,128)} %param.8) | copy-start | bytes 221188
  3.9 14.7 %copy-start.3 = (bf16[1,3,2048,256]{3,2,1,0:T(8,128)(2,1)S(1)}, bf16[1,3,2048,256]{3,2,1,0:T(8,128)(2,1)}, u32[]{:S(2)}) copy-start(bf16[1,3,2048,256]{3,2,1,0:T(8,128)(2,1)} %param.6) | copy-start | bytes 9437188
  3.9 12.4 %collective-permute-start = (bf16[3,2048,2]{1,2,0:T(2,128)(2,1)}, bf16[3,2048,2]{1,2,0:T(2,128)(2,1)}, u32[]{:S(2)}, u32[]{:S(2)}) collective-permute-start(bf16[3,2048,2]{1,2,0:T(2,128)(2,1)} %copy.117), channel_id=1, source_target_pairs={{0,2},{2,4},{4,6},{6,8},{8,10},{10,12},{12,14},{14,16},{16,18},{18... | collective-permute-start | bytes 73736 | tf_op jit(solution)/shard_map/ppermute | solution.py:18
  9.1 4.3 %copy-start.17 = (f32[256]{0:T(256)}, f32[256]{0:T(256)S(1)}, u32[]{:S(2)}) copy-start(f32[256]{0:T(256)S(1)} %iota_subtract_fusion.1) | copy-start | bytes 3076
  28.6 8.4 %copy-start.14 = (f32[32,1,256]{2,1,0:T(1,128)S(1)}, f32[32,1,256]{2,1,0:T(1,128)}, u32[]{:S(2)}) copy-start(f32[32,1,256]{2,1,0:T(1,128)} %stack.120) | copy-start | bytes 98308
  28.7 9.1 %copy-start.18 = (f32[256]{0:T(256)S(1)}, f32[256]{0:T(256)}, u32[]{:S(2)}) copy-start(f32[256]{0:T(256)} %copy-done.17) | copy-start | bytes 3076
  29.7 24.2 %all-to-all-start = ((bf16[32,32,256]{2,1,0:T(8,128)(2,1)}), bf16[32,32,256]{2,1,0:T(8,128)(2,1)}, u32[]{:S(2)}, u32[]{:S(2)}) async-start(bf16[32,32,256]{2,1,0:T(8,128)(2,1)} %bitcast.189), calls=%async_computation | async-start | bytes 1048576 | tf_op jit(solution)/shard_map/all_to_all | solution.py:330
  37.8 25.9 %copy-start.15 = (f32[32,16]{1,0:T(8,128)S(1)}, f32[32,16]{1,0:T(8,128)}, u32[]{:S(2)}) copy-start(f32[32,16]{1,0:T(8,128)} %get-tuple-element.55) | copy-start | bytes 6148
  37.8 25.9 %copy-start.16 = (f32[32,16]{1,0:T(8,128)S(1)}, f32[32,16]{1,0:T(8,128)}, u32[]{:S(2)}) copy-start(f32[32,16]{1,0:T(8,128)} %get-tuple-element.56) | copy-start | bytes 6148
  53.9 32.7 %all-to-all-start.1 = ((bf16[2,2048,128]{2,1,0:T(8,128)(2,1)}), bf16[2,2048,128]{2,1,0:T(8,128)(2,1)}, u32[]{:S(2)}, u32[]{:S(2)}) async-start(bf16[2,2048,128]{2,1,0:T(8,128)(2,1)} %bitcast.191), calls=%async_computation.1 | async-start | bytes 2097152 | tf_op jit(solution)/shard_map/all_to_all | solution.py:309
  86.7 23.8 %all-to-all-start.4 = ((bf16[32,32,256]{2,1,0:T(8,128)(2,1)}), bf16[32,32,256]{2,1,0:T(8,128)(2,1)}, u32[]{:S(2)}, u32[]{:S(2)}) async-start(bf16[32,32,256]{2,1,0:T(8,128)(2,1)} %bitcast.186), calls=%async_computation.4 | async-start | bytes 1048576 | tf_op jit(solution)/shard_map/all_to_all | solution.py:330
  96.8 18.1 %copy-start.19 = (f32[256]{0:T(256)S(1)}, f32[256]{0:T(256)}, u32[]{:S(2)}) copy-start(f32[256]{0:T(256)} %iota_add_fusion) | copy-start | bytes 3076
  110.5 21.3 %all-to-all-start.2 = ((bf16[32,32,256]{2,1,0:T(8,128)(2,1)}), bf16[32,32,256]{2,1,0:T(8,128)(2,1)}, u32[]{:S(2)}, u32[]{:S(2)}) async-start(bf16[32,32,256]{2,1,0:T(8,128)(2,1)} %bitcast.188), calls=%async_computation.2 | async-start | bytes 1048576 | tf_op jit(solution)/shard_map/all_to_all | solution.py:331
  131.8 23.3 %all-to-all-start.5 = ((bf16[32,32,256]{2,1,0:T(8,128)(2,1)}), bf16[32,32,256]{2,1,0:T(8,128)(2,1)}, u32[]{:S(2)}, u32[]{:S(2)}) async-start(bf16[32,32,256]{2,1,0:T(8,128)(2,1)} %bitcast.187), calls=%async_computation.5 | async-start | bytes 1048576 | tf_op jit(solution)/shard_map/all_to_all | solution.py:331
  173.9 2.6 collective-permute-start.3
  176.6 4.1 %collective-permute-start.4 = (f32[64,17]{0,1:T(8,128)S(1)}, f32[64,17]{0,1:T(8,128)S(1)}, u32[]{:S(2)}, u32[]{:S(2)}) collective-permute-start(f32[64,17]{0,1:T(8,128)S(1)} %fusion.53), channel_id=1, source_target_pairs={{0,128},{64,192},{128,0},{192,64},{1,129},{65,193},{129,1},{193,65... | collective-permute-start | bytes 13064 | tf_op jit(solution)/shard_map/ppermute | solution.py:379
  181.5 18.8 %all-to-all-start.9 = ((f32[32,1,1088]{2,1,0:T(1,128)}), f32[32,1,1088]{2,1,0:T(1,128)S(1)}, u32[]{:S(2)}, u32[]{:S(2)}) async-start(f32[32,1,1088]{2,1,0:T(1,128)} %reshape.308), calls=%async_computation.9 | async-start | bytes 294912 | tf_op jit(solution)/shard_map/all_to_all | solution.py:384
  200.3 21.6 %all-to-all-start.8 = ((bf16[32,32,256]{2,0,1:T(8,128)(2,1)}), bf16[32,32,256]{2,0,1:T(8,128)(2,1)}, u32[]{:S(2)}, u32[]{:S(2)}) async-start(bf16[32,32,256]{2,0,1:T(8,128)(2,1)} %copy.143), calls=%async_computation.8 | async-start | bytes 1048576 | tf_op jit(solution)/shard_map/all_to_all | solution.py:357
  204.9 42.7 %copy-start.12 = (f32[3,3,2048]{2,1,0:T(4,128)S(1)}, f32[3,3,2048]{2,1,0:T(4,128)}, u32[]{:S(2)}) copy-start(f32[3,3,2048]{2,1,0:T(4,128)} %param.8) | copy-start | bytes 221188
  221.9 21.3 %all-to-all-start.7 = ((bf16[32,32,256]{2,0,1:T(8,128)(2,1)}), bf16[32,32,256]{2,0,1:T(8,128)(2,1)}, u32[]{:S(2)}, u32[]{:S(2)}) async-start(bf16[32,32,256]{2,0,1:T(8,128)(2,1)} %copy.139), calls=%async_computation.7 | async-start | bytes 1048576 | tf_op jit(solution)/shard_map/all_to_all | solution.py:357
  243.2 21.3 %all-to-all-start.6 = ((bf16[32,32,256]{2,0,1:T(8,128)(2,1)}), bf16[32,32,256]{2,0,1:T(8,128)(2,1)}, u32[]{:S(2)}, u32[]{:S(2)}) async-start(bf16[32,32,256]{2,0,1:T(8,128)(2,1)} %copy.137), calls=%async_computation.6 | async-start | bytes 1048576 | tf_op jit(solution)/shard_map/all_to_all | solution.py:354
  264.6 21.3 %all-to-all-start.3 = ((bf16[32,32,256]{2,0,1:T(8,128)(2,1)}), bf16[32,32,256]{2,0,1:T(8,128)(2,1)}, u32[]{:S(2)}, u32[]{:S(2)}) async-start(bf16[32,32,256]{2,0,1:T(8,128)(2,1)} %copy.126), calls=%async_computation.3 | async-start | bytes 1048576 | tf_op jit(solution)/shard_map/all_to_all | solution.py:354
  277.2 8.6 %copy-start.2 = (f32[1,2048,256]{2,1,0:T(8,128)S(1)}, f32[1,2048,256]{2,1,0:T(8,128)}, u32[]{:S(2)}) copy-start(f32[1,2048,256]{2,1,0:T(8,128)} %get-tuple-element.22) | copy-start | bytes 6291460
  285.9 4.2 %copy-start.4 = (bf16[1024,256]{1,0:T(8,128)(2,1)S(1)}, bf16[1024,256]{1,0:T(8,128)(2,1)}, u32[]{:S(2)}) copy-start(bf16[1024,256]{1,0:T(8,128)(2,1)} %get-tuple-element.27) | copy-start | bytes 1572868
  285.9 4.2 %copy-start.6 = (bf16[1024,256]{1,0:T(8,128)(2,1)S(1)}, bf16[1024,256]{1,0:T(8,128)(2,1)}, u32[]{:S(2)}) copy-start(bf16[1024,256]{1,0:T(8,128)(2,1)} %get-tuple-element.32) | copy-start | bytes 1572868
  289.3 3.3 %copy-start.8 = (bf16[1024,256]{1,0:T(8,128)(2,1)S(1)}, bf16[1024,256]{1,0:T(8,128)(2,1)}, u32[]{:S(2)}) copy-start(bf16[1024,256]{1,0:T(8,128)(2,1)} %get-tuple-element.39) | copy-start | bytes 1572868
  290.5 8.8 %collective-permute-start.1 = (bf16[3,1024,2]{1,2,0:T(2,128)(2,1)S(1)}, bf16[3,1024,2]{1,2,0:T(2,128)(2,1)S(1)}, u32[]{:S(2)}, u32[]{:S(2)}) collective-permute-start(bf16[3,1024,2]{1,2,0:T(2,128)(2,1)S(1)} %copy.140), channel_id=1, source_target_pairs={{2,0},{4,2},{6,4},{8,6},{10,8},{12,10},{14,12},{16,14},{18,16},{20... | collective-permute-start | bytes 36872 | tf_op jit(solution)/shard_map/ppermute | solution.py:18
  293.6 6.9 %copy-start.5 = (bf16[1024,256]{1,0:T(8,128)(2,1)S(1)}, bf16[1024,256]{1,0:T(8,128)(2,1)}, u32[]{:S(2)}) copy-start(bf16[1024,256]{1,0:T(8,128)(2,1)} %get-tuple-element.27) | copy-start | bytes 1572868
  293.6 6.9 %copy-start.7 = (bf16[1024,256]{1,0:T(8,128)(2,1)S(1)}, bf16[1024,256]{1,0:T(8,128)(2,1)}, u32[]{:S(2)}) copy-start(bf16[1024,256]{1,0:T(8,128)(2,1)} %get-tuple-element.32) | copy-start | bytes 1572868
  293.6 6.9 %copy-start.10 = (bf16[1024,256]{1,0:T(8,128)(2,1)S(1)}, bf16[1024,256]{1,0:T(8,128)(2,1)}, u32[]{:S(2)}) copy-start(bf16[1024,256]{1,0:T(8,128)(2,1)} %copy-done.9) | copy-start | bytes 1572868
  295.2 9.1 %collective-permute-start.2 = (bf16[3,1024,2]{1,2,0:T(2,128)(2,1)S(1)}, bf16[3,1024,2]{1,2,0:T(2,128)(2,1)S(1)}, u32[]{:S(2)}, u32[]{:S(2)}) collective-permute-start(bf16[3,1024,2]{1,2,0:T(2,128)(2,1)S(1)} %copy.144), channel_id=1, source_target_pairs={{2,0},{4,2},{6,4},{8,6},{10,8},{12,10},{14,12},{16,14},{18,16},{20... | collective-permute-start | bytes 36872 | tf_op jit(solution)/shard_map/ppermute | solution.py:18
  (3 other events, 6.1 us)

commit v5 on v3

--- a/solution.py
+++ b/solution.py
@@ -306,9 +306,20 @@
     token_count = proj_rows.shape[2]
     chans_tp = proj_rows.shape[1]
     rim_width = short_filter.shape[1] - 1
-    grad_out = lax.all_to_all(cotangent[0], "tp", split_axis=0, concat_axis=1, tiled=True).astype(
-        jnp.float32
-    )
+    tp_count = lax.axis_size("tp")
+    if tp_count == 2:
+        tp_index = lax.axis_index("tp")
+        grad_rows = cotangent[0]
+        mine = lax.dynamic_slice_in_dim(grad_rows, tp_index * chans_tp, chans_tp, 0)
+        other = lax.dynamic_slice_in_dim(grad_rows, (1 - tp_index) * chans_tp, chans_tp, 0)
+        theirs = lax.ppermute(other, "tp", [(0, 1), (1, 0)])
+        first = jnp.where(tp_index == 0, mine, theirs)
+        second = jnp.where(tp_index == 0, theirs, mine)
+        grad_out = jnp.concatenate([first, second], axis=1).astype(jnp.float32)
+    else:
+        grad_out = lax.all_to_all(
+            cotangent[0], "tp", split_axis=0, concat_axis=1, tiled=True
+        ).astype(jnp.float32)
     prev_rim = from_behind(proj_rows[:, :, token_count - rim_width :], "ctx", 1)
     featured = lax.optimization_barrier(
         causal_short(proj_rows, prev_rim, short_filter).astype(jnp.bfloat16)
@@ -361,8 +372,23 @@
             hop *= 2
     else:
         local_grads = lax.psum(local_grads, "dp")
-    spread = jnp.broadcast_to(local_grads[None], (ctx_count,) + local_grads.shape)
-    gathered = lax.all_to_all(spread, "ctx", split_axis=0, concat_axis=0, tiled=True)
+    if ctx_count & (ctx_count - 1) == 0:
+        ctx_index = lax.axis_index("ctx")
+        gathered = local_grads
+        hop = 1
+        while hop < ctx_count:
+            partners = [(i, i ^ hop) for i in range(ctx_count)]
+            theirs = lax.ppermute(gathered, "ctx", partners)
+            low_side = (ctx_index & hop) == 0
+            gathered = jnp.where(
+                low_side,
+                jnp.concatenate([gathered, theirs], axis=0),
+                jnp.concatenate([theirs, gathered], axis=0),
+            )
+            hop *= 2
+    else:
+        spread = jnp.broadcast_to(local_grads[None], (ctx_count,) + local_grads.shape)
+        gathered = lax.all_to_all(spread, "ctx", split_axis=0, concat_axis=0, tiled=True)
     gathered = gathered.reshape(chans_tp, local_grads.shape[1])
     residue_grad = gathered[:, : mode_part.shape[1]]
     skip_grad = gathered[:, mode_part.shape[1]]

time: 250 us -> 230 us (0.920); the launches traced: 247 us -> 229 us
  local copies, waits for them, and re-layouts: 49.2 us -> 30.3 us
  starting transfers between devices: 42.9 us -> 53.5 us
  other arithmetic: 46.7 us -> 41.2 us
  waiting for transfers between devices: 78.7 us -> 75.3 us
    ppermute x0 -> x6, starting transfers between devices: none -> 17.9 us  [the longest x5 11.9 us: on_device(): theirs = lax.ppermute(gathered, 'ctx', partners)]
    all_to_all x1, waiting for transfers between devices: 16.6 us -> 0.01 us  [on_device(): lax.all_to_all(conv_rows, 'ctx', split_axis=1, concat_axis=0, tiled=True)]
    convert_element_type x3 -> x0, local copies, waits for them, and re-layouts: 16.3 us -> none  [on_device(): lax.all_to_all(cotangent[0], 'tp', split_axis=0, concat_axis=1, tiled=True)]
    all_to_all x2 -> x0, waiting for transfers between devices: 15.8 us -> none  [the longest x1 15.8 us: on_device(): lax.all_to_all(cotangent[0], 'tp', split_axis=0, concat_axis=1, tiled=True)]
    all_to_all x1, waiting for transfers between devices: 7.01 us -> 22 us  [on_device(): lax.all_to_all(product, 'ctx', split_axis=0, concat_axis=1, tiled=True)]
    ppermute x0 -> x6, waiting for transfers between devices: none -> 12.8 us  [the longest x5 12.3 us: on_device(): theirs = lax.ppermute(gathered, 'ctx', partners)]
    all_to_all x2 -> x0, starting transfers between devices: 11.4 us -> none  [the longest x1 7.29 us: on_device(): lax.all_to_all(cotangent[0], 'tp', split_axis=0, concat_axis=1, tiled=True)]
  transfers between devices with their start and end apart: 10 -> 14, of which waited for: 6 -> 10; matrix products, arithmetic and copies ran while one was open for 29% -> 20% of each run, Pallas kernels for 0% -> 0%
where the time goes in v5:
time: 230 us; the launch traced here: 229 us
  waiting for transfers between devices  75.3 us (33%)
  starting transfers between devices  53.5 us (23%)
  other arithmetic  41.2 us (18%)
  local copies, waits for them, and re-layouts  30.3 us (13%)
  Pallas kernels  28.2 us (12%)
    pallas_call x1, Pallas kernels, long_conv(): pl.pallas_call(long_conv_kernel, grid=(chan_count // step,), in_specs=[da...  28.2 us
    all_to_all x1, waiting for transfers between devices, on_device(): lax.all_to_all(back_rows, 'ctx', split_axis=1, concat_axis=0, tiled=True)  25.3 us
    all_to_all x1, waiting for transfers between devices, on_device(): lax.all_to_all(product, 'ctx', split_axis=0, concat_axis=1, tiled=True)  22 us
    ppermute x5, waiting for transfers between devices, on_device(): theirs = lax.ppermute(gathered, 'ctx', partners)  12.3 us
    all_to_all x1, waiting for transfers between devices, on_device(): lax.all_to_all(adjoint, 'ctx', split_axis=0, concat_axis=1, tiled=True)  12.2 us
    ppermute x5, starting transfers between devices, on_device(): theirs = lax.ppermute(gathered, 'ctx', partners)  11.9 us
    ppermute x2, starting transfers between devices, from_behind(): return lax.ppermute(shard, axis, pairs)  9.44 us
    unnamed x7, other arithmetic  7.86 us
  transfers between devices with their start and end apart: 14, of which 10 were waited for; matrix products, arithmetic and copies ran while one was open for 20% of the time, Pallas kernels for 0%

profile of v5, /device:TPU:1, one launch (start us, length us, event | category | flops | bytes accessed | tf_op | source)
XLA Modules:
  0.0 229.4 jit_solution(8046372622820761852)
XLA Ops:
  0.7 3.2 %slice.71 = bf16[3,2048,2]{2,1,0:T(8,128)(2,1)} slice(bf16[3,2048,256]{2,1,0:T(8,128)(2,1)} %bitcast.64), slice={[0:3], [0:2048], [254:256]} | slice | bytes 49152 | tf_op jit(solution)/shard_map/slice | solution.py:323
  3.9 1.7 copy.98
  5.6 4.9 %collective-permute-start = (bf16[3,2048,2]{1,2,0:T(2,128)(2,1)S(1)}, bf16[3,2048,2]{1,2,0:T(2,128)(2,1)S(1)}, u32[]{:S(2)}, u32[]{:S(2)}) collective-permute-start(bf16[3,2048,2]{1,2,0:T(2,128)(2,1)S(1)} %copy.98), channel_id=1, source_target_pairs={{0,2},{2,4},{4,6},{6,8},{8,10},{10,12},{12,14},{14,16},{16,18},{18... | collective-permute-start | bytes 73736 | tf_op jit(solution)/shard_map/ppermute | solution.py:18
  10.5 1.9 dynamic-slice_bitcast_fusion
  12.4 6.0 %collective-permute-start.1 = (bf16[2048,128]{1,0:T(8,128)(2,1)}, bf16[2048,128]{1,0:T(8,128)(2,1)}, u32[]{:S(2)}, u32[]{:S(2)}) collective-permute-start(bf16[2048,128]{1,0:T(8,128)(2,1)} %dynamic-slice_bitcast_fusion), channel_id=1, source_target_pairs={{0,1},{1,0},{2,3},{3,2},{4,5},{5,4},{6,7},{7,6},{8,9},{9,8},{10,11... | collective-permute-start | bytes 1572872 | tf_op jit(solution)/shard_map/ppermute | solution.py:315
  20.2 3.3 %maximum_convert_fusion = f32[3,2048,258]{2,1,0:T(8,128)S(1)} fusion(bf16[3,2048,256]{2,1,0:T(8,128)(2,1)S(1)} %bitcast.65, bf16[3,2048,2]{2,1,0:T(8,128)(2,1)} %copy.99), kind=kLoop, calls=%fused_computation.12 | loop fusion | flops 6340608 | bytes 9510912 | tf_op jit(solution)/shard_map/convert_element_type | solution.py:24
  23.5 6.4 %fusion.4 = bf16[3,2048,256]{2,1,0:T(8,128)(2,1)S(1)} fusion(f32[3,2048,258]{2,1,0:T(8,128)S(1)} %maximum_convert_fusion, f32[3,2048]{1,0:T(4,128)S(1)} %get-tuple-element.38, f32[3,2048]{1,0:T(4,128)S(1)} %get-tuple-element.39, f32[3,2048]{1,0:T(4,128)S(1)} %bitcast.74), kind=kLoop, calls=%fused_computation.8 | loop fusion | flops 9437184 | bytes 22093824 | tf_op jit(solution)/shard_map/convert_element_type | solution.py:325
  31.1 7.5 %all-to-all-start = ((bf16[32,64,256]{2,1,0:T(8,128)(2,1)}), bf16[32,64,256]{2,1,0:T(8,128)(2,1)}, u32[]{:S(2)}, u32[]{:S(2)}) async-start(bf16[32,64,256]{2,1,0:T(8,128)(2,1)} %bitcast.70), calls=%async_computation | async-start | bytes 2097152 | tf_op jit(solution)/shard_map/all_to_all | solution.py:336
  45.0 22.0 %all-to-all-done = bf16[32,64,256]{2,1,0:T(8,128)(2,1)} async-done(((bf16[32,64,256]{2,1,0:T(8,128)(2,1)}), bf16[32,64,256]{2,1,0:T(8,128)(2,1)}, u32[]{:S(2)}, u32[]{:S(2)}) %all-to-all-start) | async-done | bytes 1048608 | tf_op jit(solution)/shard_map/all_to_all | solution.py:336
  67.0 5.3 %all-to-all-start.1 = ((bf16[32,64,256]{2,1,0:T(8,128)(2,1)}), bf16[32,64,256]{2,1,0:T(8,128)(2,1)}, u32[]{:S(2)}, u32[]{:S(2)}) async-start(bf16[32,64,256]{2,1,0:T(8,128)(2,1)} %multiply_convert_fusion), calls=%async_computation.1 | async-start | bytes 2097152 | tf_op jit(solution)/shard_map/all_to_all | solution.py:337
  73.5 1.9 stack.62.row_ref
  85.3 2.8 %copy.130 = bf16[32,64,256]{2,0,1:T(8,128)(2,1)} copy(bf16[32,64,256]{2,1,0:T(8,128)(2,1)} %all-to-all-done) | data formatting | bytes 2097152 | tf_op jit(solution)/shard_map/all_to_all | solution.py:336
  88.0 12.2 %all-to-all-done.1 = bf16[32,64,256]{2,1,0:T(8,128)(2,1)} async-done(((bf16[32,64,256]{2,1,0:T(8,128)(2,1)}), bf16[32,64,256]{2,1,0:T(8,128)(2,1)}, u32[]{:S(2)}, u32[]{:S(2)}) %all-to-all-start.1) | async-done | bytes 1048608 | tf_op jit(solution)/shard_map/all_to_all | solution.py:337
  100.2 2.8 %copy.129 = bf16[32,64,256]{2,0,1:T(8,128)(2,1)} copy(bf16[32,64,256]{2,1,0:T(8,128)(2,1)} %all-to-all-done.1) | data formatting | bytes 2097152 | tf_op jit(solution)/shard_map/all_to_all | solution.py:337
  103.0 28.2 %shard_map.93 = (bf16[64,32,256]{2,1,0:T(8,128)(2,1)}, bf16[64,32,256]{2,1,0:T(8,128)(2,1)}, f32[64,1,16]{2,1,0:T(1,128)}, f32[64,1,128]{2,1,0:T(1,128)}) custom-call(bf16[64,32,256]{2,1,0:T(8,128)(2,1)} %bitcast.71, bf16[64,32,256]{2,1,0:T(8,128)(2,1)} %bitcast.72, f32[64,2,256]{2,1,0:T(2,128)} %pad_maximum_fusion.2.krow_ref, ...), custom_call_target="tpu_custom_call" | custom-call | flops 4563402752 | bytes 8388608 | tf_op jit(solution)/shard_map/pallas_call | solution.py:262
  131.2 2.8 %copy.113 = bf16[64,32,256]{2,0,1:T(8,128)(2,1)} copy(bf16[64,32,256]{2,1,0:T(8,128)(2,1)} %get-tuple-element.9) | data formatting | bytes 2097152 | tf_op jit(solution)/shard_map/pallas_call | solution.py:262
  134.0 4.6 %all-to-all-start.3 = ((bf16[64,32,256]{2,0,1:T(8,128)(2,1)}), bf16[64,32,256]{2,0,1:T(8,128)(2,1)}, u32[]{:S(2)}, u32[]{:S(2)}) async-start(bf16[64,32,256]{2,0,1:T(8,128)(2,1)} %copy.113), calls=%async_computation.3 | async-start | bytes 2097152 | tf_op jit(solution)/shard_map/all_to_all | solution.py:360
  138.6 2.8 %copy.112 = bf16[64,32,256]{2,0,1:T(8,128)(2,1)} copy(bf16[64,32,256]{2,1,0:T(8,128)(2,1)} %get-tuple-element.8) | data formatting | bytes 2097152 | tf_op jit(solution)/shard_map/pallas_call | solution.py:262
  141.4 25.3 %all-to-all-done.3 = bf16[64,32,256]{2,0,1:T(8,128)(2,1)} async-done(((bf16[64,32,256]{2,0,1:T(8,128)(2,1)}), bf16[64,32,256]{2,0,1:T(8,128)(2,1)}, u32[]{:S(2)}, u32[]{:S(2)}) %all-to-all-start.3) | async-done | bytes 1048608 | tf_op jit(solution)/shard_map/all_to_all | solution.py:360
  166.6 4.6 %all-to-all-start.2 = ((bf16[64,32,256]{2,0,1:T(8,128)(2,1)}), bf16[64,32,256]{2,0,1:T(8,128)(2,1)}, u32[]{:S(2)}, u32[]{:S(2)}) async-start(bf16[64,32,256]{2,0,1:T(8,128)(2,1)} %copy.112), calls=%async_computation.2 | async-start | bytes 2097152 | tf_op jit(solution)/shard_map/all_to_all | solution.py:359
  174.9 2.9 %collective-permute-start.4 = (f32[64,17]{0,1:T(8,128)S(1)}, f32[64,17]{0,1:T(8,128)S(1)}, u32[]{:S(2)}, u32[]{:S(2)}) collective-permute-start(f32[64,17]{0,1:T(8,128)S(1)} %fusion.24), channel_id=1, source_target_pairs={{0,128},{64,192},{128,0},{192,64},{1,129},{65,193},{129,1},{193,65... | collective-permute-start | bytes 13064 | tf_op jit(solution)/shard_map/ppermute | solution.py:371
  179.2 2.1 collective-permute-start.5
  183.6 5.0 %collective-permute-done.6 = f32[128,17]{0,1:T(8,128)S(1)} collective-permute-done((f32[128,17]{0,1:T(8,128)S(1)}, f32[128,17]{0,1:T(8,128)S(1)}, u32[]{:S(2)}, u32[]{:S(2)}) %collective-permute-start.6) | collective-permute-done | bytes 8736 | tf_op jit(solution)/shard_map/ppermute | solution.py:381
  188.6 4.2 %collective-permute-start.7 = (f32[256,17]{0,1:T(8,128)S(1)}, f32[256,17]{0,1:T(8,128)S(1)}, u32[]{:S(2)}, u32[]{:S(2)}) collective-permute-start(f32[256,17]{0,1:T(8,128)S(1)} %maximum_select_fusion.3), channel_id=1, source_target_pairs={{0,8},{2,10},{4,12},{6,14},{8,0},{10,2},{12,4},{14,6},{16,24},{18,... | collective-permute-start | bytes 52232 | tf_op jit(solution)/shard_map/ppermute | solution.py:381
  192.8 4.8 %collective-permute-done.7 = f32[256,17]{0,1:T(8,128)S(1)} collective-permute-done((f32[256,17]{0,1:T(8,128)S(1)}, f32[256,17]{0,1:T(8,128)S(1)}, u32[]{:S(2)}, u32[]{:S(2)}) %collective-permute-start.7) | collective-permute-done | bytes 17440 | tf_op jit(solution)/shard_map/ppermute | solution.py:381
  198.9 1.7 collective-permute-done.8
  200.6 2.9 %collective-permute-start.9 = (f32[1024,17]{0,1:T(8,128)S(1)}, f32[1024,17]{0,1:T(8,128)S(1)}, u32[]{:S(2)}, u32[]{:S(2)}) collective-permute-start(f32[1024,17]{0,1:T(8,128)S(1)} %maximum_select_fusion.1), channel_id=1, source_target_pairs={{0,32},{2,34},{4,36},{6,38},{8,40},{10,42},{12,44},{14,46},{16,48}... | collective-permute-start | bytes 208904 | tf_op jit(solution)/shard_map/ppermute | solution.py:381
  203.5 3.7 %fusion.9 = (bf16[1,2048,256]{2,1,0:T(8,128)(2,1)S(1)}, bf16[1,2048,256]{2,1,0:T(8,128)(2,1)S(1)}, bf16[1,2048,256]{2,1,0:T(8,128)(2,1)}, bf16[1,2048,256]{2,1,0:T(8,128)(2,1)S(1)}) fusion(bf16[64,32,256]{2,0,1:T(8,128)(2,1)} %all-to-all-done.3, bf16[3,2048,256]{2,1,0:T(8,128)(2,1)S(1)} %fusion.4, bf16[64,32,256]{2,0,1:T(8,128)(2,1)} %all-to-all-done.2, ...), kind=kLoop, calls=%fused_computation.20 | loop fusion | flops 8912896 | bytes 10485760 | tf_op jit(solution)/shard_map/convert.6
  210.2 1.9 copy.114
  212.1 4.5 %collective-permute-start.2 = (bf16[3,2048,2]{1,2,0:T(2,128)(2,1)S(1)}, bf16[3,2048,2]{1,2,0:T(2,128)(2,1)S(1)}, u32[]{:S(2)}, u32[]{:S(2)}) collective-permute-start(bf16[3,2048,2]{1,2,0:T(2,128)(2,1)S(1)} %copy.114), channel_id=1, source_target_pairs={{2,0},{4,2},{6,4},{8,6},{10,8},{12,10},{14,12},{16,14},{18,16},{20... | collective-permute-start | bytes 73736 | tf_op jit(solution)/shard_map/ppermute | solution.py:18
  219.5 2.6 %maximum_convert_fusion.1 = f32[3,2048,258]{2,1,0:T(8,128)S(1)} fusion(bf16[3,2048,2]{2,1,0:T(8,128)(2,1)} %copy.115, bf16[1,2048,256]{2,1,0:T(8,128)(2,1)S(1)} %copy-done.3, bf16[1,2048,256]{2,1,0:T(8,128)(2,1)S(1)} %copy-done.1, bf16[1,2048,256]{2,1,0:T(8,128)(2,1)S(1)} %copy-done.5), kind=kLoop, calls=%fused_computation.13 | loop fusion | flops 12681216 | bytes 9510912 | tf_op jit(solution)/shard_map/convert_element_type | solution.py:38
  222.1 7.3 %fusion.6 = bf16[1,3,2048,256]{3,2,1,0:T(8,128)(2,1)} fusion(f32[3,2048,258]{2,1,0:T(8,128)S(1)} %maximum_convert_fusion.1, f32[3,2048]{1,0:T(4,128)S(1)} %get-tuple-element.38, f32[3,2048]{1,0:T(4,128)S(1)} %get-tuple-element.39, f32[3,2048]{1,0:T(4,128)S(1)} %bitcast.75), kind=kLoop, calls=%fused_computation.14 | loop fusion | flops 9437184 | bytes 22093824 | tf_op jit(solution)/shard_map/broadcast_in_dim | solution.py:403
  (82 shorter events, 34.9 us)
Async XLA Ops:
  0.6 19.5 %copy-start.6 = (bf16[1,3,2048,256]{3,2,1,0:T(8,128)(2,1)S(1)}, bf16[1,3,2048,256]{3,2,1,0:T(8,128)(2,1)}, u32[]{:S(2)}) copy-start(bf16[1,3,2048,256]{3,2,1,0:T(8,128)(2,1)} %param.6) | copy-start | bytes 9437188
  0.6 17.8 %copy-start.10 = (f32[3,3,2048]{2,1,0:T(4,128)S(1)}, f32[3,3,2048]{2,1,0:T(4,128)}, u32[]{:S(2)}) copy-start(f32[3,3,2048]{2,1,0:T(4,128)} %param.8) | copy-start | bytes 221188
  5.6 13.0 %collective-permute-start = (bf16[3,2048,2]{1,2,0:T(2,128)(2,1)S(1)}, bf16[3,2048,2]{1,2,0:T(2,128)(2,1)S(1)}, u32[]{:S(2)}, u32[]{:S(2)}) collective-permute-start(bf16[3,2048,2]{1,2,0:T(2,128)(2,1)S(1)} %copy.98), channel_id=1, source_target_pairs={{0,2},{2,4},{4,6},{6,8},{8,10},{10,12},{12,14},{14,16},{16,18},{18... | collective-permute-start | bytes 73736 | tf_op jit(solution)/shard_map/ppermute | solution.py:18
  12.4 29.0 %collective-permute-start.1 = (bf16[2048,128]{1,0:T(8,128)(2,1)}, bf16[2048,128]{1,0:T(8,128)(2,1)}, u32[]{:S(2)}, u32[]{:S(2)}) collective-permute-start(bf16[2048,128]{1,0:T(8,128)(2,1)} %dynamic-slice_bitcast_fusion), channel_id=1, source_target_pairs={{0,1},{1,0},{2,3},{3,2},{4,5},{5,4},{6,7},{7,6},{8,9},{9,8},{10,11... | collective-permute-start | bytes 1572872 | tf_op jit(solution)/shard_map/ppermute | solution.py:315
  31.1 35.9 %all-to-all-start = ((bf16[32,64,256]{2,1,0:T(8,128)(2,1)}), bf16[32,64,256]{2,1,0:T(8,128)(2,1)}, u32[]{:S(2)}, u32[]{:S(2)}) async-start(bf16[32,64,256]{2,1,0:T(8,128)(2,1)} %bitcast.70), calls=%async_computation | async-start | bytes 2097152 | tf_op jit(solution)/shard_map/all_to_all | solution.py:336
  39.6 1.8 copy-start.9
  42.7 0.8 copy-start.7
  42.7 1.0 copy-start.8
  67.0 33.2 %all-to-all-start.1 = ((bf16[32,64,256]{2,1,0:T(8,128)(2,1)}), bf16[32,64,256]{2,1,0:T(8,128)(2,1)}, u32[]{:S(2)}, u32[]{:S(2)}) async-start(bf16[32,64,256]{2,1,0:T(8,128)(2,1)} %multiply_convert_fusion), calls=%async_computation.1 | async-start | bytes 2097152 | tf_op jit(solution)/shard_map/all_to_all | solution.py:337
  131.2 40.0 %copy-start.11 = (f32[64,1,16]{2,1,0:T(1,128)S(1)}, f32[64,1,16]{2,1,0:T(1,128)}, u32[]{:S(2)}) copy-start(f32[64,1,16]{2,1,0:T(1,128)} %get-tuple-element.10) | copy-start | bytes 12292
  131.2 40.1 %copy-start.12 = (f32[64,1,128]{2,1,0:T(1,128)S(1)}, f32[64,1,128]{2,1,0:T(1,128)}, u32[]{:S(2)}) copy-start(f32[64,1,128]{2,1,0:T(1,128)} %get-tuple-element.11) | copy-start | bytes 98308
  134.0 32.6 %all-to-all-start.3 = ((bf16[64,32,256]{2,0,1:T(8,128)(2,1)}), bf16[64,32,256]{2,0,1:T(8,128)(2,1)}, u32[]{:S(2)}, u32[]{:S(2)}) async-start(bf16[64,32,256]{2,0,1:T(8,128)(2,1)} %copy.113), calls=%async_computation.3 | async-start | bytes 2097152 | tf_op jit(solution)/shard_map/all_to_all | solution.py:360
  166.6 36.9 %all-to-all-start.2 = ((bf16[64,32,256]{2,0,1:T(8,128)(2,1)}), bf16[64,32,256]{2,0,1:T(8,128)(2,1)}, u32[]{:S(2)}, u32[]{:S(2)}) async-start(bf16[64,32,256]{2,0,1:T(8,128)(2,1)} %copy.112), calls=%async_computation.2 | async-start | bytes 2097152 | tf_op jit(solution)/shard_map/all_to_all | solution.py:359
  171.9 3.0 %collective-permute-start.3 = (f32[64,17]{0,1:T(8,128)S(1)}, f32[64,17]{0,1:T(8,128)S(1)}, u32[]{:S(2)}, u32[]{:S(2)}) collective-permute-start(f32[64,17]{0,1:T(8,128)S(1)} %pad_maximum_fusion.3), channel_id=1, source_target_pairs={{0,64},{64,0},{128,192},{192,128},{1,65},{65,1},{129,193},{193,129... | collective-permute-start | bytes 13064 | tf_op jit(solution)/shard_map/ppermute | solution.py:371
  174.9 4.3 %collective-permute-start.4 = (f32[64,17]{0,1:T(8,128)S(1)}, f32[64,17]{0,1:T(8,128)S(1)}, u32[]{:S(2)}, u32[]{:S(2)}) collective-permute-start(f32[64,17]{0,1:T(8,128)S(1)} %fusion.24), channel_id=1, source_target_pairs={{0,128},{64,192},{128,0},{192,64},{1,129},{65,193},{129,1},{193,65... | collective-permute-start | bytes 13064 | tf_op jit(solution)/shard_map/ppermute | solution.py:371
  179.2 2.9 %collective-permute-start.5 = (f32[64,17]{0,1:T(8,128)S(1)}, f32[64,17]{0,1:T(8,128)S(1)}, u32[]{:S(2)}, u32[]{:S(2)}) collective-permute-start(f32[64,17]{0,1:T(8,128)S(1)} %add.49), channel_id=1, source_target_pairs={{0,2},{2,0},{4,6},{6,4},{8,10},{10,8},{12,14},{14,12},{16,18},{18,... | collective-permute-start | bytes 13064 | tf_op jit(solution)/shard_map/ppermute | solution.py:381
  182.2 6.3 %collective-permute-start.6 = (f32[128,17]{0,1:T(8,128)S(1)}, f32[128,17]{0,1:T(8,128)S(1)}, u32[]{:S(2)}, u32[]{:S(2)}) collective-permute-start(f32[128,17]{0,1:T(8,128)S(1)} %maximum_select_fusion.4), channel_id=1, source_target_pairs={{0,4},{2,6},{4,0},{6,2},{8,12},{10,14},{12,8},{14,10},{16,20},{18,... | collective-permute-start | bytes 26120 | tf_op jit(solution)/shard_map/ppermute | solution.py:381
  188.6 9.0 %collective-permute-start.7 = (f32[256,17]{0,1:T(8,128)S(1)}, f32[256,17]{0,1:T(8,128)S(1)}, u32[]{:S(2)}, u32[]{:S(2)}) collective-permute-start(f32[256,17]{0,1:T(8,128)S(1)} %maximum_select_fusion.3), channel_id=1, source_target_pairs={{0,8},{2,10},{4,12},{6,14},{8,0},{10,2},{12,4},{14,6},{16,24},{18,... | collective-permute-start | bytes 52232 | tf_op jit(solution)/shard_map/ppermute | solution.py:381
  197.6 3.0 %collective-permute-start.8 = (f32[512,17]{0,1:T(8,128)S(1)}, f32[512,17]{0,1:T(8,128)S(1)}, u32[]{:S(2)}, u32[]{:S(2)}) collective-permute-start(f32[512,17]{0,1:T(8,128)S(1)} %maximum_select_fusion.2), channel_id=1, source_target_pairs={{0,16},{2,18},{4,20},{6,22},{8,24},{10,26},{12,28},{14,30},{16,0},... | collective-permute-start | bytes 104456 | tf_op jit(solution)/shard_map/ppermute | solution.py:381
  200.6 16.0 %collective-permute-start.9 = (f32[1024,17]{0,1:T(8,128)S(1)}, f32[1024,17]{0,1:T(8,128)S(1)}, u32[]{:S(2)}, u32[]{:S(2)}) collective-permute-start(f32[1024,17]{0,1:T(8,128)S(1)} %maximum_select_fusion.1), channel_id=1, source_target_pairs={{0,32},{2,34},{4,36},{6,38},{8,40},{10,42},{12,44},{14,46},{16,48}... | collective-permute-start | bytes 208904 | tf_op jit(solution)/shard_map/ppermute | solution.py:381
  207.2 1.0 copy-start
  207.2 1.3 copy-start.2
  207.2 1.6 copy-start.4
  210.2 9.3 %copy-start.1 = (bf16[1,2048,256]{2,1,0:T(8,128)(2,1)S(1)}, bf16[1,2048,256]{2,1,0:T(8,128)(2,1)}, u32[]{:S(2)}) copy-start(bf16[1,2048,256]{2,1,0:T(8,128)(2,1)} %copy-done) | copy-start | bytes 3145732
  210.2 9.3 %copy-start.3 = (bf16[1,2048,256]{2,1,0:T(8,128)(2,1)S(1)}, bf16[1,2048,256]{2,1,0:T(8,128)(2,1)}, u32[]{:S(2)}) copy-start(bf16[1,2048,256]{2,1,0:T(8,128)(2,1)} %copy-done.2) | copy-start | bytes 3145732
  210.2 9.3 %copy-start.5 = (bf16[1,2048,256]{2,1,0:T(8,128)(2,1)S(1)}, bf16[1,2048,256]{2,1,0:T(8,128)(2,1)}, u32[]{:S(2)}) copy-start(bf16[1,2048,256]{2,1,0:T(8,128)(2,1)} %copy-done.4) | copy-start | bytes 3145732
  212.1 5.8 %collective-permute-start.2 = (bf16[3,2048,2]{1,2,0:T(2,128)(2,1)S(1)}, bf16[3,2048,2]{1,2,0:T(2,128)(2,1)S(1)}, u32[]{:S(2)}, u32[]{:S(2)}) collective-permute-start(bf16[3,2048,2]{1,2,0:T(2,128)(2,1)S(1)} %copy.114), channel_id=1, source_target_pairs={{2,0},{4,2},{6,4},{8,6},{10,8},{12,10},{14,12},{16,14},{18,16},{20... | collective-permute-start | bytes 73736 | tf_op jit(solution)/shard_map/ppermute | solution.py:18

commit v6 on v5

--- a/solution.py
+++ b/solution.py
@@ -355,10 +355,7 @@
     back_rows = back_blocks.reshape(chan_count, length)
     mode_part = mode_part[:, 0, :]
     skip_part = skip_part[:, 0, 0]
-    signal, back_signal = (
-        lax.all_to_all(conv_rows, "ctx", split_axis=1, concat_axis=0, tiled=True),
-        lax.all_to_all(back_rows, "ctx", split_axis=1, concat_axis=0, tiled=True),
-    )
+    signal = lax.all_to_all(conv_rows, "ctx", split_axis=1, concat_axis=0, tiled=True)
     grad_scale = 1.0 / math.sqrt(token_total)
     local_grads = jnp.concatenate(
         [mode_part * jnp.sqrt(2.0 * rate_rows) * grad_scale, skip_part[:, None] * grad_scale], axis=1
@@ -389,17 +386,21 @@
     else:
         spread = jnp.broadcast_to(local_grads[None], (ctx_count,) + local_grads.shape)
         gathered = lax.all_to_all(spread, "ctx", split_axis=0, concat_axis=0, tiled=True)
+    back_rows, gathered = lax.optimization_barrier((back_rows, gathered))
+    back_signal = lax.all_to_all(back_rows, "ctx", split_axis=1, concat_axis=0, tiled=True)
     gathered = gathered.reshape(chans_tp, local_grads.shape[1])
     residue_grad = gathered[:, : mode_part.shape[1]]
     skip_grad = gathered[:, mode_part.shape[1]]
     conv_wide = signal.astype(jnp.float32)
+    hyena_out = (query_feat * conv_wide).astype(jnp.bfloat16)
+    query_grad = (grad_out * conv_wide).astype(jnp.bfloat16)[None]
+    query_rim = from_behind(query_grad[:, :, :rim_width], "ctx", -1)
+    query_input = anticausal_short(query_grad, query_rim, short_filter[0:1]).astype(jnp.bfloat16)
     back_wide = back_signal.astype(jnp.float32)
-    hyena_out = (query_feat * conv_wide).astype(jnp.bfloat16)
-    feature_grad = jnp.stack(
-        [grad_out * conv_wide, back_wide * value_feat, back_wide * key_feat]
-    ).astype(jnp.bfloat16)
+    feature_grad = jnp.stack([back_wide * value_feat, back_wide * key_feat]).astype(jnp.bfloat16)
     next_rim = from_behind(feature_grad[:, :, :rim_width], "ctx", -1)
-    input_grad = anticausal_short(feature_grad, next_rim, short_filter).astype(jnp.bfloat16)
+    input_grad = anticausal_short(feature_grad, next_rim, short_filter[1:]).astype(jnp.bfloat16)
+    input_grad = jnp.concatenate([query_input, input_grad], axis=0)
     return (hyena_out[None], input_grad[None], residue_grad, skip_grad)
 
 

time: 230 us -> 237 us (1.030)
  the two profiles are of different devices: /device:TPU:1 before, /device:TPU:10 now
where the time goes in v6:
time: 237 us; the launch traced here: 236 us
  waiting for transfers between devices  74.3 us (31%)
  starting transfers between devices  64.4 us (27%)
  other arithmetic  43.7 us (18%)
  Pallas kernels  28.2 us (12%)
  local copies, waits for them, and re-layouts  24.7 us (10%)
    pallas_call x1, Pallas kernels, long_conv(): pl.pallas_call(long_conv_kernel, grid=(chan_count // step,), in_specs=[da...  28.2 us
    all_to_all x1, waiting for transfers between devices, on_device(): lax.all_to_all(product, 'ctx', split_axis=0, concat_axis=1, tiled=True)  21.1 us
    ppermute x5, waiting for transfers between devices, on_device(): theirs = lax.ppermute(gathered, 'ctx', partners)  18.2 us
    ppermute x3, starting transfers between devices, from_behind(): return lax.ppermute(shard, axis, pairs)  17.5 us
    ppermute x3, waiting for transfers between devices, from_behind(): return lax.ppermute(shard, axis, pairs)  16.1 us
    all_to_all x1, waiting for transfers between devices, on_device(): lax.all_to_all(adjoint, 'ctx', split_axis=0, concat_axis=1, tiled=True)  10.5 us
    ppermute x5, starting transfers between devices, on_device(): theirs = lax.ppermute(gathered, 'ctx', partners)  8.95 us
    all_to_all x1, starting transfers between devices, on_device(): lax.all_to_all(product, 'ctx', split_axis=0, concat_axis=1, tiled=True)  8.37 us
  transfers between devices with their start and end apart: 15, of which 11 were waited for; matrix products, arithmetic and copies ran while one was open for 18% of the time, Pallas kernels for 0%

profile of v6, /device:TPU:10, one launch (start us, length us, event | category | flops | bytes accessed | tf_op | source)
XLA Modules:
  0.0 236.5 jit_solution(6265945161433204698)
XLA Ops:
  0.7 3.2 %slice.116 = bf16[3,2048,2]{2,1,0:T(8,128)(2,1)} slice(bf16[3,2048,256]{2,1,0:T(8,128)(2,1)} %bitcast.85), slice={[0:3], [0:2048], [254:256]} | slice | bytes 49152 | tf_op jit(solution)/shard_map/slice | solution.py:323
  5.6 1.9 collective-permute-start
  9.4 7.2 %collective-permute-start.1 = (bf16[2048,128]{1,0:T(8,128)(2,1)}, bf16[2048,128]{1,0:T(8,128)(2,1)}, u32[]{:S(2)}, u32[]{:S(2)}) collective-permute-start(bf16[2048,128]{1,0:T(8,128)(2,1)} %dynamic-slice_bitcast_fusion), channel_id=1, source_target_pairs={{0,1},{1,0},{2,3},{3,2},{4,5},{5,4},{6,7},{7,6},{8,9},{9,8},{10,11... | collective-permute-start | bytes 1572872 | tf_op jit(solution)/shard_map/ppermute | solution.py:315
  18.3 3.3 %maximum_convert_fusion = f32[3,2048,258]{2,1,0:T(8,128)S(1)} fusion(bf16[3,2048,256]{2,1,0:T(8,128)(2,1)S(1)} %bitcast.86, bf16[3,2048,2]{2,1,0:T(8,128)(2,1)} %copy.101), kind=kLoop, calls=%fused_computation.6 | loop fusion | flops 6340608 | bytes 9510912 | tf_op jit(solution)/shard_map/convert_element_type | solution.py:24
  21.6 6.4 %fusion.1 = bf16[3,2048,256]{2,1,0:T(8,128)(2,1)S(1)} fusion(f32[3,2048,258]{2,1,0:T(8,128)S(1)} %maximum_convert_fusion, f32[3,2048]{1,0:T(4,128)S(1)} %get-tuple-element.47, f32[3,2048]{1,0:T(4,128)S(1)} %get-tuple-element.48, f32[3,2048]{1,0:T(4,128)S(1)} %bitcast.95), kind=kLoop, calls=%fused_computation.2 | loop fusion | flops 9437184 | bytes 22093824 | tf_op jit(solution)/shard_map/convert_element_type | solution.py:325
  29.5 8.4 %all-to-all-start = ((bf16[32,64,256]{2,1,0:T(8,128)(2,1)}), bf16[32,64,256]{2,1,0:T(8,128)(2,1)}, u32[]{:S(2)}, u32[]{:S(2)}) async-start(bf16[32,64,256]{2,1,0:T(8,128)(2,1)} %bitcast.88), calls=%async_computation | async-start | bytes 2097152 | tf_op jit(solution)/shard_map/all_to_all | solution.py:336
  42.8 21.1 %all-to-all-done = bf16[32,64,256]{2,1,0:T(8,128)(2,1)} async-done(((bf16[32,64,256]{2,1,0:T(8,128)(2,1)}), bf16[32,64,256]{2,1,0:T(8,128)(2,1)}, u32[]{:S(2)}, u32[]{:S(2)}) %all-to-all-start) | async-done | bytes 1048608 | tf_op jit(solution)/shard_map/all_to_all | solution.py:336
  64.0 7.3 %all-to-all-start.1 = ((bf16[32,64,256]{2,1,0:T(8,128)(2,1)}), bf16[32,64,256]{2,1,0:T(8,128)(2,1)S(1)}, u32[]{:S(2)}, u32[]{:S(2)}) async-start(bf16[32,64,256]{2,1,0:T(8,128)(2,1)} %multiply_convert_fusion.1), calls=%async_computation.1 | async-start | bytes 2097152 | tf_op jit(solution)/shard_map/all_to_all | solution.py:337
  83.4 2.8 %copy.142 = bf16[32,64,256]{2,0,1:T(8,128)(2,1)} copy(bf16[32,64,256]{2,1,0:T(8,128)(2,1)} %all-to-all-done) | data formatting | bytes 2097152 | tf_op jit(solution)/shard_map/all_to_all | solution.py:336
  86.2 10.5 %all-to-all-done.1 = bf16[32,64,256]{2,1,0:T(8,128)(2,1)S(1)} async-done(((bf16[32,64,256]{2,1,0:T(8,128)(2,1)}), bf16[32,64,256]{2,1,0:T(8,128)(2,1)S(1)}, u32[]{:S(2)}, u32[]{:S(2)}) %all-to-all-start.1) | async-done | bytes 1048608 | tf_op jit(solution)/shard_map/all_to_all | solution.py:337
  98.3 28.2 %shard_map.93 = (bf16[64,32,256]{2,1,0:T(8,128)(2,1)}, bf16[64,32,256]{2,1,0:T(8,128)(2,1)}, f32[64,1,16]{2,1,0:T(1,128)}, f32[64,1,128]{2,1,0:T(1,128)}) custom-call(bf16[64,32,256]{2,1,0:T(8,128)(2,1)} %bitcast.92, bf16[64,32,256]{2,1,0:T(8,128)(2,1)} %bitcast.93, f32[64,2,256]{2,1,0:T(2,128)} %pad_maximum_fusion.2.krow_ref, ...), custom_call_target="tpu_custom_call" | custom-call | flops 4563402752 | bytes 8388608 | tf_op jit(solution)/shard_map/pallas_call | solution.py:262
  126.5 2.9 %copy.114 = bf16[64,32,256]{2,0,1:T(8,128)(2,1)} copy(bf16[64,32,256]{2,1,0:T(8,128)(2,1)} %get-tuple-element.10) | data formatting | bytes 2097152 | tf_op jit(solution)/shard_map/pallas_call | solution.py:262
  129.3 6.4 %all-to-all-start.2 = ((bf16[64,32,256]{2,0,1:T(8,128)(2,1)}), bf16[64,32,256]{2,0,1:T(8,128)(2,1)S(1)}, u32[]{:S(2)}, u32[]{:S(2)}) async-start(bf16[64,32,256]{2,0,1:T(8,128)(2,1)} %copy.114), calls=%async_computation.2 | async-start | bytes 2097152 | tf_op jit(solution)/shard_map/all_to_all | solution.py:358
  136.9 3.2 %collective-permute-done.3 = f32[64,17]{0,1:T(8,128)S(1)} collective-permute-done((f32[64,17]{0,1:T(8,128)S(1)}, f32[64,17]{0,1:T(8,128)S(1)}, u32[]{:S(2)}, u32[]{:S(2)}) %collective-permute-start.3) | collective-permute-done | bytes 4384 | tf_op jit(solution)/shard_map/ppermute | solution.py:368
  140.2 2.3 collective-permute-start.4
  142.5 2.9 %collective-permute-done.4 = f32[64,17]{0,1:T(8,128)S(1)} collective-permute-done((f32[64,17]{0,1:T(8,128)S(1)}, f32[64,17]{0,1:T(8,128)S(1)}, u32[]{:S(2)}, u32[]{:S(2)}) %collective-permute-start.4) | collective-permute-done | bytes 4384 | tf_op jit(solution)/shard_map/ppermute | solution.py:368
  148.2 5.3 %collective-permute-done.6 = f32[128,17]{0,1:T(8,128)S(1)} collective-permute-done((f32[128,17]{0,1:T(8,128)S(1)}, f32[128,17]{0,1:T(8,128)S(1)}, u32[]{:S(2)}, u32[]{:S(2)}) %collective-permute-start.6) | collective-permute-done | bytes 8736 | tf_op jit(solution)/shard_map/ppermute | solution.py:378
  153.5 4.4 %collective-permute-start.7 = (f32[256,17]{0,1:T(8,128)S(1)}, f32[256,17]{0,1:T(8,128)S(1)}, u32[]{:S(2)}, u32[]{:S(2)}) collective-permute-start(f32[256,17]{0,1:T(8,128)S(1)} %maximum_select_fusion.3), channel_id=1, source_target_pairs={{0,8},{2,10},{4,12},{6,14},{8,0},{10,2},{12,4},{14,6},{16,24},{18,... | collective-permute-start | bytes 52232 | tf_op jit(solution)/shard_map/ppermute | solution.py:378
  157.9 4.9 %collective-permute-done.7 = f32[256,17]{0,1:T(8,128)S(1)} collective-permute-done((f32[256,17]{0,1:T(8,128)S(1)}, f32[256,17]{0,1:T(8,128)S(1)}, u32[]{:S(2)}, u32[]{:S(2)}) %collective-permute-start.7) | collective-permute-done | bytes 17440 | tf_op jit(solution)/shard_map/ppermute | solution.py:378
  163.3 3.6 %collective-permute-done.8 = f32[512,17]{0,1:T(8,128)S(1)} collective-permute-done((f32[512,17]{0,1:T(8,128)S(1)}, f32[512,17]{0,1:T(8,128)S(1)}, u32[]{:S(2)}, u32[]{:S(2)}) %collective-permute-start.8) | collective-permute-done | bytes 34848 | tf_op jit(solution)/shard_map/ppermute | solution.py:378
  166.9 2.5 %collective-permute-start.9 = (f32[1024,17]{0,1:T(8,128)S(1)}, f32[1024,17]{0,1:T(8,128)S(1)}, u32[]{:S(2)}, u32[]{:S(2)}) collective-permute-start(f32[1024,17]{0,1:T(8,128)S(1)} %maximum_select_fusion.1), channel_id=1, source_target_pairs={{0,32},{2,34},{4,36},{6,38},{8,40},{10,42},{12,44},{14,46},{16,48}... | collective-permute-start | bytes 208904 | tf_op jit(solution)/shard_map/ppermute | solution.py:378
  170.1 3.2 %collective-permute-done.9 = f32[1024,17]{0,1:T(8,128)S(1)} collective-permute-done((f32[1024,17]{0,1:T(8,128)S(1)}, f32[1024,17]{0,1:T(8,128)S(1)}, u32[]{:S(2)}, u32[]{:S(2)}) %collective-permute-start.9) | collective-permute-done | bytes 69664 | tf_op jit(solution)/shard_map/ppermute | solution.py:378
  174.5 5.9 %all-to-all-start.3 = ((bf16[64,32,256]{2,0,1:T(8,128)(2,1)}), bf16[64,32,256]{2,0,1:T(8,128)(2,1)}, u32[]{:S(2)}, u32[]{:S(2)}) async-start(bf16[64,32,256]{2,0,1:T(8,128)(2,1)} %bitcast.75), calls=%async_computation.3 | async-start | bytes 2097152 | tf_op jit(solution)/shard_map/all_to_all | solution.py:390
  182.1 4.9 %collective-permute-start.2 = (bf16[1,2048,2]{2,1,0:T(8,128)(2,1)S(1)}, bf16[1,2048,2]{2,1,0:T(8,128)(2,1)S(1)}, u32[]{:S(2)}, u32[]{:S(2)}) collective-permute-start(bf16[1,2048,2]{2,1,0:T(8,128)(2,1)S(1)} %fusion.17), channel_id=1, source_target_pairs={{2,0},{4,2},{6,4},{8,6},{10,8},{12,10},{14,12},{16,14},{18,16},{20... | collective-permute-start | bytes 24584 | tf_op jit(solution)/shard_map/ppermute | solution.py:18
  187.4 16.1 %collective-permute-done.2 = bf16[1,2048,2]{2,1,0:T(8,128)(2,1)S(1)} collective-permute-done((bf16[1,2048,2]{2,1,0:T(8,128)(2,1)S(1)}, bf16[1,2048,2]{2,1,0:T(8,128)(2,1)S(1)}, u32[]{:S(2)}, u32[]{:S(2)}) %collective-permute-start.2) | collective-permute-done | bytes 8224 | tf_op jit(solution)/shard_map/ppermute | solution.py:18
  203.7 2.2 all-to-all-done.3
  205.9 4.2 %fusion.8 = (bf16[1,2048,256]{2,1,0:T(8,128)(2,1)S(1)}, bf16[1,2048,256]{2,1,0:T(8,128)(2,1)S(1)}, bf16[1,2048,256]{2,1,0:T(8,128)(2,1)}) fusion(bf16[64,32,256]{2,0,1:T(8,128)(2,1)} %all-to-all-done.3, bf16[3,2048,256]{2,1,0:T(8,128)(2,1)} %copy-done, bf16[64,32,256]{2,0,1:T(8,128)(2,1)} %copy-done.1), kind=kLoop, calls=%fused_computation.20 | loop fusion | flops 5767168 | bytes 8388608 | tf_op jit(solution)/shard_map/convert.7
  214.0 10.6 %collective-permute-start.10 = (bf16[2,2048,2]{1,2,0:T(2,128)(2,1)S(1)}, bf16[2,2048,2]{1,2,0:T(2,128)(2,1)S(1)}, u32[]{:S(2)}, u32[]{:S(2)}) collective-permute-start(bf16[2,2048,2]{1,2,0:T(2,128)(2,1)S(1)} %copy.118), channel_id=1, source_target_pairs={{2,0},{4,2},{6,4},{8,6},{10,8},{12,10},{14,12},{16,14},{18,16},{20... | collective-permute-start | bytes 49160 | tf_op jit(solution)/shard_map/ppermute | solution.py:18
  224.7 3.0 %fusion.10 = bf16[1,2048,256]{2,1,0:T(8,128)(2,1)} fusion(f32[1,2048,258]{2,1,0:T(8,128)S(1)} %maximum_convert_fusion.2, f32[2048]{0:T(1024)S(1)} %bitcast.105, f32[2048]{0:T(1024)S(1)} %bitcast.106, f32[2048]{0:T(1024)S(1)} %bitcast.104), kind=kLoop, calls=%fused_computation.23 | loop fusion | flops 3145728 | bytes 7364608 | tf_op jit(solution)/shard_map/convert_element_type | solution.py:398
  228.2 2.0 maximum_convert_fusion.1
  230.2 4.3 %fusion.4 = bf16[2,2048,256]{2,1,0:T(8,128)(2,1)S(1)} fusion(f32[2,2048,258]{2,1,0:T(8,128)S(1)} %maximum_convert_fusion.1, f32[2,2048]{1,0:T(2,128)S(1)} %get-tuple-element.49, f32[2,2048]{1,0:T(2,128)S(1)} %get-tuple-element.50, f32[2,2048]{1,0:T(2,128)S(1)} %bitcast.102), kind=kLoop, calls=%fused_computation.9 | loop fusion | flops 6291456 | bytes 14729216 | tf_op jit(solution)/shard_map/convert_element_type | solution.py:402
  234.5 1.9 maximum_bitcast_fusion
  (95 shorter events, 38.3 us)
Async XLA Ops:
  0.6 15.9 %copy-start.8 = (f32[3,3,2048]{2,1,0:T(4,128)S(1)}, f32[3,3,2048]{2,1,0:T(4,128)}, u32[]{:S(2)}) copy-start(f32[3,3,2048]{2,1,0:T(4,128)} %param.8) | copy-start | bytes 221188
  0.6 17.7 %copy-start.4 = (bf16[1,3,2048,256]{3,2,1,0:T(8,128)(2,1)S(1)}, bf16[1,3,2048,256]{3,2,1,0:T(8,128)(2,1)}, u32[]{:S(2)}) copy-start(bf16[1,3,2048,256]{3,2,1,0:T(8,128)(2,1)} %param.6) | copy-start | bytes 9437188
  5.6 11.1 %collective-permute-start = (bf16[3,2048,2]{1,2,0:T(2,128)(2,1)S(1)}, bf16[3,2048,2]{1,2,0:T(2,128)(2,1)S(1)}, u32[]{:S(2)}, u32[]{:S(2)}) collective-permute-start(bf16[3,2048,2]{1,2,0:T(2,128)(2,1)S(1)} %copy.100), channel_id=1, source_target_pairs={{0,2},{2,4},{4,6},{6,8},{8,10},{10,12},{12,14},{14,16},{16,18},{18... | collective-permute-start | bytes 73736 | tf_op jit(solution)/shard_map/ppermute | solution.py:18
  9.4 30.7 %collective-permute-start.1 = (bf16[2048,128]{1,0:T(8,128)(2,1)}, bf16[2048,128]{1,0:T(8,128)(2,1)}, u32[]{:S(2)}, u32[]{:S(2)}) collective-permute-start(bf16[2048,128]{1,0:T(8,128)(2,1)} %dynamic-slice_bitcast_fusion), channel_id=1, source_target_pairs={{0,1},{1,0},{2,3},{3,2},{4,5},{5,4},{6,7},{7,6},{8,9},{9,8},{10,11... | collective-permute-start | bytes 1572872 | tf_op jit(solution)/shard_map/ppermute | solution.py:315
  28.0 12.1 %copy-start = (bf16[3,2048,256]{2,1,0:T(8,128)(2,1)}, bf16[3,2048,256]{2,1,0:T(8,128)(2,1)S(1)}, u32[]{:S(2)}) copy-start(bf16[3,2048,256]{2,1,0:T(8,128)(2,1)S(1)} %fusion.1) | copy-start | bytes 9437188
  29.5 34.5 %all-to-all-start = ((bf16[32,64,256]{2,1,0:T(8,128)(2,1)}), bf16[32,64,256]{2,1,0:T(8,128)(2,1)}, u32[]{:S(2)}, u32[]{:S(2)}) async-start(bf16[32,64,256]{2,1,0:T(8,128)(2,1)} %bitcast.88), calls=%async_computation | async-start | bytes 2097152 | tf_op jit(solution)/shard_map/all_to_all | solution.py:336
  38.8 1.3 copy-start.7
  41.4 31.1 %copy-start.9 = (f32[64,16]{1,0:T(8,128)S(1)}, f32[64,16]{1,0:T(8,128)}, u32[]{:S(2)}) copy-start(f32[64,16]{1,0:T(8,128)} %get-tuple-element.44) | copy-start | bytes 12292
  41.4 31.1 %copy-start.10 = (f32[64,16]{1,0:T(8,128)S(1)}, f32[64,16]{1,0:T(8,128)}, u32[]{:S(2)}) copy-start(f32[64,16]{1,0:T(8,128)} %get-tuple-element.45) | copy-start | bytes 12292
  64.0 32.8 %all-to-all-start.1 = ((bf16[32,64,256]{2,1,0:T(8,128)(2,1)}), bf16[32,64,256]{2,1,0:T(8,128)(2,1)S(1)}, u32[]{:S(2)}, u32[]{:S(2)}) async-start(bf16[32,64,256]{2,1,0:T(8,128)(2,1)} %multiply_convert_fusion.1), calls=%async_computation.1 | async-start | bytes 2097152 | tf_op jit(solution)/shard_map/all_to_all | solution.py:337
  126.4 9.3 %copy-start.11 = (f32[64,1,16]{2,1,0:T(1,128)S(1)}, f32[64,1,16]{2,1,0:T(1,128)}, u32[]{:S(2)}) copy-start(f32[64,1,16]{2,1,0:T(1,128)} %get-tuple-element.12) | copy-start | bytes 12292
  126.5 9.4 %copy-start.12 = (f32[64,1,128]{2,1,0:T(1,128)S(1)}, f32[64,1,128]{2,1,0:T(1,128)}, u32[]{:S(2)}) copy-start(f32[64,1,128]{2,1,0:T(1,128)} %get-tuple-element.13) | copy-start | bytes 98308
  126.5 43.0 %copy-start.6 = (bf16[64,32,256]{2,1,0:T(8,128)(2,1)S(1)}, bf16[64,32,256]{2,1,0:T(8,128)(2,1)}, u32[]{:S(2)}) copy-start(bf16[64,32,256]{2,1,0:T(8,128)(2,1)} %get-tuple-element.11) | copy-start | bytes 3145732
  129.3 45.1 %all-to-all-start.2 = ((bf16[64,32,256]{2,0,1:T(8,128)(2,1)}), bf16[64,32,256]{2,0,1:T(8,128)(2,1)S(1)}, u32[]{:S(2)}, u32[]{:S(2)}) async-start(bf16[64,32,256]{2,0,1:T(8,128)(2,1)} %copy.114), calls=%async_computation.2 | async-start | bytes 2097152 | tf_op jit(solution)/shard_map/all_to_all | solution.py:358
  136.4 3.8 %collective-permute-start.3 = (f32[64,17]{0,1:T(8,128)S(1)}, f32[64,17]{0,1:T(8,128)S(1)}, u32[]{:S(2)}, u32[]{:S(2)}) collective-permute-start(f32[64,17]{0,1:T(8,128)S(1)} %pad_maximum_fusion.3), channel_id=1, source_target_pairs={{0,64},{64,0},{128,192},{192,128},{1,65},{65,1},{129,193},{193,129... | collective-permute-start | bytes 13064 | tf_op jit(solution)/shard_map/ppermute | solution.py:368
  140.2 5.2 %collective-permute-start.4 = (f32[64,17]{0,1:T(8,128)S(1)}, f32[64,17]{0,1:T(8,128)S(1)}, u32[]{:S(2)}, u32[]{:S(2)}) collective-permute-start(f32[64,17]{0,1:T(8,128)S(1)} %fusion.26), channel_id=1, source_target_pairs={{0,128},{64,192},{128,0},{192,64},{1,129},{65,193},{129,1},{193,65... | collective-permute-start | bytes 13064 | tf_op jit(solution)/shard_map/ppermute | solution.py:368
  145.4 1.2 collective-permute-start.5
  146.6 6.8 %collective-permute-start.6 = (f32[128,17]{0,1:T(8,128)S(1)}, f32[128,17]{0,1:T(8,128)S(1)}, u32[]{:S(2)}, u32[]{:S(2)}) collective-permute-start(f32[128,17]{0,1:T(8,128)S(1)} %maximum_select_fusion.4), channel_id=1, source_target_pairs={{0,4},{2,6},{4,0},{6,2},{8,12},{10,14},{12,8},{14,10},{16,20},{18,... | collective-permute-start | bytes 26120 | tf_op jit(solution)/shard_map/ppermute | solution.py:378
  153.5 9.2 %collective-permute-start.7 = (f32[256,17]{0,1:T(8,128)S(1)}, f32[256,17]{0,1:T(8,128)S(1)}, u32[]{:S(2)}, u32[]{:S(2)}) collective-permute-start(f32[256,17]{0,1:T(8,128)S(1)} %maximum_select_fusion.3), channel_id=1, source_target_pairs={{0,8},{2,10},{4,12},{6,14},{8,0},{10,2},{12,4},{14,6},{16,24},{18,... | collective-permute-start | bytes 52232 | tf_op jit(solution)/shard_map/ppermute | solution.py:378
  162.7 4.2 %collective-permute-start.8 = (f32[512,17]{0,1:T(8,128)S(1)}, f32[512,17]{0,1:T(8,128)S(1)}, u32[]{:S(2)}, u32[]{:S(2)}) collective-permute-start(f32[512,17]{0,1:T(8,128)S(1)} %maximum_select_fusion.2), channel_id=1, source_target_pairs={{0,16},{2,18},{4,20},{6,22},{8,24},{10,26},{12,28},{14,30},{16,0},... | collective-permute-start | bytes 104456 | tf_op jit(solution)/shard_map/ppermute | solution.py:378
  166.9 6.4 %collective-permute-start.9 = (f32[1024,17]{0,1:T(8,128)S(1)}, f32[1024,17]{0,1:T(8,128)S(1)}, u32[]{:S(2)}, u32[]{:S(2)}) collective-permute-start(f32[1024,17]{0,1:T(8,128)S(1)} %maximum_select_fusion.1), channel_id=1, source_target_pairs={{0,32},{2,34},{4,36},{6,38},{8,40},{10,42},{12,44},{14,46},{16,48}... | collective-permute-start | bytes 208904 | tf_op jit(solution)/shard_map/ppermute | solution.py:378
  174.5 12.6 %copy-start.1 = (bf16[64,32,256]{2,0,1:T(8,128)(2,1)}, bf16[64,32,256]{2,0,1:T(8,128)(2,1)S(1)}, u32[]{:S(2)}) copy-start(bf16[64,32,256]{2,0,1:T(8,128)(2,1)S(1)} %all-to-all-done.2) | copy-start | bytes 3145732
  174.5 31.4 %all-to-all-start.3 = ((bf16[64,32,256]{2,0,1:T(8,128)(2,1)}), bf16[64,32,256]{2,0,1:T(8,128)(2,1)}, u32[]{:S(2)}, u32[]{:S(2)}) async-start(bf16[64,32,256]{2,0,1:T(8,128)(2,1)} %bitcast.75), calls=%async_computation.3 | async-start | bytes 2097152 | tf_op jit(solution)/shard_map/all_to_all | solution.py:390
  182.1 21.4 %collective-permute-start.2 = (bf16[1,2048,2]{2,1,0:T(8,128)(2,1)S(1)}, bf16[1,2048,2]{2,1,0:T(8,128)(2,1)S(1)}, u32[]{:S(2)}, u32[]{:S(2)}) collective-permute-start(bf16[1,2048,2]{2,1,0:T(8,128)(2,1)S(1)} %fusion.17), channel_id=1, source_target_pairs={{2,0},{4,2},{6,4},{8,6},{10,8},{12,10},{14,12},{16,14},{18,16},{20... | collective-permute-start | bytes 24584 | tf_op jit(solution)/shard_map/ppermute | solution.py:18
  210.1 1.0 copy-start.2
  210.1 1.3 copy-start.3
  214.0 13.6 %collective-permute-start.10 = (bf16[2,2048,2]{1,2,0:T(2,128)(2,1)S(1)}, bf16[2,2048,2]{1,2,0:T(2,128)(2,1)S(1)}, u32[]{:S(2)}, u32[]{:S(2)}) collective-permute-start(bf16[2,2048,2]{1,2,0:T(2,128)(2,1)S(1)} %copy.118), channel_id=1, source_target_pairs={{2,0},{4,2},{6,4},{8,6},{10,8},{12,10},{14,12},{16,14},{18,16},{20... | collective-permute-start | bytes 49160 | tf_op jit(solution)/shard_map/ppermute | solution.py:18
  230.2 4.3 %copy-start.5 = (bf16[1,2048,256]{2,1,0:T(8,128)(2,1)S(1)}, bf16[1,2048,256]{2,1,0:T(8,128)(2,1)}, u32[]{:S(2)}) copy-start(bf16[1,2048,256]{2,1,0:T(8,128)(2,1)} %fusion.10) | copy-start | bytes 3145732

commit v7 on v5

--- a/solution.py
+++ b/solution.py
@@ -355,10 +355,7 @@
     back_rows = back_blocks.reshape(chan_count, length)
     mode_part = mode_part[:, 0, :]
     skip_part = skip_part[:, 0, 0]
-    signal, back_signal = (
-        lax.all_to_all(conv_rows, "ctx", split_axis=1, concat_axis=0, tiled=True),
-        lax.all_to_all(back_rows, "ctx", split_axis=1, concat_axis=0, tiled=True),
-    )
+    signal = lax.all_to_all(conv_rows, "ctx", split_axis=1, concat_axis=0, tiled=True)
     grad_scale = 1.0 / math.sqrt(token_total)
     local_grads = jnp.concatenate(
         [mode_part * jnp.sqrt(2.0 * rate_rows) * grad_scale, skip_part[:, None] * grad_scale], axis=1
@@ -372,6 +369,8 @@
             hop *= 2
     else:
         local_grads = lax.psum(local_grads, "dp")
+    back_rows, local_grads = lax.optimization_barrier((back_rows, local_grads))
+    back_signal = lax.all_to_all(back_rows, "ctx", split_axis=1, concat_axis=0, tiled=True)
     if ctx_count & (ctx_count - 1) == 0:
         ctx_index = lax.axis_index("ctx")
         gathered = local_grads

time: 230 us -> 230 us (level)
    all_to_all x1, waiting for transfers between devices: 25.3 us -> 0.01 us  [on_device(): lax.all_to_all(back_rows, 'ctx', split_axis=1, concat_axis=0, tiled=True)]
    all_to_all x1, waiting for transfers between devices: 0.01 us -> 18.4 us  [on_device(): lax.all_to_all(conv_rows, 'ctx', split_axis=1, concat_axis=0, tiled=True)]
    ppermute x5, waiting for transfers between devices: 12.3 us -> 21.9 us  [on_device(): theirs = lax.ppermute(gathered, 'ctx', partners)]
    pallas_call x2 -> x1, local copies, waits for them, and re-layouts: 5.57 us -> 2.79 us  [long_conv(): pl.pallas_call(long_conv_kernel, grid=(chan_count // step,), in_specs=[da...]
    unnamed x29 -> x30, local copies, waits for them, and re-layouts: 2.76 us -> 4.61 us
  transfers between devices with their start and end apart: 14 -> 14, of which waited for: 10 -> 9; matrix products, arithmetic and copies ran while one was open for 20% -> 21% of each run, Pallas kernels for 0% -> 0%
where the time goes in v7:
time: 230 us; the launch traced here: 229 us
  waiting for transfers between devices  76.7 us (33%)
  starting transfers between devices  52 us (23%)
  other arithmetic  41.2 us (18%)
  local copies, waits for them, and re-layouts  30.4 us (13%)
  Pallas kernels  28.2 us (12%)
    pallas_call x1, Pallas kernels, long_conv(): pl.pallas_call(long_conv_kernel, grid=(chan_count // step,), in_specs=[da...  28.2 us
    all_to_all x1, waiting for transfers between devices, on_device(): lax.all_to_all(product, 'ctx', split_axis=0, concat_axis=1, tiled=True)  22 us
    ppermute x5, waiting for transfers between devices, on_device(): theirs = lax.ppermute(gathered, 'ctx', partners)  21.9 us
    all_to_all x1, waiting for transfers between devices, on_device(): lax.all_to_all(conv_rows, 'ctx', split_axis=1, concat_axis=0, tiled=True)  18.4 us
    all_to_all x1, waiting for transfers between devices, on_device(): lax.all_to_all(adjoint, 'ctx', split_axis=0, concat_axis=1, tiled=True)  12.2 us
    ppermute x5, starting transfers between devices, on_device(): theirs = lax.ppermute(gathered, 'ctx', partners)  10.3 us
    ppermute x2, starting transfers between devices, from_behind(): return lax.ppermute(shard, axis, pairs)  9.44 us
    unnamed x7, other arithmetic  7.86 us
  transfers between devices with their start and end apart: 14, of which 9 were waited for; matrix products, arithmetic and copies ran while one was open for 21% of the time, Pallas kernels for 0%

profile of v7, /device:TPU:1, one launch (start us, length us, event | category | flops | bytes accessed | tf_op | source)
XLA Modules:
  0.0 229.4 jit_solution(15678697894474020068)
XLA Ops:
  0.7 3.2 %slice.71 = bf16[3,2048,2]{2,1,0:T(8,128)(2,1)} slice(bf16[3,2048,256]{2,1,0:T(8,128)(2,1)} %bitcast.70), slice={[0:3], [0:2048], [254:256]} | slice | bytes 49152 | tf_op jit(solution)/shard_map/slice | solution.py:323
  3.9 1.7 copy.99
  5.6 4.9 %collective-permute-start = (bf16[3,2048,2]{1,2,0:T(2,128)(2,1)S(1)}, bf16[3,2048,2]{1,2,0:T(2,128)(2,1)S(1)}, u32[]{:S(2)}, u32[]{:S(2)}) collective-permute-start(bf16[3,2048,2]{1,2,0:T(2,128)(2,1)S(1)} %copy.99), channel_id=1, source_target_pairs={{0,2},{2,4},{4,6},{6,8},{8,10},{10,12},{12,14},{14,16},{16,18},{18... | collective-permute-start | bytes 73736 | tf_op jit(solution)/shard_map/ppermute | solution.py:18
  10.5 1.9 dynamic-slice_bitcast_fusion
  12.4 6.0 %collective-permute-start.1 = (bf16[2048,128]{1,0:T(8,128)(2,1)}, bf16[2048,128]{1,0:T(8,128)(2,1)}, u32[]{:S(2)}, u32[]{:S(2)}) collective-permute-start(bf16[2048,128]{1,0:T(8,128)(2,1)} %dynamic-slice_bitcast_fusion), channel_id=1, source_target_pairs={{0,1},{1,0},{2,3},{3,2},{4,5},{5,4},{6,7},{7,6},{8,9},{9,8},{10,11... | collective-permute-start | bytes 1572872 | tf_op jit(solution)/shard_map/ppermute | solution.py:315
  20.2 3.3 %maximum_convert_fusion = f32[3,2048,258]{2,1,0:T(8,128)S(1)} fusion(bf16[3,2048,256]{2,1,0:T(8,128)(2,1)S(1)} %bitcast.71, bf16[3,2048,2]{2,1,0:T(8,128)(2,1)} %copy.100), kind=kLoop, calls=%fused_computation.12 | loop fusion | flops 6340608 | bytes 9510912 | tf_op jit(solution)/shard_map/convert_element_type | solution.py:24
  23.5 6.4 %fusion.4 = bf16[3,2048,256]{2,1,0:T(8,128)(2,1)S(1)} fusion(f32[3,2048,258]{2,1,0:T(8,128)S(1)} %maximum_convert_fusion, f32[3,2048]{1,0:T(4,128)S(1)} %get-tuple-element.42, f32[3,2048]{1,0:T(4,128)S(1)} %get-tuple-element.43, f32[3,2048]{1,0:T(4,128)S(1)} %bitcast.83), kind=kLoop, calls=%fused_computation.8 | loop fusion | flops 9437184 | bytes 22093824 | tf_op jit(solution)/shard_map/convert_element_type | solution.py:325
  31.1 7.5 %all-to-all-start = ((bf16[32,64,256]{2,1,0:T(8,128)(2,1)}), bf16[32,64,256]{2,1,0:T(8,128)(2,1)}, u32[]{:S(2)}, u32[]{:S(2)}) async-start(bf16[32,64,256]{2,1,0:T(8,128)(2,1)} %bitcast.76), calls=%async_computation | async-start | bytes 2097152 | tf_op jit(solution)/shard_map/all_to_all | solution.py:336
  45.0 22.0 %all-to-all-done = bf16[32,64,256]{2,1,0:T(8,128)(2,1)} async-done(((bf16[32,64,256]{2,1,0:T(8,128)(2,1)}), bf16[32,64,256]{2,1,0:T(8,128)(2,1)}, u32[]{:S(2)}, u32[]{:S(2)}) %all-to-all-start) | async-done | bytes 1048608 | tf_op jit(solution)/shard_map/all_to_all | solution.py:336
  67.0 5.3 %all-to-all-start.1 = ((bf16[32,64,256]{2,1,0:T(8,128)(2,1)}), bf16[32,64,256]{2,1,0:T(8,128)(2,1)}, u32[]{:S(2)}, u32[]{:S(2)}) async-start(bf16[32,64,256]{2,1,0:T(8,128)(2,1)} %multiply_convert_fusion), calls=%async_computation.1 | async-start | bytes 2097152 | tf_op jit(solution)/shard_map/all_to_all | solution.py:337
  73.5 1.9 stack.62.row_ref
  85.3 2.8 %copy.135 = bf16[32,64,256]{2,0,1:T(8,128)(2,1)} copy(bf16[32,64,256]{2,1,0:T(8,128)(2,1)} %all-to-all-done) | data formatting | bytes 2097152 | tf_op jit(solution)/shard_map/all_to_all | solution.py:336
  88.0 12.2 %all-to-all-done.1 = bf16[32,64,256]{2,1,0:T(8,128)(2,1)} async-done(((bf16[32,64,256]{2,1,0:T(8,128)(2,1)}), bf16[32,64,256]{2,1,0:T(8,128)(2,1)}, u32[]{:S(2)}, u32[]{:S(2)}) %all-to-all-start.1) | async-done | bytes 1048608 | tf_op jit(solution)/shard_map/all_to_all | solution.py:337
  100.2 2.8 %copy.134 = bf16[32,64,256]{2,0,1:T(8,128)(2,1)} copy(bf16[32,64,256]{2,1,0:T(8,128)(2,1)} %all-to-all-done.1) | data formatting | bytes 2097152 | tf_op jit(solution)/shard_map/all_to_all | solution.py:337
  103.0 28.2 %shard_map.93 = (bf16[64,32,256]{2,1,0:T(8,128)(2,1)}, bf16[64,32,256]{2,1,0:T(8,128)(2,1)}, f32[64,1,16]{2,1,0:T(1,128)}, f32[64,1,128]{2,1,0:T(1,128)}) custom-call(bf16[64,32,256]{2,1,0:T(8,128)(2,1)} %bitcast.80, bf16[64,32,256]{2,1,0:T(8,128)(2,1)} %bitcast.81, f32[64,2,256]{2,1,0:T(2,128)} %pad_maximum_fusion.2.krow_ref, ...), custom_call_target="tpu_custom_call" | custom-call | flops 4563402752 | bytes 8388608 | tf_op jit(solution)/shard_map/pallas_call | solution.py:262
  131.2 2.8 %copy.113 = bf16[64,32,256]{2,0,1:T(8,128)(2,1)} copy(bf16[64,32,256]{2,1,0:T(8,128)(2,1)} %get-tuple-element.10) | data formatting | bytes 2097152 | tf_op jit(solution)/shard_map/pallas_call | solution.py:262
  134.0 4.6 %all-to-all-start.2 = ((bf16[64,32,256]{2,0,1:T(8,128)(2,1)}), bf16[64,32,256]{2,0,1:T(8,128)(2,1)}, u32[]{:S(2)}, u32[]{:S(2)}) async-start(bf16[64,32,256]{2,0,1:T(8,128)(2,1)} %copy.113), calls=%async_computation.2 | async-start | bytes 2097152 | tf_op jit(solution)/shard_map/all_to_all | solution.py:358
  140.7 1.6 collective-permute-done.2
  142.3 2.9 %collective-permute-start.3 = (f32[64,17]{0,1:T(8,128)S(1)}, f32[64,17]{0,1:T(8,128)S(1)}, u32[]{:S(2)}, u32[]{:S(2)}) collective-permute-start(f32[64,17]{0,1:T(8,128)S(1)} %fusion.24), channel_id=1, source_target_pairs={{0,128},{64,192},{128,0},{192,64},{1,129},{65,193},{129,1},{193,65... | collective-permute-start | bytes 13064 | tf_op jit(solution)/shard_map/ppermute | solution.py:368
  145.2 1.9 copy.126
  148.2 18.4 %all-to-all-done.2 = bf16[64,32,256]{2,0,1:T(8,128)(2,1)} async-done(((bf16[64,32,256]{2,0,1:T(8,128)(2,1)}), bf16[64,32,256]{2,0,1:T(8,128)(2,1)}, u32[]{:S(2)}, u32[]{:S(2)}) %all-to-all-start.2) | async-done | bytes 1048608 | tf_op jit(solution)/shard_map/all_to_all | solution.py:358
  166.6 4.6 %all-to-all-start.3 = ((bf16[64,32,256]{2,0,1:T(8,128)(2,1)}), bf16[64,32,256]{2,0,1:T(8,128)(2,1)}, u32[]{:S(2)}, u32[]{:S(2)}) async-start(bf16[64,32,256]{2,0,1:T(8,128)(2,1)} %bitcast.77), calls=%async_computation.3 | async-start | bytes 2097152 | tf_op jit(solution)/shard_map/all_to_all | solution.py:373
  174.0 14.6 %collective-permute-done.6 = f32[128,17]{0,1:T(8,128)S(1)} collective-permute-done((f32[128,17]{0,1:T(8,128)S(1)}, f32[128,17]{0,1:T(8,128)S(1)}, u32[]{:S(2)}, u32[]{:S(2)}) %collective-permute-start.6) | collective-permute-done | bytes 8736 | tf_op jit(solution)/shard_map/ppermute | solution.py:380
  188.6 4.2 %collective-permute-start.7 = (f32[256,17]{0,1:T(8,128)S(1)}, f32[256,17]{0,1:T(8,128)S(1)}, u32[]{:S(2)}, u32[]{:S(2)}) collective-permute-start(f32[256,17]{0,1:T(8,128)S(1)} %maximum_select_fusion.3), channel_id=1, source_target_pairs={{0,8},{2,10},{4,12},{6,14},{8,0},{10,2},{12,4},{14,6},{16,24},{18,... | collective-permute-start | bytes 52232 | tf_op jit(solution)/shard_map/ppermute | solution.py:380
  192.8 4.8 %collective-permute-done.7 = f32[256,17]{0,1:T(8,128)S(1)} collective-permute-done((f32[256,17]{0,1:T(8,128)S(1)}, f32[256,17]{0,1:T(8,128)S(1)}, u32[]{:S(2)}, u32[]{:S(2)}) %collective-permute-start.7) | collective-permute-done | bytes 17440 | tf_op jit(solution)/shard_map/ppermute | solution.py:380
  198.9 1.7 collective-permute-done.8
  200.6 2.9 %collective-permute-start.9 = (f32[1024,17]{0,1:T(8,128)S(1)}, f32[1024,17]{0,1:T(8,128)S(1)}, u32[]{:S(2)}, u32[]{:S(2)}) collective-permute-start(f32[1024,17]{0,1:T(8,128)S(1)} %maximum_select_fusion.1), channel_id=1, source_target_pairs={{0,32},{2,34},{4,36},{6,38},{8,40},{10,42},{12,44},{14,46},{16,48}... | collective-permute-start | bytes 208904 | tf_op jit(solution)/shard_map/ppermute | solution.py:380
  203.5 3.7 %fusion.9 = (bf16[1,2048,256]{2,1,0:T(8,128)(2,1)S(1)}, bf16[1,2048,256]{2,1,0:T(8,128)(2,1)S(1)}, bf16[1,2048,256]{2,1,0:T(8,128)(2,1)}, bf16[1,2048,256]{2,1,0:T(8,128)(2,1)S(1)}) fusion(bf16[64,32,256]{2,0,1:T(8,128)(2,1)} %all-to-all-done.3, bf16[3,2048,256]{2,1,0:T(8,128)(2,1)S(1)} %fusion.4, bf16[64,32,256]{2,0,1:T(8,128)(2,1)} %all-to-all-done.2, ...), kind=kLoop, calls=%fused_computation.20 | loop fusion | flops 8912896 | bytes 10485760 | tf_op jit(solution)/shard_map/convert.6
  210.2 1.9 copy.117
  212.1 4.5 %collective-permute-start.4 = (bf16[3,2048,2]{1,2,0:T(2,128)(2,1)S(1)}, bf16[3,2048,2]{1,2,0:T(2,128)(2,1)S(1)}, u32[]{:S(2)}, u32[]{:S(2)}) collective-permute-start(bf16[3,2048,2]{1,2,0:T(2,128)(2,1)S(1)} %copy.117), channel_id=1, source_target_pairs={{2,0},{4,2},{6,4},{8,6},{10,8},{12,10},{14,12},{16,14},{18,16},{20... | collective-permute-start | bytes 73736 | tf_op jit(solution)/shard_map/ppermute | solution.py:18
  219.5 2.6 %maximum_convert_fusion.1 = f32[3,2048,258]{2,1,0:T(8,128)S(1)} fusion(bf16[3,2048,2]{2,1,0:T(8,128)(2,1)} %copy.118, bf16[1,2048,256]{2,1,0:T(8,128)(2,1)S(1)} %copy-done.3, bf16[1,2048,256]{2,1,0:T(8,128)(2,1)S(1)} %copy-done.1, bf16[1,2048,256]{2,1,0:T(8,128)(2,1)S(1)} %copy-done.5), kind=kLoop, calls=%fused_computation.13 | loop fusion | flops 12681216 | bytes 9510912 | tf_op jit(solution)/shard_map/convert_element_type | solution.py:38
  222.1 7.3 %fusion.6 = bf16[1,3,2048,256]{3,2,1,0:T(8,128)(2,1)} fusion(f32[3,2048,258]{2,1,0:T(8,128)S(1)} %maximum_convert_fusion.1, f32[3,2048]{1,0:T(4,128)S(1)} %get-tuple-element.42, f32[3,2048]{1,0:T(4,128)S(1)} %get-tuple-element.43, f32[3,2048]{1,0:T(4,128)S(1)} %bitcast.84), kind=kLoop, calls=%fused_computation.14 | loop fusion | flops 9437184 | bytes 22093824 | tf_op jit(solution)/shard_map/broadcast_in_dim | solution.py:402
  (83 shorter events, 33.5 us)
Async XLA Ops:
  0.6 19.5 %copy-start.6 = (bf16[1,3,2048,256]{3,2,1,0:T(8,128)(2,1)S(1)}, bf16[1,3,2048,256]{3,2,1,0:T(8,128)(2,1)}, u32[]{:S(2)}) copy-start(bf16[1,3,2048,256]{3,2,1,0:T(8,128)(2,1)} %param.6) | copy-start | bytes 9437188
  0.6 17.8 %copy-start.10 = (f32[3,3,2048]{2,1,0:T(4,128)S(1)}, f32[3,3,2048]{2,1,0:T(4,128)}, u32[]{:S(2)}) copy-start(f32[3,3,2048]{2,1,0:T(4,128)} %param.8) | copy-start | bytes 221188
  5.6 13.0 %collective-permute-start = (bf16[3,2048,2]{1,2,0:T(2,128)(2,1)S(1)}, bf16[3,2048,2]{1,2,0:T(2,128)(2,1)S(1)}, u32[]{:S(2)}, u32[]{:S(2)}) collective-permute-start(bf16[3,2048,2]{1,2,0:T(2,128)(2,1)S(1)} %copy.99), channel_id=1, source_target_pairs={{0,2},{2,4},{4,6},{6,8},{8,10},{10,12},{12,14},{14,16},{16,18},{18... | collective-permute-start | bytes 73736 | tf_op jit(solution)/shard_map/ppermute | solution.py:18
  12.4 29.0 %collective-permute-start.1 = (bf16[2048,128]{1,0:T(8,128)(2,1)}, bf16[2048,128]{1,0:T(8,128)(2,1)}, u32[]{:S(2)}, u32[]{:S(2)}) collective-permute-start(bf16[2048,128]{1,0:T(8,128)(2,1)} %dynamic-slice_bitcast_fusion), channel_id=1, source_target_pairs={{0,1},{1,0},{2,3},{3,2},{4,5},{5,4},{6,7},{7,6},{8,9},{9,8},{10,11... | collective-permute-start | bytes 1572872 | tf_op jit(solution)/shard_map/ppermute | solution.py:315
  31.1 35.9 %all-to-all-start = ((bf16[32,64,256]{2,1,0:T(8,128)(2,1)}), bf16[32,64,256]{2,1,0:T(8,128)(2,1)}, u32[]{:S(2)}, u32[]{:S(2)}) async-start(bf16[32,64,256]{2,1,0:T(8,128)(2,1)} %bitcast.76), calls=%async_computation | async-start | bytes 2097152 | tf_op jit(solution)/shard_map/all_to_all | solution.py:336
  39.6 1.8 copy-start.9
  42.7 0.8 copy-start.7
  42.7 1.0 copy-start.8
  67.0 33.2 %all-to-all-start.1 = ((bf16[32,64,256]{2,1,0:T(8,128)(2,1)}), bf16[32,64,256]{2,1,0:T(8,128)(2,1)}, u32[]{:S(2)}, u32[]{:S(2)}) async-start(bf16[32,64,256]{2,1,0:T(8,128)(2,1)} %multiply_convert_fusion), calls=%async_computation.1 | async-start | bytes 2097152 | tf_op jit(solution)/shard_map/all_to_all | solution.py:337
  131.2 7.4 %copy-start.11 = (f32[64,1,16]{2,1,0:T(1,128)S(1)}, f32[64,1,16]{2,1,0:T(1,128)}, u32[]{:S(2)}) copy-start(f32[64,1,16]{2,1,0:T(1,128)} %get-tuple-element.12) | copy-start | bytes 12292
  131.2 7.5 %copy-start.12 = (f32[64,1,128]{2,1,0:T(1,128)S(1)}, f32[64,1,128]{2,1,0:T(1,128)}, u32[]{:S(2)}) copy-start(f32[64,1,128]{2,1,0:T(1,128)} %get-tuple-element.13) | copy-start | bytes 98308
  134.0 32.6 %all-to-all-start.2 = ((bf16[64,32,256]{2,0,1:T(8,128)(2,1)}), bf16[64,32,256]{2,0,1:T(8,128)(2,1)}, u32[]{:S(2)}, u32[]{:S(2)}) async-start(bf16[64,32,256]{2,0,1:T(8,128)(2,1)} %copy.113), calls=%async_computation.2 | async-start | bytes 2097152 | tf_op jit(solution)/shard_map/all_to_all | solution.py:358
  139.3 3.0 %collective-permute-start.2 = (f32[64,17]{0,1:T(8,128)S(1)}, f32[64,17]{0,1:T(8,128)S(1)}, u32[]{:S(2)}, u32[]{:S(2)}) collective-permute-start(f32[64,17]{0,1:T(8,128)S(1)} %pad_maximum_fusion.3), channel_id=1, source_target_pairs={{0,64},{64,0},{128,192},{192,128},{1,65},{65,1},{129,193},{193,129... | collective-permute-start | bytes 13064 | tf_op jit(solution)/shard_map/ppermute | solution.py:368
  142.3 4.8 %collective-permute-start.3 = (f32[64,17]{0,1:T(8,128)S(1)}, f32[64,17]{0,1:T(8,128)S(1)}, u32[]{:S(2)}, u32[]{:S(2)}) collective-permute-start(f32[64,17]{0,1:T(8,128)S(1)} %fusion.24), channel_id=1, source_target_pairs={{0,128},{64,192},{128,0},{192,64},{1,129},{65,193},{129,1},{193,65... | collective-permute-start | bytes 13064 | tf_op jit(solution)/shard_map/ppermute | solution.py:368
  166.6 36.8 %all-to-all-start.3 = ((bf16[64,32,256]{2,0,1:T(8,128)(2,1)}), bf16[64,32,256]{2,0,1:T(8,128)(2,1)}, u32[]{:S(2)}, u32[]{:S(2)}) async-start(bf16[64,32,256]{2,0,1:T(8,128)(2,1)} %bitcast.77), calls=%async_computation.3 | async-start | bytes 2097152 | tf_op jit(solution)/shard_map/all_to_all | solution.py:373
  171.2 1.3 collective-permute-start.5
  172.6 15.9 %collective-permute-start.6 = (f32[128,17]{0,1:T(8,128)S(1)}, f32[128,17]{0,1:T(8,128)S(1)}, u32[]{:S(2)}, u32[]{:S(2)}) collective-permute-start(f32[128,17]{0,1:T(8,128)S(1)} %maximum_select_fusion.4), channel_id=1, source_target_pairs={{0,4},{2,6},{4,0},{6,2},{8,12},{10,14},{12,8},{14,10},{16,20},{18,... | collective-permute-start | bytes 26120 | tf_op jit(solution)/shard_map/ppermute | solution.py:380
  188.6 9.0 %collective-permute-start.7 = (f32[256,17]{0,1:T(8,128)S(1)}, f32[256,17]{0,1:T(8,128)S(1)}, u32[]{:S(2)}, u32[]{:S(2)}) collective-permute-start(f32[256,17]{0,1:T(8,128)S(1)} %maximum_select_fusion.3), channel_id=1, source_target_pairs={{0,8},{2,10},{4,12},{6,14},{8,0},{10,2},{12,4},{14,6},{16,24},{18,... | collective-permute-start | bytes 52232 | tf_op jit(solution)/shard_map/ppermute | solution.py:380
  197.6 3.0 %collective-permute-start.8 = (f32[512,17]{0,1:T(8,128)S(1)}, f32[512,17]{0,1:T(8,128)S(1)}, u32[]{:S(2)}, u32[]{:S(2)}) collective-permute-start(f32[512,17]{0,1:T(8,128)S(1)} %maximum_select_fusion.2), channel_id=1, source_target_pairs={{0,16},{2,18},{4,20},{6,22},{8,24},{10,26},{12,28},{14,30},{16,0},... | collective-permute-start | bytes 104456 | tf_op jit(solution)/shard_map/ppermute | solution.py:380
  200.6 16.0 %collective-permute-start.9 = (f32[1024,17]{0,1:T(8,128)S(1)}, f32[1024,17]{0,1:T(8,128)S(1)}, u32[]{:S(2)}, u32[]{:S(2)}) collective-permute-start(f32[1024,17]{0,1:T(8,128)S(1)} %maximum_select_fusion.1), channel_id=1, source_target_pairs={{0,32},{2,34},{4,36},{6,38},{8,40},{10,42},{12,44},{14,46},{16,48}... | collective-permute-start | bytes 208904 | tf_op jit(solution)/shard_map/ppermute | solution.py:380
  207.2 1.0 copy-start
  207.2 1.3 copy-start.2
  207.2 1.6 copy-start.4
  210.2 9.3 %copy-start.1 = (bf16[1,2048,256]{2,1,0:T(8,128)(2,1)S(1)}, bf16[1,2048,256]{2,1,0:T(8,128)(2,1)}, u32[]{:S(2)}) copy-start(bf16[1,2048,256]{2,1,0:T(8,128)(2,1)} %copy-done) | copy-start | bytes 3145732
  210.2 9.3 %copy-start.3 = (bf16[1,2048,256]{2,1,0:T(8,128)(2,1)S(1)}, bf16[1,2048,256]{2,1,0:T(8,128)(2,1)}, u32[]{:S(2)}) copy-start(bf16[1,2048,256]{2,1,0:T(8,128)(2,1)} %copy-done.2) | copy-start | bytes 3145732
  210.2 9.3 %copy-start.5 = (bf16[1,2048,256]{2,1,0:T(8,128)(2,1)S(1)}, bf16[1,2048,256]{2,1,0:T(8,128)(2,1)}, u32[]{:S(2)}) copy-start(bf16[1,2048,256]{2,1,0:T(8,128)(2,1)} %copy-done.4) | copy-start | bytes 3145732
  212.1 5.8 %collective-permute-start.4 = (bf16[3,2048,2]{1,2,0:T(2,128)(2,1)S(1)}, bf16[3,2048,2]{1,2,0:T(2,128)(2,1)S(1)}, u32[]{:S(2)}, u32[]{:S(2)}) collective-permute-start(bf16[3,2048,2]{1,2,0:T(2,128)(2,1)S(1)} %copy.117), channel_id=1, source_target_pairs={{2,0},{4,2},{6,4},{8,6},{10,8},{12,10},{14,12},{16,14},{18,16},{20... | collective-permute-start | bytes 73736 | tf_op jit(solution)/shard_map/ppermute | solution.py:18

commit v8 on v5

--- a/solution.py
+++ b/solution.py
@@ -154,7 +154,11 @@
     return jnp.where(keep, rolled, 0.0)
 
 
-def long_conv_kernel(u_ref, dz_ref, krow_ref, tab_ref, row_ref, z_ref, du_ref, mode_ref, skip_ref):
+def long_conv_kernel(backward, *refs):
+    if backward:
+        u_ref, dz_ref, krow_ref, tab_ref, row_ref, du_ref, mode_ref, skip_ref = refs
+    else:
+        u_ref, krow_ref, tab_ref, row_ref, z_ref = refs
     chans, blocks, width = u_ref.shape
     modes = tab_ref.shape[2]
     col = lax.broadcasted_iota(jnp.int32, (width, width), 1)
@@ -165,7 +169,6 @@
 
     def one_channel(c, carry):
         u_narrow = u_ref[c]
-        dz_narrow = dz_ref[c]
         tabs = tab_ref[c]
         rows = row_ref[c]
         krow = krow_ref[c]
@@ -176,37 +179,50 @@
         rate_row = rows[6:7, :]
         step_row = rows[5:6, :]
         gain = rows[7:8, 0:1]
-        ahead = pltpu.roll(jnp.broadcast_to(krow[0:1, :], (width, width)), 0, 1, stride=1, stride_axis=0)
-        ahead = jnp.where(upper, ahead, 0.0)
-        behind = pltpu.roll(jnp.broadcast_to(krow[1:2, :], (width, width)), 1, 1, stride=1, stride_axis=0)
+        u_wide = u_narrow.astype(jnp.float32)
+        ends = mat_nt(u_narrow, fall_end[0]) + mat_nt(u_narrow, fall_end[1])
+        fwd_state = ends
+        level = 0
+        span = 1
+        while span < blocks:
+            decay = rows[level : level + 1, :]
+            fwd_state = fwd_state + decay * shifted(fwd_state, span, blocks)
+            level += 1
+            span *= 2
+        state_before = shifted(fwd_state, 1, blocks)
+        if not backward:
+            ahead = pltpu.roll(
+                jnp.broadcast_to(krow[0:1, :], (width, width)), 0, 1, stride=1, stride_axis=0
+            )
+            ahead = jnp.where(upper, ahead, 0.0)
+            a_high, a_low = split_pair(ahead)
+            z_in = mat_nn(
+                jnp.concatenate([u_narrow, u_narrow], axis=1), jnp.concatenate([a_high, a_low], axis=0)
+            )
+            z_carry = wide_nn(state_before, gain_fwd)
+            z_ref[c] = (z_in + z_carry + gain * u_wide).astype(z_ref.dtype)
+            return carry
+        dz_narrow = dz_ref[c]
+        behind = pltpu.roll(
+            jnp.broadcast_to(krow[1:2, :], (width, width)), 1, 1, stride=1, stride_axis=0
+        )
         behind = jnp.where(lower, behind, 0.0)
-        a_high, a_low = split_pair(ahead)
         b_high, b_low = split_pair(behind)
-        z_in = mat_nn(
-            jnp.concatenate([u_narrow, u_narrow], axis=1), jnp.concatenate([a_high, a_low], axis=0)
-        )
         du_in = mat_nn(
             jnp.concatenate([dz_narrow, dz_narrow], axis=1), jnp.concatenate([b_high, b_low], axis=0)
         )
-        ends = mat_nt(u_narrow, fall_end[0]) + mat_nt(u_narrow, fall_end[1])
         starts = mat_nt(dz_narrow, fall_start[0]) + mat_nt(dz_narrow, fall_start[1])
-        fwd_state = ends
         bwd_state = starts
         level = 0
         span = 1
         while span < blocks:
             decay = rows[level : level + 1, :]
-            fwd_state = fwd_state + decay * shifted(fwd_state, span, blocks)
             bwd_state = bwd_state + decay * shifted(bwd_state, -span, blocks)
             level += 1
             span *= 2
-        state_before = shifted(fwd_state, 1, blocks)
         state_after = shifted(bwd_state, -1, blocks)
-        z_carry = wide_nn(state_before, gain_fwd)
         du_carry = wide_nn(state_after, gain_bwd)
-        u_wide = u_narrow.astype(jnp.float32)
         dz_wide = dz_narrow.astype(jnp.float32)
-        z_ref[c] = (z_in + z_carry + gain * u_wide).astype(z_ref.dtype)
         du_ref[c] = (du_in + du_carry + gain * dz_wide).astype(du_ref.dtype)
         rise = jnp.exp(lag_ids * rate_row)
         crossed = mat_tn(u_narrow, dz_narrow)
@@ -221,7 +237,7 @@
         skip_ref[c] = jnp.broadcast_to(jnp.sum(u_wide * dz_wide), skip_ref.shape[1:])
         return carry
 
-    lax.fori_loop(0, chans, one_channel, 0, unroll=8)
+    lax.fori_loop(0, chans, one_channel, 0, unroll=chans)
 
 
 def long_conv_tables(rate_rows, weight_rows, gain_rows, width, blocks):
@@ -259,33 +275,42 @@
     tabs, rows, krow = long_conv_tables(rate_rows, weight_rows, gain_rows, width, blocks)
     step = min(chans_per_step, chan_count)
     data_spec = pl.BlockSpec((step, blocks, width), lambda i: (i, 0, 0))
-    return pl.pallas_call(
-        long_conv_kernel,
+    side_specs = [
+        pl.BlockSpec((step,) + krow.shape[1:], lambda i: (i, 0, 0)),
+        pl.BlockSpec((step,) + tabs.shape[1:], lambda i: (i, 0, 0, 0)),
+        pl.BlockSpec((step,) + rows.shape[1:], lambda i: (i, 0, 0)),
+    ]
+    forward = pl.pallas_call(
+        partial(long_conv_kernel, False),
         grid=(chan_count // step,),
-        in_specs=[
-            data_spec,
-            data_spec,
-            pl.BlockSpec((step,) + krow.shape[1:], lambda i: (i, 0, 0)),
-            pl.BlockSpec((step,) + tabs.shape[1:], lambda i: (i, 0, 0, 0)),
-            pl.BlockSpec((step,) + rows.shape[1:], lambda i: (i, 0, 0)),
-        ],
+        in_specs=[data_spec] + side_specs,
+        out_specs=data_spec,
+        out_shape=jax.ShapeDtypeStruct(u_blocks.shape, jnp.bfloat16),
+        cost_estimate=pl.CostEstimate(
+            flops=chan_count * 300 * width * width * blocks, transcendentals=0,
+            bytes_accessed=chan_count * blocks * width * 4 + tabs.size * 2,
+        ),
+    )(u_blocks, krow, tabs, rows)
+    backward = pl.pallas_call(
+        partial(long_conv_kernel, True),
+        grid=(chan_count // step,),
+        in_specs=[data_spec, data_spec] + side_specs,
         out_specs=[
-            data_spec,
             data_spec,
             pl.BlockSpec((step, 1, modes), lambda i: (i, 0, 0)),
             pl.BlockSpec((step, 1, 128), lambda i: (i, 0, 0)),
         ],
         out_shape=[
             jax.ShapeDtypeStruct(u_blocks.shape, jnp.bfloat16),
-            jax.ShapeDtypeStruct(u_blocks.shape, jnp.bfloat16),
             jax.ShapeDtypeStruct((chan_count, 1, modes), jnp.float32),
             jax.ShapeDtypeStruct((chan_count, 1, 128), jnp.float32),
         ],
         cost_estimate=pl.CostEstimate(
-            flops=chan_count * 34 * width * width * blocks, transcendentals=chan_count * width * modes,
-            bytes_accessed=chan_count * blocks * width * 8 + tabs.size * 2,
+            flops=chan_count * 500 * width * width * blocks, transcendentals=chan_count * width * modes,
+            bytes_accessed=chan_count * blocks * width * 6 + tabs.size * 2,
         ),
     )(u_blocks, dz_blocks, krow, tabs, rows)
+    return (forward,) + tuple(backward)
 
 
 def grouped(function, arrays, group_size):

time: 230 us -> 213 us (0.926)
  waiting for transfers between devices: 75.3 us -> 46.6 us
  Pallas kernels: 28.2 us -> 36.6 us
  starting transfers between devices: 53.5 us -> 56.4 us
    all_to_all x1, waiting for transfers between devices: 25.3 us -> 0.01 us  [on_device(): lax.all_to_all(back_rows, 'ctx', split_axis=1, concat_axis=0, tiled=True)]
    pallas_call x1 -> x2, Pallas kernels: 28.2 us -> 36.6 us  [the longest x1 24.8 us: long_conv(): pl.pallas_call(partial(long_conv_kernel, True), grid=(chan_count // step,...]
    all_to_all x1, starting transfers between devices: 4.57 us -> 7.85 us  [on_device(): lax.all_to_all(back_rows, 'ctx', split_axis=1, concat_axis=0, tiled=True)]
  transfers between devices with their start and end apart: 14 -> 14, of which waited for: 10 -> 8; matrix products, arithmetic and copies ran while one was open for 20% -> 26% of each run, Pallas kernels for 0% -> 17%
where the time goes in v8:
time: 213 us; the launch traced here: 212 us
  starting transfers between devices  56.4 us (26%)
  waiting for transfers between devices  46.6 us (22%)
  other arithmetic  41.1 us (19%)
  Pallas kernels  36.6 us (17%)
  local copies, waits for them, and re-layouts  30.4 us (14%)
    pallas_call x1, Pallas kernels, long_conv(): pl.pallas_call(partial(long_conv_kernel, True), grid=(chan_count // step,...  24.8 us
    all_to_all x1, waiting for transfers between devices, on_device(): lax.all_to_all(product, 'ctx', split_axis=0, concat_axis=1, tiled=True)  20.6 us
    ppermute x5, waiting for transfers between devices, on_device(): theirs = lax.ppermute(gathered, 'ctx', partners)  12.4 us
    ppermute x5, starting transfers between devices, on_device(): theirs = lax.ppermute(gathered, 'ctx', partners)  11.9 us
    pallas_call x1, Pallas kernels, long_conv(): pl.pallas_call(partial(long_conv_kernel, False), grid=(chan_count // step...  11.8 us
    all_to_all x1, waiting for transfers between devices, on_device(): lax.all_to_all(adjoint, 'ctx', split_axis=0, concat_axis=1, tiled=True)  10.6 us
    ppermute x2, starting transfers between devices, from_behind(): return lax.ppermute(shard, axis, pairs)  9.69 us
    unnamed x7, other arithmetic  7.91 us
  transfers between devices with their start and end apart: 14, of which 8 were waited for; matrix products, arithmetic and copies ran while one was open for 26% of the time, Pallas kernels for 17%

profile of v8, /device:TPU:1, one launch (start us, length us, event | category | flops | bytes accessed | tf_op | source)
XLA Modules:
  0.0 212.0 jit_solution(1770029018106248740)
XLA Ops:
  0.6 1.9 slice.71
  3.9 5.2 %collective-permute-start = (bf16[3,2048,2]{1,2,0:T(2,128)(2,1)}, bf16[3,2048,2]{1,2,0:T(2,128)(2,1)}, u32[]{:S(2)}, u32[]{:S(2)}) collective-permute-start(bf16[3,2048,2]{1,2,0:T(2,128)(2,1)} %copy.100), channel_id=1, source_target_pairs={{0,2},{2,4},{4,6},{6,8},{8,10},{10,12},{12,14},{14,16},{16,18},{18... | collective-permute-start | bytes 73736 | tf_op jit(solution)/shard_map/ppermute | solution.py:18
  9.1 1.9 dynamic-slice_bitcast_fusion
  11.0 6.0 %collective-permute-start.1 = (bf16[2048,128]{1,0:T(8,128)(2,1)}, bf16[2048,128]{1,0:T(8,128)(2,1)}, u32[]{:S(2)}, u32[]{:S(2)}) collective-permute-start(bf16[2048,128]{1,0:T(8,128)(2,1)} %dynamic-slice_bitcast_fusion), channel_id=1, source_target_pairs={{0,1},{1,0},{2,3},{3,2},{4,5},{5,4},{6,7},{7,6},{8,9},{9,8},{10,11... | collective-permute-start | bytes 1572872 | tf_op jit(solution)/shard_map/ppermute | solution.py:340
  27.8 1.8 stack.62.refs_3_.refs_4_
  29.6 2.3 %copy.101 = bf16[3,2048,2]{2,1,0:T(8,128)(2,1)} copy(bf16[3,2048,2]{1,2,0:T(2,128)(2,1)} %collective-permute-done) | data formatting | bytes 49152 | tf_op jit(solution)/shard_map/ppermute | solution.py:18
  31.9 3.3 %maximum_convert_fusion = f32[3,2048,258]{2,1,0:T(8,128)S(1)} fusion(bf16[3,2048,256]{2,1,0:T(8,128)(2,1)S(1)} %bitcast.65, bf16[3,2048,2]{2,1,0:T(8,128)(2,1)} %copy.101), kind=kLoop, calls=%fused_computation.12 | loop fusion | flops 6340608 | bytes 9510912 | tf_op jit(solution)/shard_map/convert_element_type | solution.py:24
  35.2 6.4 %fusion.4 = bf16[3,2048,256]{2,1,0:T(8,128)(2,1)S(1)} fusion(f32[3,2048,258]{2,1,0:T(8,128)S(1)} %maximum_convert_fusion, f32[3,2048]{1,0:T(4,128)S(1)} %get-tuple-element.36, f32[3,2048]{1,0:T(4,128)S(1)} %get-tuple-element.37, f32[3,2048]{1,0:T(4,128)S(1)} %bitcast.75), kind=kLoop, calls=%fused_computation.8 | loop fusion | flops 9437184 | bytes 22093824 | tf_op jit(solution)/shard_map/convert_element_type | solution.py:350
  42.9 7.5 %all-to-all-start = ((bf16[32,64,256]{2,1,0:T(8,128)(2,1)}), bf16[32,64,256]{2,1,0:T(8,128)(2,1)}, u32[]{:S(2)}, u32[]{:S(2)}) async-start(bf16[32,64,256]{2,1,0:T(8,128)(2,1)} %bitcast.70), calls=%async_computation | async-start | bytes 2097152 | tf_op jit(solution)/shard_map/all_to_all | solution.py:361
  57.7 20.6 %all-to-all-done = bf16[32,64,256]{2,1,0:T(8,128)(2,1)} async-done(((bf16[32,64,256]{2,1,0:T(8,128)(2,1)}), bf16[32,64,256]{2,1,0:T(8,128)(2,1)}, u32[]{:S(2)}, u32[]{:S(2)}) %all-to-all-start) | async-done | bytes 1048608 | tf_op jit(solution)/shard_map/all_to_all | solution.py:361
  78.3 4.6 %all-to-all-start.2 = ((bf16[32,64,256]{2,1,0:T(8,128)(2,1)}), bf16[32,64,256]{2,1,0:T(8,128)(2,1)}, u32[]{:S(2)}, u32[]{:S(2)}) async-start(bf16[32,64,256]{2,1,0:T(8,128)(2,1)} %multiply_convert_fusion), calls=%async_computation.2 | async-start | bytes 2097152 | tf_op jit(solution)/shard_map/all_to_all | solution.py:362
  82.9 2.8 %copy.132 = bf16[32,64,256]{2,0,1:T(8,128)(2,1)} copy(bf16[32,64,256]{2,1,0:T(8,128)(2,1)} %all-to-all-done) | data formatting | bytes 2097152 | tf_op jit(solution)/shard_map/all_to_all | solution.py:361
  85.7 11.8 %shard_map.93 = bf16[64,32,256]{2,1,0:T(8,128)(2,1)} custom-call(bf16[64,32,256]{2,1,0:T(8,128)(2,1)} %bitcast.71, f32[64,2,256]{2,1,0:T(2,128)} %pad_maximum_fusion.2.refs_1_.refs_2_, bf16[64,8,16,256]{3,2,1,0:T(8,128)(2,1)} %fusion.16.refs_2_.refs_3_, f32[64,8,16]{2,1,0:T(8,128)} %stack.62.refs_3_.refs_4_), custom_call_target="tpu_custom_call" | custom-call | flops 40265318400 | bytes 6291456 | tf_op jit(solution)/shard_map/pallas_call | solution.py:283
  97.5 2.8 %copy.113 = bf16[64,32,256]{2,0,1:T(8,128)(2,1)} copy(bf16[64,32,256]{2,1,0:T(8,128)(2,1)} %shard_map.93) | data formatting | bytes 2097152 | tf_op jit(solution)/shard_map/pallas_call | solution.py:283
  100.3 10.6 %all-to-all-done.2 = bf16[32,64,256]{2,1,0:T(8,128)(2,1)} async-done(((bf16[32,64,256]{2,1,0:T(8,128)(2,1)}), bf16[32,64,256]{2,1,0:T(8,128)(2,1)}, u32[]{:S(2)}, u32[]{:S(2)}) %all-to-all-start.2) | async-done | bytes 1048608 | tf_op jit(solution)/shard_map/all_to_all | solution.py:362
  110.9 4.6 %all-to-all-start.1 = ((bf16[64,32,256]{2,0,1:T(8,128)(2,1)}), bf16[64,32,256]{2,0,1:T(8,128)(2,1)}, u32[]{:S(2)}, u32[]{:S(2)}) async-start(bf16[64,32,256]{2,0,1:T(8,128)(2,1)} %copy.113), calls=%async_computation.1 | async-start | bytes 2097152 | tf_op jit(solution)/shard_map/all_to_all | solution.py:384
  115.5 2.8 %copy.131 = bf16[32,64,256]{2,0,1:T(8,128)(2,1)} copy(bf16[32,64,256]{2,1,0:T(8,128)(2,1)} %all-to-all-done.2) | data formatting | bytes 2097152 | tf_op jit(solution)/shard_map/all_to_all | solution.py:362
  118.2 24.8 %shard_map.94 = (bf16[64,32,256]{2,1,0:T(8,128)(2,1)}, f32[64,1,16]{2,1,0:T(1,128)}, f32[64,1,128]{2,1,0:T(1,128)}) custom-call(bf16[64,32,256]{2,1,0:T(8,128)(2,1)} %bitcast.72, bf16[64,32,256]{2,1,0:T(8,128)(2,1)} %bitcast.73, f32[64,2,256]{2,1,0:T(2,128)} %pad_maximum_fusion.2.refs_1_.refs_2_, bf16[64,8,16,256]{3,2,1,0:T(8,128)(2,1)} %fusion.16.refs_2_.refs_3_, ...), custom_call_target="tpu_custom_call" | custom-call | flops 67108864000 | bytes 7340032 | tf_op jit(solution)/shard_map/pallas_call | solution.py:294
  143.0 2.8 %copy.115 = bf16[64,32,256]{2,0,1:T(8,128)(2,1)} copy(bf16[64,32,256]{2,1,0:T(8,128)(2,1)} %get-tuple-element.7) | data formatting | bytes 2097152 | tf_op jit(solution)/shard_map/pallas_call | solution.py:294
  145.8 7.9 %all-to-all-start.3 = ((bf16[64,32,256]{2,0,1:T(8,128)(2,1)}), bf16[64,32,256]{2,0,1:T(8,128)(2,1)}, u32[]{:S(2)}, u32[]{:S(2)}) async-start(bf16[64,32,256]{2,0,1:T(8,128)(2,1)} %copy.115), calls=%async_computation.3 | async-start | bytes 2097152 | tf_op jit(solution)/shard_map/all_to_all | solution.py:385
  157.4 2.9 %collective-permute-start.4 = (f32[64,17]{0,1:T(8,128)S(1)}, f32[64,17]{0,1:T(8,128)S(1)}, u32[]{:S(2)}, u32[]{:S(2)}) collective-permute-start(f32[64,17]{0,1:T(8,128)S(1)} %fusion.24), channel_id=1, source_target_pairs={{0,128},{64,192},{128,0},{192,64},{1,129},{65,193},{129,1},{193,65... | collective-permute-start | bytes 13064 | tf_op jit(solution)/shard_map/ppermute | solution.py:396
  161.7 2.0 collective-permute-start.5
  166.0 5.0 %collective-permute-done.6 = f32[128,17]{0,1:T(8,128)S(1)} collective-permute-done((f32[128,17]{0,1:T(8,128)S(1)}, f32[128,17]{0,1:T(8,128)S(1)}, u32[]{:S(2)}, u32[]{:S(2)}) %collective-permute-start.6) | collective-permute-done | bytes 8736 | tf_op jit(solution)/shard_map/ppermute | solution.py:406
  171.0 4.2 %collective-permute-start.7 = (f32[256,17]{0,1:T(8,128)S(1)}, f32[256,17]{0,1:T(8,128)S(1)}, u32[]{:S(2)}, u32[]{:S(2)}) collective-permute-start(f32[256,17]{0,1:T(8,128)S(1)} %maximum_select_fusion.3), channel_id=1, source_target_pairs={{0,8},{2,10},{4,12},{6,14},{8,0},{10,2},{12,4},{14,6},{16,24},{18,... | collective-permute-start | bytes 52232 | tf_op jit(solution)/shard_map/ppermute | solution.py:406
  175.2 4.8 %collective-permute-done.7 = f32[256,17]{0,1:T(8,128)S(1)} collective-permute-done((f32[256,17]{0,1:T(8,128)S(1)}, f32[256,17]{0,1:T(8,128)S(1)}, u32[]{:S(2)}, u32[]{:S(2)}) %collective-permute-start.7) | collective-permute-done | bytes 17440 | tf_op jit(solution)/shard_map/ppermute | solution.py:406
  181.3 1.8 collective-permute-done.8
  183.0 3.0 %collective-permute-start.9 = (f32[1024,17]{0,1:T(8,128)S(1)}, f32[1024,17]{0,1:T(8,128)S(1)}, u32[]{:S(2)}, u32[]{:S(2)}) collective-permute-start(f32[1024,17]{0,1:T(8,128)S(1)} %maximum_select_fusion.1), channel_id=1, source_target_pairs={{0,32},{2,34},{4,36},{6,38},{8,40},{10,42},{12,44},{14,46},{16,48}... | collective-permute-start | bytes 208904 | tf_op jit(solution)/shard_map/ppermute | solution.py:406
  186.0 3.7 %fusion.9 = (bf16[1,2048,256]{2,1,0:T(8,128)(2,1)S(1)}, bf16[1,2048,256]{2,1,0:T(8,128)(2,1)S(1)}, bf16[1,2048,256]{2,1,0:T(8,128)(2,1)}, bf16[1,2048,256]{2,1,0:T(8,128)(2,1)S(1)}) fusion(bf16[64,32,256]{2,0,1:T(8,128)(2,1)} %all-to-all-done.3, bf16[3,2048,256]{2,1,0:T(8,128)(2,1)S(1)} %fusion.4, bf16[64,32,256]{2,0,1:T(8,128)(2,1)} %all-to-all-done.1, ...), kind=kLoop, calls=%fused_computation.20 | loop fusion | flops 8912896 | bytes 10485760 | tf_op jit(solution)/shard_map/convert.6
  192.8 1.9 copy.116
  194.7 4.5 %collective-permute-start.2 = (bf16[3,2048,2]{1,2,0:T(2,128)(2,1)S(1)}, bf16[3,2048,2]{1,2,0:T(2,128)(2,1)S(1)}, u32[]{:S(2)}, u32[]{:S(2)}) collective-permute-start(bf16[3,2048,2]{1,2,0:T(2,128)(2,1)S(1)} %copy.116), channel_id=1, source_target_pairs={{2,0},{4,2},{6,4},{8,6},{10,8},{12,10},{14,12},{16,14},{18,16},{20... | collective-permute-start | bytes 73736 | tf_op jit(solution)/shard_map/ppermute | solution.py:18
  202.1 2.6 %maximum_convert_fusion.1 = f32[3,2048,258]{2,1,0:T(8,128)S(1)} fusion(bf16[3,2048,2]{2,1,0:T(8,128)(2,1)} %copy.117, bf16[1,2048,256]{2,1,0:T(8,128)(2,1)S(1)} %copy-done.3, bf16[1,2048,256]{2,1,0:T(8,128)(2,1)S(1)} %copy-done.1, bf16[1,2048,256]{2,1,0:T(8,128)(2,1)S(1)} %copy-done.5), kind=kLoop, calls=%fused_computation.13 | loop fusion | flops 12681216 | bytes 9510912 | tf_op jit(solution)/shard_map/convert_element_type | solution.py:38
  204.7 7.3 %fusion.6 = bf16[1,3,2048,256]{3,2,1,0:T(8,128)(2,1)} fusion(f32[3,2048,258]{2,1,0:T(8,128)S(1)} %maximum_convert_fusion.1, f32[3,2048]{1,0:T(4,128)S(1)} %get-tuple-element.36, f32[3,2048]{1,0:T(4,128)S(1)} %get-tuple-element.37, f32[3,2048]{1,0:T(4,128)S(1)} %bitcast.76), kind=kLoop, calls=%fused_computation.14 | loop fusion | flops 9437184 | bytes 22093824 | tf_op jit(solution)/shard_map/broadcast_in_dim | solution.py:428
  (81 shorter events, 35.3 us)
Async XLA Ops:
  3.9 28.0 %copy-start.6 = (bf16[1,3,2048,256]{3,2,1,0:T(8,128)(2,1)S(1)}, bf16[1,3,2048,256]{3,2,1,0:T(8,128)(2,1)}, u32[]{:S(2)}) copy-start(bf16[1,3,2048,256]{3,2,1,0:T(8,128)(2,1)} %param.6) | copy-start | bytes 9437188
  3.9 25.8 %collective-permute-start = (bf16[3,2048,2]{1,2,0:T(2,128)(2,1)}, bf16[3,2048,2]{1,2,0:T(2,128)(2,1)}, u32[]{:S(2)}, u32[]{:S(2)}) collective-permute-start(bf16[3,2048,2]{1,2,0:T(2,128)(2,1)} %copy.100), channel_id=1, source_target_pairs={{0,2},{2,4},{4,6},{6,8},{8,10},{10,12},{12,14},{14,16},{16,18},{18... | collective-permute-start | bytes 73736 | tf_op jit(solution)/shard_map/ppermute | solution.py:18
  11.0 43.0 %collective-permute-start.1 = (bf16[2048,128]{1,0:T(8,128)(2,1)}, bf16[2048,128]{1,0:T(8,128)(2,1)}, u32[]{:S(2)}, u32[]{:S(2)}) collective-permute-start(bf16[2048,128]{1,0:T(8,128)(2,1)} %dynamic-slice_bitcast_fusion), channel_id=1, source_target_pairs={{0,1},{1,0},{2,3},{3,2},{4,5},{5,4},{6,7},{7,6},{8,9},{9,8},{10,11... | collective-permute-start | bytes 1572872 | tf_op jit(solution)/shard_map/ppermute | solution.py:340
  42.9 35.4 %all-to-all-start = ((bf16[32,64,256]{2,1,0:T(8,128)(2,1)}), bf16[32,64,256]{2,1,0:T(8,128)(2,1)}, u32[]{:S(2)}, u32[]{:S(2)}) async-start(bf16[32,64,256]{2,1,0:T(8,128)(2,1)} %bitcast.70), calls=%async_computation | async-start | bytes 2097152 | tf_op jit(solution)/shard_map/all_to_all | solution.py:361
  50.4 3.7 %copy-start.9 = (bf16[1,4096,128]{2,1,0:T(8,128)(2,1)S(1)}, bf16[1,4096,128]{2,1,0:T(8,128)(2,1)}, u32[]{:S(2)}) copy-start(bf16[1,4096,128]{2,1,0:T(8,128)(2,1)} %param.7) | copy-start | bytes 3145732
  55.3 0.8 copy-start.7
  55.3 1.1 copy-start.8
  78.3 32.6 %all-to-all-start.2 = ((bf16[32,64,256]{2,1,0:T(8,128)(2,1)}), bf16[32,64,256]{2,1,0:T(8,128)(2,1)}, u32[]{:S(2)}, u32[]{:S(2)}) async-start(bf16[32,64,256]{2,1,0:T(8,128)(2,1)} %multiply_convert_fusion), calls=%async_computation.2 | async-start | bytes 2097152 | tf_op jit(solution)/shard_map/all_to_all | solution.py:362
  110.9 34.9 %all-to-all-start.1 = ((bf16[64,32,256]{2,0,1:T(8,128)(2,1)}), bf16[64,32,256]{2,0,1:T(8,128)(2,1)}, u32[]{:S(2)}, u32[]{:S(2)}) async-start(bf16[64,32,256]{2,0,1:T(8,128)(2,1)} %copy.113), calls=%async_computation.1 | async-start | bytes 2097152 | tf_op jit(solution)/shard_map/all_to_all | solution.py:384
  143.0 10.7 %copy-start.10 = (f32[64,1,16]{2,1,0:T(1,128)S(1)}, f32[64,1,16]{2,1,0:T(1,128)}, u32[]{:S(2)}) copy-start(f32[64,1,16]{2,1,0:T(1,128)} %get-tuple-element.8) | copy-start | bytes 12292
  143.0 10.8 %copy-start.11 = (f32[64,1,128]{2,1,0:T(1,128)S(1)}, f32[64,1,128]{2,1,0:T(1,128)}, u32[]{:S(2)}) copy-start(f32[64,1,128]{2,1,0:T(1,128)} %get-tuple-element.9) | copy-start | bytes 98308
  145.8 40.2 %all-to-all-start.3 = ((bf16[64,32,256]{2,0,1:T(8,128)(2,1)}), bf16[64,32,256]{2,0,1:T(8,128)(2,1)}, u32[]{:S(2)}, u32[]{:S(2)}) async-start(bf16[64,32,256]{2,0,1:T(8,128)(2,1)} %copy.115), calls=%async_computation.3 | async-start | bytes 2097152 | tf_op jit(solution)/shard_map/all_to_all | solution.py:385
  154.3 3.0 %collective-permute-start.3 = (f32[64,17]{0,1:T(8,128)S(1)}, f32[64,17]{0,1:T(8,128)S(1)}, u32[]{:S(2)}, u32[]{:S(2)}) collective-permute-start(f32[64,17]{0,1:T(8,128)S(1)} %pad_maximum_fusion.3), channel_id=1, source_target_pairs={{0,64},{64,0},{128,192},{192,128},{1,65},{65,1},{129,193},{193,129... | collective-permute-start | bytes 13064 | tf_op jit(solution)/shard_map/ppermute | solution.py:396
  157.4 4.3 %collective-permute-start.4 = (f32[64,17]{0,1:T(8,128)S(1)}, f32[64,17]{0,1:T(8,128)S(1)}, u32[]{:S(2)}, u32[]{:S(2)}) collective-permute-start(f32[64,17]{0,1:T(8,128)S(1)} %fusion.24), channel_id=1, source_target_pairs={{0,128},{64,192},{128,0},{192,64},{1,129},{65,193},{129,1},{193,65... | collective-permute-start | bytes 13064 | tf_op jit(solution)/shard_map/ppermute | solution.py:396
  161.7 2.8 %collective-permute-start.5 = (f32[64,17]{0,1:T(8,128)S(1)}, f32[64,17]{0,1:T(8,128)S(1)}, u32[]{:S(2)}, u32[]{:S(2)}) collective-permute-start(f32[64,17]{0,1:T(8,128)S(1)} %add.49), channel_id=1, source_target_pairs={{0,2},{2,0},{4,6},{6,4},{8,10},{10,8},{12,14},{14,12},{16,18},{18,... | collective-permute-start | bytes 13064 | tf_op jit(solution)/shard_map/ppermute | solution.py:406
  164.5 6.5 %collective-permute-start.6 = (f32[128,17]{0,1:T(8,128)S(1)}, f32[128,17]{0,1:T(8,128)S(1)}, u32[]{:S(2)}, u32[]{:S(2)}) collective-permute-start(f32[128,17]{0,1:T(8,128)S(1)} %maximum_select_fusion.4), channel_id=1, source_target_pairs={{0,4},{2,6},{4,0},{6,2},{8,12},{10,14},{12,8},{14,10},{16,20},{18,... | collective-permute-start | bytes 26120 | tf_op jit(solution)/shard_map/ppermute | solution.py:406
  171.0 8.9 %collective-permute-start.7 = (f32[256,17]{0,1:T(8,128)S(1)}, f32[256,17]{0,1:T(8,128)S(1)}, u32[]{:S(2)}, u32[]{:S(2)}) collective-permute-start(f32[256,17]{0,1:T(8,128)S(1)} %maximum_select_fusion.3), channel_id=1, source_target_pairs={{0,8},{2,10},{4,12},{6,14},{8,0},{10,2},{12,4},{14,6},{16,24},{18,... | collective-permute-start | bytes 52232 | tf_op jit(solution)/shard_map/ppermute | solution.py:406
  180.0 3.0 %collective-permute-start.8 = (f32[512,17]{0,1:T(8,128)S(1)}, f32[512,17]{0,1:T(8,128)S(1)}, u32[]{:S(2)}, u32[]{:S(2)}) collective-permute-start(f32[512,17]{0,1:T(8,128)S(1)} %maximum_select_fusion.2), channel_id=1, source_target_pairs={{0,16},{2,18},{4,20},{6,22},{8,24},{10,26},{12,28},{14,30},{16,0},... | collective-permute-start | bytes 104456 | tf_op jit(solution)/shard_map/ppermute | solution.py:406
  183.0 16.2 %collective-permute-start.9 = (f32[1024,17]{0,1:T(8,128)S(1)}, f32[1024,17]{0,1:T(8,128)S(1)}, u32[]{:S(2)}, u32[]{:S(2)}) collective-permute-start(f32[1024,17]{0,1:T(8,128)S(1)} %maximum_select_fusion.1), channel_id=1, source_target_pairs={{0,32},{2,34},{4,36},{6,38},{8,40},{10,42},{12,44},{14,46},{16,48}... | collective-permute-start | bytes 208904 | tf_op jit(solution)/shard_map/ppermute | solution.py:406
  189.8 1.0 copy-start
  189.8 1.3 copy-start.2
  189.8 1.6 copy-start.4
  192.8 9.3 %copy-start.1 = (bf16[1,2048,256]{2,1,0:T(8,128)(2,1)S(1)}, bf16[1,2048,256]{2,1,0:T(8,128)(2,1)}, u32[]{:S(2)}) copy-start(bf16[1,2048,256]{2,1,0:T(8,128)(2,1)} %copy-done) | copy-start | bytes 3145732
  192.8 9.3 %copy-start.3 = (bf16[1,2048,256]{2,1,0:T(8,128)(2,1)S(1)}, bf16[1,2048,256]{2,1,0:T(8,128)(2,1)}, u32[]{:S(2)}) copy-start(bf16[1,2048,256]{2,1,0:T(8,128)(2,1)} %copy-done.2) | copy-start | bytes 3145732
  192.8 9.3 %copy-start.5 = (bf16[1,2048,256]{2,1,0:T(8,128)(2,1)S(1)}, bf16[1,2048,256]{2,1,0:T(8,128)(2,1)}, u32[]{:S(2)}) copy-start(bf16[1,2048,256]{2,1,0:T(8,128)(2,1)} %copy-done.4) | copy-start | bytes 3145732
  194.7 5.8 %collective-permute-start.2 = (bf16[3,2048,2]{1,2,0:T(2,128)(2,1)S(1)}, bf16[3,2048,2]{1,2,0:T(2,128)(2,1)S(1)}, u32[]{:S(2)}, u32[]{:S(2)}) collective-permute-start(bf16[3,2048,2]{1,2,0:T(2,128)(2,1)S(1)} %copy.116), channel_id=1, source_target_pairs={{2,0},{4,2},{6,4},{8,6},{10,8},{12,10},{14,12},{16,14},{18,16},{20... | collective-permute-start | bytes 73736 | tf_op jit(solution)/shard_map/ppermute | solution.py:18

commit v9 on v8

--- a/solution.py
+++ b/solution.py
@@ -269,7 +269,7 @@
     return tabs, jnp.stack(levels, axis=1), krow
 
 
-def long_conv(u_blocks, dz_blocks, rate_rows, weight_rows, gain_rows, chans_per_step=8):
+def long_conv(u_blocks, dz_blocks, rate_rows, weight_rows, gain_rows, chans_per_step=16):
     chan_count, blocks, width = u_blocks.shape
     modes = rate_rows.shape[1]
     tabs, rows, krow = long_conv_tables(rate_rows, weight_rows, gain_rows, width, blocks)

time: 213 us -> 211 us (level)
  transfers between devices with their start and end apart: 14 -> 14, of which waited for: 8 -> 8; matrix products, arithmetic and copies ran while one was open for 26% -> 26% of each run, Pallas kernels for 17% -> 16%
where the time goes in v9:
time: 211 us; the launch traced here: 210 us
  starting transfers between devices  56.4 us (27%)
  waiting for transfers between devices  46.8 us (22%)
  other arithmetic  41.1 us (19%)
  Pallas kernels  34.6 us (16%)
  local copies, waits for them, and re-layouts  30.4 us (14%)
    pallas_call x1, Pallas kernels, long_conv(): pl.pallas_call(partial(long_conv_kernel, True), grid=(chan_count // step,...  23.3 us
    all_to_all x1, waiting for transfers between devices, on_device(): lax.all_to_all(product, 'ctx', split_axis=0, concat_axis=1, tiled=True)  20.6 us
    ppermute x5, waiting for transfers between devices, on_device(): theirs = lax.ppermute(gathered, 'ctx', partners)  12.2 us
    ppermute x5, starting transfers between devices, on_device(): theirs = lax.ppermute(gathered, 'ctx', partners)  11.9 us
    pallas_call x1, Pallas kernels, long_conv(): pl.pallas_call(partial(long_conv_kernel, False), grid=(chan_count // step...  11.3 us
    all_to_all x1, waiting for transfers between devices, on_device(): lax.all_to_all(adjoint, 'ctx', split_axis=0, concat_axis=1, tiled=True)  11 us
    ppermute x2, starting transfers between devices, from_behind(): return lax.ppermute(shard, axis, pairs)  9.69 us
    unnamed x7, other arithmetic  7.91 us
  transfers between devices with their start and end apart: 14, of which 8 were waited for; matrix products, arithmetic and copies ran while one was open for 26% of the time, Pallas kernels for 16%

profile of v9, /device:TPU:1, one launch (start us, length us, event | category | flops | bytes accessed | tf_op | source)
XLA Modules:
  0.0 210.3 jit_solution(14521949030961460561)
XLA Ops:
  0.6 1.9 slice.71
  3.9 5.2 %collective-permute-start = (bf16[3,2048,2]{1,2,0:T(2,128)(2,1)}, bf16[3,2048,2]{1,2,0:T(2,128)(2,1)}, u32[]{:S(2)}, u32[]{:S(2)}) collective-permute-start(bf16[3,2048,2]{1,2,0:T(2,128)(2,1)} %copy.100), channel_id=1, source_target_pairs={{0,2},{2,4},{4,6},{6,8},{8,10},{10,12},{12,14},{14,16},{16,18},{18... | collective-permute-start | bytes 73736 | tf_op jit(solution)/shard_map/ppermute | solution.py:18
  9.1 1.9 dynamic-slice_bitcast_fusion
  11.0 6.0 %collective-permute-start.1 = (bf16[2048,128]{1,0:T(8,128)(2,1)}, bf16[2048,128]{1,0:T(8,128)(2,1)}, u32[]{:S(2)}, u32[]{:S(2)}) collective-permute-start(bf16[2048,128]{1,0:T(8,128)(2,1)} %dynamic-slice_bitcast_fusion), channel_id=1, source_target_pairs={{0,1},{1,0},{2,3},{3,2},{4,5},{5,4},{6,7},{7,6},{8,9},{9,8},{10,11... | collective-permute-start | bytes 1572872 | tf_op jit(solution)/shard_map/ppermute | solution.py:340
  27.8 1.8 stack.62.refs_3_.refs_4_
  29.6 2.3 %copy.101 = bf16[3,2048,2]{2,1,0:T(8,128)(2,1)} copy(bf16[3,2048,2]{1,2,0:T(2,128)(2,1)} %collective-permute-done) | data formatting | bytes 49152 | tf_op jit(solution)/shard_map/ppermute | solution.py:18
  31.9 3.3 %maximum_convert_fusion = f32[3,2048,258]{2,1,0:T(8,128)S(1)} fusion(bf16[3,2048,256]{2,1,0:T(8,128)(2,1)S(1)} %bitcast.65, bf16[3,2048,2]{2,1,0:T(8,128)(2,1)} %copy.101), kind=kLoop, calls=%fused_computation.12 | loop fusion | flops 6340608 | bytes 9510912 | tf_op jit(solution)/shard_map/convert_element_type | solution.py:24
  35.2 6.4 %fusion.4 = bf16[3,2048,256]{2,1,0:T(8,128)(2,1)S(1)} fusion(f32[3,2048,258]{2,1,0:T(8,128)S(1)} %maximum_convert_fusion, f32[3,2048]{1,0:T(4,128)S(1)} %get-tuple-element.36, f32[3,2048]{1,0:T(4,128)S(1)} %get-tuple-element.37, f32[3,2048]{1,0:T(4,128)S(1)} %bitcast.75), kind=kLoop, calls=%fused_computation.8 | loop fusion | flops 9437184 | bytes 22093824 | tf_op jit(solution)/shard_map/convert_element_type | solution.py:350
  42.9 7.5 %all-to-all-start = ((bf16[32,64,256]{2,1,0:T(8,128)(2,1)}), bf16[32,64,256]{2,1,0:T(8,128)(2,1)}, u32[]{:S(2)}, u32[]{:S(2)}) async-start(bf16[32,64,256]{2,1,0:T(8,128)(2,1)} %bitcast.70), calls=%async_computation | async-start | bytes 2097152 | tf_op jit(solution)/shard_map/all_to_all | solution.py:361
  57.7 20.6 %all-to-all-done = bf16[32,64,256]{2,1,0:T(8,128)(2,1)} async-done(((bf16[32,64,256]{2,1,0:T(8,128)(2,1)}), bf16[32,64,256]{2,1,0:T(8,128)(2,1)}, u32[]{:S(2)}, u32[]{:S(2)}) %all-to-all-start) | async-done | bytes 1048608 | tf_op jit(solution)/shard_map/all_to_all | solution.py:361
  78.3 4.6 %all-to-all-start.2 = ((bf16[32,64,256]{2,1,0:T(8,128)(2,1)}), bf16[32,64,256]{2,1,0:T(8,128)(2,1)}, u32[]{:S(2)}, u32[]{:S(2)}) async-start(bf16[32,64,256]{2,1,0:T(8,128)(2,1)} %multiply_convert_fusion), calls=%async_computation.2 | async-start | bytes 2097152 | tf_op jit(solution)/shard_map/all_to_all | solution.py:362
  82.9 2.8 %copy.132 = bf16[32,64,256]{2,0,1:T(8,128)(2,1)} copy(bf16[32,64,256]{2,1,0:T(8,128)(2,1)} %all-to-all-done) | data formatting | bytes 2097152 | tf_op jit(solution)/shard_map/all_to_all | solution.py:361
  85.7 11.3 %shard_map.93 = bf16[64,32,256]{2,1,0:T(8,128)(2,1)} custom-call(bf16[64,32,256]{2,1,0:T(8,128)(2,1)} %bitcast.71, f32[64,2,256]{2,1,0:T(2,128)} %pad_maximum_fusion.2.refs_1_.refs_2_, bf16[64,8,16,256]{3,2,1,0:T(8,128)(2,1)} %fusion.16.refs_2_.refs_3_, f32[64,8,16]{2,1,0:T(8,128)} %stack.62.refs_3_.refs_4_), custom_call_target="tpu_custom_call" | custom-call | flops 40265318400 | bytes 6291456 | tf_op jit(solution)/shard_map/pallas_call | solution.py:283
  97.0 2.8 %copy.113 = bf16[64,32,256]{2,0,1:T(8,128)(2,1)} copy(bf16[64,32,256]{2,1,0:T(8,128)(2,1)} %shard_map.93) | data formatting | bytes 2097152 | tf_op jit(solution)/shard_map/pallas_call | solution.py:283
  99.8 11.0 %all-to-all-done.2 = bf16[32,64,256]{2,1,0:T(8,128)(2,1)} async-done(((bf16[32,64,256]{2,1,0:T(8,128)(2,1)}), bf16[32,64,256]{2,1,0:T(8,128)(2,1)}, u32[]{:S(2)}, u32[]{:S(2)}) %all-to-all-start.2) | async-done | bytes 1048608 | tf_op jit(solution)/shard_map/all_to_all | solution.py:362
  110.9 4.6 %all-to-all-start.1 = ((bf16[64,32,256]{2,0,1:T(8,128)(2,1)}), bf16[64,32,256]{2,0,1:T(8,128)(2,1)}, u32[]{:S(2)}, u32[]{:S(2)}) async-start(bf16[64,32,256]{2,0,1:T(8,128)(2,1)} %copy.113), calls=%async_computation.1 | async-start | bytes 2097152 | tf_op jit(solution)/shard_map/all_to_all | solution.py:384
  115.5 2.8 %copy.131 = bf16[32,64,256]{2,0,1:T(8,128)(2,1)} copy(bf16[32,64,256]{2,1,0:T(8,128)(2,1)} %all-to-all-done.2) | data formatting | bytes 2097152 | tf_op jit(solution)/shard_map/all_to_all | solution.py:362
  118.2 23.3 %shard_map.94 = (bf16[64,32,256]{2,1,0:T(8,128)(2,1)}, f32[64,1,16]{2,1,0:T(1,128)}, f32[64,1,128]{2,1,0:T(1,128)}) custom-call(bf16[64,32,256]{2,1,0:T(8,128)(2,1)} %bitcast.72, bf16[64,32,256]{2,1,0:T(8,128)(2,1)} %bitcast.73, f32[64,2,256]{2,1,0:T(2,128)} %pad_maximum_fusion.2.refs_1_.refs_2_, bf16[64,8,16,256]{3,2,1,0:T(8,128)(2,1)} %fusion.16.refs_2_.refs_3_, ...), custom_call_target="tpu_custom_call" | custom-call | flops 67108864000 | bytes 7340032 | tf_op jit(solution)/shard_map/pallas_call | solution.py:294
  141.6 2.8 %copy.115 = bf16[64,32,256]{2,0,1:T(8,128)(2,1)} copy(bf16[64,32,256]{2,1,0:T(8,128)(2,1)} %get-tuple-element.7) | data formatting | bytes 2097152 | tf_op jit(solution)/shard_map/pallas_call | solution.py:294
  144.4 7.9 %all-to-all-start.3 = ((bf16[64,32,256]{2,0,1:T(8,128)(2,1)}), bf16[64,32,256]{2,0,1:T(8,128)(2,1)}, u32[]{:S(2)}, u32[]{:S(2)}) async-start(bf16[64,32,256]{2,0,1:T(8,128)(2,1)} %copy.115), calls=%async_computation.3 | async-start | bytes 2097152 | tf_op jit(solution)/shard_map/all_to_all | solution.py:385
  155.9 2.9 %collective-permute-start.4 = (f32[64,17]{0,1:T(8,128)S(1)}, f32[64,17]{0,1:T(8,128)S(1)}, u32[]{:S(2)}, u32[]{:S(2)}) collective-permute-start(f32[64,17]{0,1:T(8,128)S(1)} %fusion.24), channel_id=1, source_target_pairs={{0,128},{64,192},{128,0},{192,64},{1,129},{65,193},{129,1},{193,65... | collective-permute-start | bytes 13064 | tf_op jit(solution)/shard_map/ppermute | solution.py:396
  160.2 2.0 collective-permute-start.5
  164.8 4.8 %collective-permute-done.6 = f32[128,17]{0,1:T(8,128)S(1)} collective-permute-done((f32[128,17]{0,1:T(8,128)S(1)}, f32[128,17]{0,1:T(8,128)S(1)}, u32[]{:S(2)}, u32[]{:S(2)}) %collective-permute-start.6) | collective-permute-done | bytes 8736 | tf_op jit(solution)/shard_map/ppermute | solution.py:406
  169.6 4.2 %collective-permute-start.7 = (f32[256,17]{0,1:T(8,128)S(1)}, f32[256,17]{0,1:T(8,128)S(1)}, u32[]{:S(2)}, u32[]{:S(2)}) collective-permute-start(f32[256,17]{0,1:T(8,128)S(1)} %maximum_select_fusion.3), channel_id=1, source_target_pairs={{0,8},{2,10},{4,12},{6,14},{8,0},{10,2},{12,4},{14,6},{16,24},{18,... | collective-permute-start | bytes 52232 | tf_op jit(solution)/shard_map/ppermute | solution.py:406
  173.8 4.8 %collective-permute-done.7 = f32[256,17]{0,1:T(8,128)S(1)} collective-permute-done((f32[256,17]{0,1:T(8,128)S(1)}, f32[256,17]{0,1:T(8,128)S(1)}, u32[]{:S(2)}, u32[]{:S(2)}) %collective-permute-start.7) | collective-permute-done | bytes 17440 | tf_op jit(solution)/shard_map/ppermute | solution.py:406
  179.8 1.8 collective-permute-done.8
  181.6 2.8 %collective-permute-start.9 = (f32[1024,17]{0,1:T(8,128)S(1)}, f32[1024,17]{0,1:T(8,128)S(1)}, u32[]{:S(2)}, u32[]{:S(2)}) collective-permute-start(f32[1024,17]{0,1:T(8,128)S(1)} %maximum_select_fusion.1), channel_id=1, source_target_pairs={{0,32},{2,34},{4,36},{6,38},{8,40},{10,42},{12,44},{14,46},{16,48}... | collective-permute-start | bytes 208904 | tf_op jit(solution)/shard_map/ppermute | solution.py:406
  184.4 3.7 %fusion.9 = (bf16[1,2048,256]{2,1,0:T(8,128)(2,1)S(1)}, bf16[1,2048,256]{2,1,0:T(8,128)(2,1)S(1)}, bf16[1,2048,256]{2,1,0:T(8,128)(2,1)}, bf16[1,2048,256]{2,1,0:T(8,128)(2,1)S(1)}) fusion(bf16[64,32,256]{2,0,1:T(8,128)(2,1)} %all-to-all-done.3, bf16[3,2048,256]{2,1,0:T(8,128)(2,1)S(1)} %fusion.4, bf16[64,32,256]{2,0,1:T(8,128)(2,1)} %all-to-all-done.1, ...), kind=kLoop, calls=%fused_computation.20 | loop fusion | flops 8912896 | bytes 10485760 | tf_op jit(solution)/shard_map/convert.6
  191.2 1.9 copy.116
  193.0 4.5 %collective-permute-start.2 = (bf16[3,2048,2]{1,2,0:T(2,128)(2,1)S(1)}, bf16[3,2048,2]{1,2,0:T(2,128)(2,1)S(1)}, u32[]{:S(2)}, u32[]{:S(2)}) collective-permute-start(bf16[3,2048,2]{1,2,0:T(2,128)(2,1)S(1)} %copy.116), channel_id=1, source_target_pairs={{2,0},{4,2},{6,4},{8,6},{10,8},{12,10},{14,12},{16,14},{18,16},{20... | collective-permute-start | bytes 73736 | tf_op jit(solution)/shard_map/ppermute | solution.py:18
  200.4 2.6 %maximum_convert_fusion.1 = f32[3,2048,258]{2,1,0:T(8,128)S(1)} fusion(bf16[3,2048,2]{2,1,0:T(8,128)(2,1)} %copy.117, bf16[1,2048,256]{2,1,0:T(8,128)(2,1)S(1)} %copy-done.3, bf16[1,2048,256]{2,1,0:T(8,128)(2,1)S(1)} %copy-done.1, bf16[1,2048,256]{2,1,0:T(8,128)(2,1)S(1)} %copy-done.5), kind=kLoop, calls=%fused_computation.13 | loop fusion | flops 12681216 | bytes 9510912 | tf_op jit(solution)/shard_map/convert_element_type | solution.py:38
  203.0 7.3 %fusion.6 = bf16[1,3,2048,256]{3,2,1,0:T(8,128)(2,1)} fusion(f32[3,2048,258]{2,1,0:T(8,128)S(1)} %maximum_convert_fusion.1, f32[3,2048]{1,0:T(4,128)S(1)} %get-tuple-element.36, f32[3,2048]{1,0:T(4,128)S(1)} %get-tuple-element.37, f32[3,2048]{1,0:T(4,128)S(1)} %bitcast.76), kind=kLoop, calls=%fused_computation.14 | loop fusion | flops 9437184 | bytes 22093824 | tf_op jit(solution)/shard_map/broadcast_in_dim | solution.py:428
  (81 shorter events, 35.5 us)
Async XLA Ops:
  3.9 28.0 %copy-start.6 = (bf16[1,3,2048,256]{3,2,1,0:T(8,128)(2,1)S(1)}, bf16[1,3,2048,256]{3,2,1,0:T(8,128)(2,1)}, u32[]{:S(2)}) copy-start(bf16[1,3,2048,256]{3,2,1,0:T(8,128)(2,1)} %param.6) | copy-start | bytes 9437188
  3.9 25.8 %collective-permute-start = (bf16[3,2048,2]{1,2,0:T(2,128)(2,1)}, bf16[3,2048,2]{1,2,0:T(2,128)(2,1)}, u32[]{:S(2)}, u32[]{:S(2)}) collective-permute-start(bf16[3,2048,2]{1,2,0:T(2,128)(2,1)} %copy.100), channel_id=1, source_target_pairs={{0,2},{2,4},{4,6},{6,8},{8,10},{10,12},{12,14},{14,16},{16,18},{18... | collective-permute-start | bytes 73736 | tf_op jit(solution)/shard_map/ppermute | solution.py:18
  11.0 43.0 %collective-permute-start.1 = (bf16[2048,128]{1,0:T(8,128)(2,1)}, bf16[2048,128]{1,0:T(8,128)(2,1)}, u32[]{:S(2)}, u32[]{:S(2)}) collective-permute-start(bf16[2048,128]{1,0:T(8,128)(2,1)} %dynamic-slice_bitcast_fusion), channel_id=1, source_target_pairs={{0,1},{1,0},{2,3},{3,2},{4,5},{5,4},{6,7},{7,6},{8,9},{9,8},{10,11... | collective-permute-start | bytes 1572872 | tf_op jit(solution)/shard_map/ppermute | solution.py:340
  42.9 35.4 %all-to-all-start = ((bf16[32,64,256]{2,1,0:T(8,128)(2,1)}), bf16[32,64,256]{2,1,0:T(8,128)(2,1)}, u32[]{:S(2)}, u32[]{:S(2)}) async-start(bf16[32,64,256]{2,1,0:T(8,128)(2,1)} %bitcast.70), calls=%async_computation | async-start | bytes 2097152 | tf_op jit(solution)/shard_map/all_to_all | solution.py:361
  50.4 3.7 %copy-start.9 = (bf16[1,4096,128]{2,1,0:T(8,128)(2,1)S(1)}, bf16[1,4096,128]{2,1,0:T(8,128)(2,1)}, u32[]{:S(2)}) copy-start(bf16[1,4096,128]{2,1,0:T(8,128)(2,1)} %param.7) | copy-start | bytes 3145732
  55.3 0.8 copy-start.7
  55.3 1.1 copy-start.8
  78.3 32.6 %all-to-all-start.2 = ((bf16[32,64,256]{2,1,0:T(8,128)(2,1)}), bf16[32,64,256]{2,1,0:T(8,128)(2,1)}, u32[]{:S(2)}, u32[]{:S(2)}) async-start(bf16[32,64,256]{2,1,0:T(8,128)(2,1)} %multiply_convert_fusion), calls=%async_computation.2 | async-start | bytes 2097152 | tf_op jit(solution)/shard_map/all_to_all | solution.py:362
  110.9 33.5 %all-to-all-start.1 = ((bf16[64,32,256]{2,0,1:T(8,128)(2,1)}), bf16[64,32,256]{2,0,1:T(8,128)(2,1)}, u32[]{:S(2)}, u32[]{:S(2)}) async-start(bf16[64,32,256]{2,0,1:T(8,128)(2,1)} %copy.113), calls=%async_computation.1 | async-start | bytes 2097152 | tf_op jit(solution)/shard_map/all_to_all | solution.py:384
  141.5 10.7 %copy-start.10 = (f32[64,1,16]{2,1,0:T(1,128)S(1)}, f32[64,1,16]{2,1,0:T(1,128)}, u32[]{:S(2)}) copy-start(f32[64,1,16]{2,1,0:T(1,128)} %get-tuple-element.8) | copy-start | bytes 12292
  141.6 10.8 %copy-start.11 = (f32[64,1,128]{2,1,0:T(1,128)S(1)}, f32[64,1,128]{2,1,0:T(1,128)}, u32[]{:S(2)}) copy-start(f32[64,1,128]{2,1,0:T(1,128)} %get-tuple-element.9) | copy-start | bytes 98308
  144.4 40.0 %all-to-all-start.3 = ((bf16[64,32,256]{2,0,1:T(8,128)(2,1)}), bf16[64,32,256]{2,0,1:T(8,128)(2,1)}, u32[]{:S(2)}, u32[]{:S(2)}) async-start(bf16[64,32,256]{2,0,1:T(8,128)(2,1)} %copy.115), calls=%async_computation.3 | async-start | bytes 2097152 | tf_op jit(solution)/shard_map/all_to_all | solution.py:385
  152.9 3.0 %collective-permute-start.3 = (f32[64,17]{0,1:T(8,128)S(1)}, f32[64,17]{0,1:T(8,128)S(1)}, u32[]{:S(2)}, u32[]{:S(2)}) collective-permute-start(f32[64,17]{0,1:T(8,128)S(1)} %pad_maximum_fusion.3), channel_id=1, source_target_pairs={{0,64},{64,0},{128,192},{192,128},{1,65},{65,1},{129,193},{193,129... | collective-permute-start | bytes 13064 | tf_op jit(solution)/shard_map/ppermute | solution.py:396
  155.9 4.3 %collective-permute-start.4 = (f32[64,17]{0,1:T(8,128)S(1)}, f32[64,17]{0,1:T(8,128)S(1)}, u32[]{:S(2)}, u32[]{:S(2)}) collective-permute-start(f32[64,17]{0,1:T(8,128)S(1)} %fusion.24), channel_id=1, source_target_pairs={{0,128},{64,192},{128,0},{192,64},{1,129},{65,193},{129,1},{193,65... | collective-permute-start | bytes 13064 | tf_op jit(solution)/shard_map/ppermute | solution.py:396
  160.2 2.8 %collective-permute-start.5 = (f32[64,17]{0,1:T(8,128)S(1)}, f32[64,17]{0,1:T(8,128)S(1)}, u32[]{:S(2)}, u32[]{:S(2)}) collective-permute-start(f32[64,17]{0,1:T(8,128)S(1)} %add.49), channel_id=1, source_target_pairs={{0,2},{2,0},{4,6},{6,4},{8,10},{10,8},{12,14},{14,12},{16,18},{18,... | collective-permute-start | bytes 13064 | tf_op jit(solution)/shard_map/ppermute | solution.py:406
  163.1 6.5 %collective-permute-start.6 = (f32[128,17]{0,1:T(8,128)S(1)}, f32[128,17]{0,1:T(8,128)S(1)}, u32[]{:S(2)}, u32[]{:S(2)}) collective-permute-start(f32[128,17]{0,1:T(8,128)S(1)} %maximum_select_fusion.4), channel_id=1, source_target_pairs={{0,4},{2,6},{4,0},{6,2},{8,12},{10,14},{12,8},{14,10},{16,20},{18,... | collective-permute-start | bytes 26120 | tf_op jit(solution)/shard_map/ppermute | solution.py:406
  169.6 8.9 %collective-permute-start.7 = (f32[256,17]{0,1:T(8,128)S(1)}, f32[256,17]{0,1:T(8,128)S(1)}, u32[]{:S(2)}, u32[]{:S(2)}) collective-permute-start(f32[256,17]{0,1:T(8,128)S(1)} %maximum_select_fusion.3), channel_id=1, source_target_pairs={{0,8},{2,10},{4,12},{6,14},{8,0},{10,2},{12,4},{14,6},{16,24},{18,... | collective-permute-start | bytes 52232 | tf_op jit(solution)/shard_map/ppermute | solution.py:406
  178.5 3.0 %collective-permute-start.8 = (f32[512,17]{0,1:T(8,128)S(1)}, f32[512,17]{0,1:T(8,128)S(1)}, u32[]{:S(2)}, u32[]{:S(2)}) collective-permute-start(f32[512,17]{0,1:T(8,128)S(1)} %maximum_select_fusion.2), channel_id=1, source_target_pairs={{0,16},{2,18},{4,20},{6,22},{8,24},{10,26},{12,28},{14,30},{16,0},... | collective-permute-start | bytes 104456 | tf_op jit(solution)/shard_map/ppermute | solution.py:406
  181.6 16.0 %collective-permute-start.9 = (f32[1024,17]{0,1:T(8,128)S(1)}, f32[1024,17]{0,1:T(8,128)S(1)}, u32[]{:S(2)}, u32[]{:S(2)}) collective-permute-start(f32[1024,17]{0,1:T(8,128)S(1)} %maximum_select_fusion.1), channel_id=1, source_target_pairs={{0,32},{2,34},{4,36},{6,38},{8,40},{10,42},{12,44},{14,46},{16,48}... | collective-permute-start | bytes 208904 | tf_op jit(solution)/shard_map/ppermute | solution.py:406
  188.1 1.0 copy-start
  188.1 1.3 copy-start.2
  188.1 1.6 copy-start.4
  191.1 9.3 %copy-start.1 = (bf16[1,2048,256]{2,1,0:T(8,128)(2,1)S(1)}, bf16[1,2048,256]{2,1,0:T(8,128)(2,1)}, u32[]{:S(2)}) copy-start(bf16[1,2048,256]{2,1,0:T(8,128)(2,1)} %copy-done) | copy-start | bytes 3145732
  191.2 9.3 %copy-start.3 = (bf16[1,2048,256]{2,1,0:T(8,128)(2,1)S(1)}, bf16[1,2048,256]{2,1,0:T(8,128)(2,1)}, u32[]{:S(2)}) copy-start(bf16[1,2048,256]{2,1,0:T(8,128)(2,1)} %copy-done.2) | copy-start | bytes 3145732
  191.2 9.3 %copy-start.5 = (bf16[1,2048,256]{2,1,0:T(8,128)(2,1)S(1)}, bf16[1,2048,256]{2,1,0:T(8,128)(2,1)}, u32[]{:S(2)}) copy-start(bf16[1,2048,256]{2,1,0:T(8,128)(2,1)} %copy-done.4) | copy-start | bytes 3145732
  193.0 5.8 %collective-permute-start.2 = (bf16[3,2048,2]{1,2,0:T(2,128)(2,1)S(1)}, bf16[3,2048,2]{1,2,0:T(2,128)(2,1)S(1)}, u32[]{:S(2)}, u32[]{:S(2)}) collective-permute-start(bf16[3,2048,2]{1,2,0:T(2,128)(2,1)S(1)} %copy.116), channel_id=1, source_target_pairs={{2,0},{4,2},{6,4},{8,6},{10,8},{12,10},{14,12},{16,14},{18,16},{20... | collective-permute-start | bytes 73736 | tf_op jit(solution)/shard_map/ppermute | solution.py:18

commit v10 on v9

--- a/solution.py
+++ b/solution.py
@@ -366,6 +366,9 @@
     rate_rows = lax.dynamic_slice_in_dim(decay_rate, chan_start, chan_count, 0)
     weight_rows = lax.dynamic_slice_in_dim(weight_all, chan_start, chan_count, 0)
     gain_rows = lax.dynamic_slice_in_dim(skip_gain, chan_start, chan_count, 0)
+    rate_rows, weight_rows, gain_rows, product_all = lax.optimization_barrier(
+        (rate_rows, weight_rows, gain_rows, product_all)
+    )
     length = product_all.shape[1]
     block_len = math.gcd(256, length)
     block_count = length // block_len

time: 211 us -> 221 us (1.047)
  waiting for transfers between devices: 46.8 us -> 55.4 us
  other arithmetic: 41.1 us -> 34.7 us
  starting transfers between devices: 56.4 us -> 61.4 us
    ppermute x1, waiting for transfers between devices: 0.01 us -> 36.7 us  [on_device(): theirs = lax.ppermute(other, 'tp', [(0, 1), (1, 0)])]
    all_to_all x1, waiting for transfers between devices: 20.6 us -> 0.56 us  [on_device(): lax.all_to_all(product, 'ctx', split_axis=0, concat_axis=1, tiled=True)]
    all_to_all x1, waiting for transfers between devices: 11 us -> 1.95 us  [on_device(): lax.all_to_all(adjoint, 'ctx', split_axis=0, concat_axis=1, tiled=True)]
    unnamed x7, other arithmetic: 7.91 us -> 1.95 us
    unnamed x27 -> x37, local copies, waits for them, and re-layouts: 2.85 us -> 6.34 us
    all_to_all x1, starting transfers between devices: 4.64 us -> 7.53 us  [on_device(): lax.all_to_all(adjoint, 'ctx', split_axis=0, concat_axis=1, tiled=True)]
  transfers between devices with their start and end apart: 14 -> 14, of which waited for: 8 -> 10; matrix products, arithmetic and copies ran while one was open for 26% -> 16% of each run, Pallas kernels for 16% -> 16%
where the time goes in v10:
time: 221 us; the launch traced here: 220 us
  starting transfers between devices  61.4 us (28%)
  waiting for transfers between devices  55.4 us (25%)
  other arithmetic  34.7 us (16%)
  Pallas kernels  34.6 us (16%)
  local copies, waits for them, and re-layouts  32.6 us (15%)
    ppermute x1, waiting for transfers between devices, on_device(): theirs = lax.ppermute(other, 'tp', [(0, 1), (1, 0)])  36.7 us
    pallas_call x1, Pallas kernels, long_conv(): pl.pallas_call(partial(long_conv_kernel, True), grid=(chan_count // step,...  23.3 us
    ppermute x5, waiting for transfers between devices, on_device(): theirs = lax.ppermute(gathered, 'ctx', partners)  12.4 us
    ppermute x5, starting transfers between devices, on_device(): theirs = lax.ppermute(gathered, 'ctx', partners)  11.7 us
    pallas_call x1, Pallas kernels, long_conv(): pl.pallas_call(partial(long_conv_kernel, False), grid=(chan_count // step...  11.3 us
    ppermute x2, starting transfers between devices, from_behind(): return lax.ppermute(shard, axis, pairs)  9.44 us
    all_to_all x1, starting transfers between devices, on_device(): lax.all_to_all(product, 'ctx', split_axis=0, concat_axis=1, tiled=True)  9.35 us
    all_to_all x1, starting transfers between devices, on_device(): lax.all_to_all(back_rows, 'ctx', split_axis=1, concat_axis=0, tiled=True)  7.75 us
  transfers between devices with their start and end apart: 14, of which 10 were waited for; matrix products, arithmetic and copies ran while one was open for 16% of the time, Pallas kernels for 16%

profile of v10, /device:TPU:1, one launch (start us, length us, event | category | flops | bytes accessed | tf_op | source)
XLA Modules:
  0.0 219.7 jit_solution(17658811412006095114)
XLA Ops:
  0.7 3.2 %slice.71 = bf16[3,2048,2]{2,1,0:T(8,128)(2,1)} slice(bf16[3,2048,256]{2,1,0:T(8,128)(2,1)} %bitcast.66), slice={[0:3], [0:2048], [254:256]} | slice | bytes 49152 | tf_op jit(solution)/shard_map/slice | solution.py:348
  3.9 1.7 copy.63
  5.6 4.9 %collective-permute-start = (bf16[3,2048,2]{1,2,0:T(2,128)(2,1)S(1)}, bf16[3,2048,2]{1,2,0:T(2,128)(2,1)S(1)}, u32[]{:S(2)}, u32[]{:S(2)}) collective-permute-start(bf16[3,2048,2]{1,2,0:T(2,128)(2,1)S(1)} %copy.63), channel_id=1, source_target_pairs={{0,2},{2,4},{4,6},{6,8},{8,10},{10,12},{12,14},{14,16},{16,18},{18... | collective-permute-start | bytes 73736 | tf_op jit(solution)/shard_map/ppermute | solution.py:18
  13.0 3.3 %maximum_convert_fusion = f32[3,2048,258]{2,1,0:T(8,128)S(1)} fusion(bf16[3,2048,256]{2,1,0:T(8,128)(2,1)S(1)} %bitcast.67, bf16[3,2048,2]{2,1,0:T(8,128)(2,1)} %copy.64), kind=kLoop, calls=%fused_computation.12 | loop fusion | flops 6340608 | bytes 9510912 | tf_op jit(solution)/shard_map/convert_element_type | solution.py:24
  16.3 6.4 %fusion.4 = bf16[3,2048,256]{2,1,0:T(8,128)(2,1)S(1)} fusion(f32[3,2048,258]{2,1,0:T(8,128)S(1)} %maximum_convert_fusion, f32[3,2048]{1,0:T(4,128)S(1)} %get-tuple-element.44, f32[3,2048]{1,0:T(4,128)S(1)} %get-tuple-element.45, f32[3,2048]{1,0:T(4,128)S(1)} %bitcast.78), kind=kLoop, calls=%fused_computation.8 | loop fusion | flops 9437184 | bytes 22093824 | tf_op jit(solution)/shard_map/convert_element_type | solution.py:350
  24.0 9.4 %all-to-all-start = ((bf16[32,64,256]{2,1,0:T(8,128)(2,1)}), bf16[32,64,256]{2,1,0:T(8,128)(2,1)}, u32[]{:S(2)}, u32[]{:S(2)}) async-start(bf16[32,64,256]{2,1,0:T(8,128)(2,1)} %bitcast.72), calls=%async_computation | async-start | bytes 2097152 | tf_op jit(solution)/shard_map/all_to_all | solution.py:361
  33.4 1.9 dynamic-slice_bitcast_fusion
  35.2 5.5 %collective-permute-start.1 = (bf16[2048,128]{1,0:T(8,128)(2,1)}, bf16[2048,128]{1,0:T(8,128)(2,1)}, u32[]{:S(2)}, u32[]{:S(2)}) collective-permute-start(bf16[2048,128]{1,0:T(8,128)(2,1)} %dynamic-slice_bitcast_fusion), channel_id=1, source_target_pairs={{0,1},{1,0},{2,3},{3,2},{4,5},{5,4},{6,7},{7,6},{8,9},{9,8},{10,11... | collective-permute-start | bytes 1572872 | tf_op jit(solution)/shard_map/ppermute | solution.py:340
  42.6 36.7 %collective-permute-done.1 = bf16[2048,128]{1,0:T(8,128)(2,1)} collective-permute-done((bf16[2048,128]{1,0:T(8,128)(2,1)}, bf16[2048,128]{1,0:T(8,128)(2,1)}, u32[]{:S(2)}, u32[]{:S(2)}) %collective-permute-start.1) | collective-permute-done | bytes 524320 | tf_op jit(solution)/shard_map/ppermute | solution.py:340
  83.7 7.5 %all-to-all-start.2 = ((bf16[32,64,256]{2,1,0:T(8,128)(2,1)}), bf16[32,64,256]{2,1,0:T(8,128)(2,1)}, u32[]{:S(2)}, u32[]{:S(2)}) async-start(bf16[32,64,256]{2,1,0:T(8,128)(2,1)} %multiply_convert_fusion), calls=%async_computation.2 | async-start | bytes 2097152 | tf_op jit(solution)/shard_map/all_to_all | solution.py:362
  91.3 2.3 %copy.85 = bf16[32,8,8,256]{3,2,0,1:T(8,128)(2,1)} copy(bf16[32,8,8,256]{3,2,1,0:T(8,128)(2,1)} %bitcast.43) | data formatting | bytes 2097152 | tf_op jit(solution)/shard_map/all_to_all | solution.py:361
  95.0 2.5 %copy.86 = bf16[8,8,32,256]{3,2,1,0:T(8,128)(2,1)} copy(bf16[8,8,32,256]{3,1,2,0:T(8,128)(2,1)} %bitcast.73) | data formatting | bytes 2097152
  103.1 11.3 %shard_map.93 = bf16[64,32,256]{2,1,0:T(8,128)(2,1)} custom-call(bf16[64,32,256]{2,1,0:T(8,128)(2,1)} %bitcast.74, f32[64,2,256]{2,1,0:T(2,128)} %pad_maximum_fusion.2.refs_1_.refs_2_, bf16[64,8,16,256]{3,2,1,0:T(8,128)(2,1)} %copy-done.13, f32[64,8,16]{2,1,0:T(8,128)} %stack.62.refs_3_.refs_4_), custom_call_target="tpu_custom_call" | custom-call | flops 40265318400 | bytes 6291456 | tf_op jit(solution)/shard_map/pallas_call | solution.py:283
  114.5 2.8 %copy.75 = bf16[64,32,256]{2,0,1:T(8,128)(2,1)} copy(bf16[64,32,256]{2,1,0:T(8,128)(2,1)} %shard_map.93) | data formatting | bytes 2097152 | tf_op jit(solution)/shard_map/pallas_call | solution.py:283
  117.2 1.9 all-to-all-done.2
  119.2 5.8 %all-to-all-start.1 = ((bf16[64,32,256]{2,0,1:T(8,128)(2,1)}), bf16[64,32,256]{2,0,1:T(8,128)(2,1)}, u32[]{:S(2)}, u32[]{:S(2)}) async-start(bf16[64,32,256]{2,0,1:T(8,128)(2,1)} %copy.75), calls=%async_computation.1 | async-start | bytes 2097152 | tf_op jit(solution)/shard_map/all_to_all | solution.py:387
  125.0 2.8 %copy.91 = bf16[32,64,256]{2,0,1:T(8,128)(2,1)} copy(bf16[32,64,256]{2,1,0:T(8,128)(2,1)} %all-to-all-done.2) | data formatting | bytes 2097152 | tf_op jit(solution)/shard_map/all_to_all | solution.py:362
  127.8 23.3 %shard_map.94 = (bf16[64,32,256]{2,1,0:T(8,128)(2,1)}, f32[64,1,16]{2,1,0:T(1,128)}, f32[64,1,128]{2,1,0:T(1,128)}) custom-call(bf16[64,32,256]{2,1,0:T(8,128)(2,1)} %bitcast.75, bf16[64,32,256]{2,1,0:T(8,128)(2,1)} %bitcast.76, f32[64,2,256]{2,1,0:T(2,128)} %pad_maximum_fusion.2.refs_1_.refs_2_, bf16[64,8,16,256]{3,2,1,0:T(8,128)(2,1)} %copy-done.13, ...), custom_call_target="tpu_custom_call" | custom-call | flops 67108864000 | bytes 7340032 | tf_op jit(solution)/shard_map/pallas_call | solution.py:294
  151.1 2.8 %copy.77 = bf16[64,32,256]{2,0,1:T(8,128)(2,1)} copy(bf16[64,32,256]{2,1,0:T(8,128)(2,1)} %get-tuple-element.15) | data formatting | bytes 2097152 | tf_op jit(solution)/shard_map/pallas_call | solution.py:294
  153.9 7.7 %all-to-all-start.3 = ((bf16[64,32,256]{2,0,1:T(8,128)(2,1)}), bf16[64,32,256]{2,0,1:T(8,128)(2,1)}, u32[]{:S(2)}, u32[]{:S(2)}) async-start(bf16[64,32,256]{2,0,1:T(8,128)(2,1)} %copy.77), calls=%async_computation.3 | async-start | bytes 2097152 | tf_op jit(solution)/shard_map/all_to_all | solution.py:388
  165.3 2.9 %collective-permute-start.4 = (f32[64,17]{0,1:T(8,128)S(1)}, f32[64,17]{0,1:T(8,128)S(1)}, u32[]{:S(2)}, u32[]{:S(2)}) collective-permute-start(f32[64,17]{0,1:T(8,128)S(1)} %fusion.24), channel_id=1, source_target_pairs={{0,128},{64,192},{128,0},{192,64},{1,129},{65,193},{129,1},{193,65... | collective-permute-start | bytes 13064 | tf_op jit(solution)/shard_map/ppermute | solution.py:399
  169.6 2.0 collective-permute-start.5
  174.0 5.0 %collective-permute-done.6 = f32[128,17]{0,1:T(8,128)S(1)} collective-permute-done((f32[128,17]{0,1:T(8,128)S(1)}, f32[128,17]{0,1:T(8,128)S(1)}, u32[]{:S(2)}, u32[]{:S(2)}) %collective-permute-start.6) | collective-permute-done | bytes 8736 | tf_op jit(solution)/shard_map/ppermute | solution.py:409
  179.0 4.2 %collective-permute-start.7 = (f32[256,17]{0,1:T(8,128)S(1)}, f32[256,17]{0,1:T(8,128)S(1)}, u32[]{:S(2)}, u32[]{:S(2)}) collective-permute-start(f32[256,17]{0,1:T(8,128)S(1)} %maximum_select_fusion.3), channel_id=1, source_target_pairs={{0,8},{2,10},{4,12},{6,14},{8,0},{10,2},{12,4},{14,6},{16,24},{18,... | collective-permute-start | bytes 52232 | tf_op jit(solution)/shard_map/ppermute | solution.py:409
  183.2 4.8 %collective-permute-done.7 = f32[256,17]{0,1:T(8,128)S(1)} collective-permute-done((f32[256,17]{0,1:T(8,128)S(1)}, f32[256,17]{0,1:T(8,128)S(1)}, u32[]{:S(2)}, u32[]{:S(2)}) %collective-permute-start.7) | collective-permute-done | bytes 17440 | tf_op jit(solution)/shard_map/ppermute | solution.py:409
  189.2 1.8 collective-permute-done.8
  191.0 2.8 %collective-permute-start.9 = (f32[1024,17]{0,1:T(8,128)S(1)}, f32[1024,17]{0,1:T(8,128)S(1)}, u32[]{:S(2)}, u32[]{:S(2)}) collective-permute-start(f32[1024,17]{0,1:T(8,128)S(1)} %maximum_select_fusion.1), channel_id=1, source_target_pairs={{0,32},{2,34},{4,36},{6,38},{8,40},{10,42},{12,44},{14,46},{16,48}... | collective-permute-start | bytes 208904 | tf_op jit(solution)/shard_map/ppermute | solution.py:409
  193.8 3.7 %fusion.9 = (bf16[1,2048,256]{2,1,0:T(8,128)(2,1)S(1)}, bf16[1,2048,256]{2,1,0:T(8,128)(2,1)S(1)}, bf16[1,2048,256]{2,1,0:T(8,128)(2,1)}, bf16[1,2048,256]{2,1,0:T(8,128)(2,1)S(1)}) fusion(bf16[64,32,256]{2,0,1:T(8,128)(2,1)} %all-to-all-done.3, bf16[3,2048,256]{2,1,0:T(8,128)(2,1)S(1)} %fusion.4, bf16[64,32,256]{2,0,1:T(8,128)(2,1)} %all-to-all-done.1, ...), kind=kLoop, calls=%fused_computation.20 | loop fusion | flops 8912896 | bytes 10485760 | tf_op jit(solution)/shard_map/convert.6
  200.6 1.9 copy.78
  202.4 4.5 %collective-permute-start.2 = (bf16[3,2048,2]{1,2,0:T(2,128)(2,1)S(1)}, bf16[3,2048,2]{1,2,0:T(2,128)(2,1)S(1)}, u32[]{:S(2)}, u32[]{:S(2)}) collective-permute-start(bf16[3,2048,2]{1,2,0:T(2,128)(2,1)S(1)} %copy.78), channel_id=1, source_target_pairs={{2,0},{4,2},{6,4},{8,6},{10,8},{12,10},{14,12},{16,14},{18,16},{20... | collective-permute-start | bytes 73736 | tf_op jit(solution)/shard_map/ppermute | solution.py:18
  209.8 2.6 %maximum_convert_fusion.1 = f32[3,2048,258]{2,1,0:T(8,128)S(1)} fusion(bf16[3,2048,2]{2,1,0:T(8,128)(2,1)} %copy.79, bf16[1,2048,256]{2,1,0:T(8,128)(2,1)S(1)} %copy-done.3, bf16[1,2048,256]{2,1,0:T(8,128)(2,1)S(1)} %copy-done.1, bf16[1,2048,256]{2,1,0:T(8,128)(2,1)S(1)} %copy-done.5), kind=kLoop, calls=%fused_computation.13 | loop fusion | flops 12681216 | bytes 9510912 | tf_op jit(solution)/shard_map/convert_element_type | solution.py:38
  212.4 7.3 %fusion.6 = bf16[1,3,2048,256]{3,2,1,0:T(8,128)(2,1)} fusion(f32[3,2048,258]{2,1,0:T(8,128)S(1)} %maximum_convert_fusion.1, f32[3,2048]{1,0:T(4,128)S(1)} %get-tuple-element.44, f32[3,2048]{1,0:T(4,128)S(1)} %get-tuple-element.45, f32[3,2048]{1,0:T(4,128)S(1)} %bitcast.79), kind=kLoop, calls=%fused_computation.14 | loop fusion | flops 9437184 | bytes 22093824 | tf_op jit(solution)/shard_map/broadcast_in_dim | solution.py:431
  (92 shorter events, 31.6 us)
Async XLA Ops:
  0.6 12.4 %copy-start.6 = (bf16[1,3,2048,256]{3,2,1,0:T(8,128)(2,1)S(1)}, bf16[1,3,2048,256]{3,2,1,0:T(8,128)(2,1)}, u32[]{:S(2)}) copy-start(bf16[1,3,2048,256]{3,2,1,0:T(8,128)(2,1)} %param.6) | copy-start | bytes 9437188
  0.6 9.9 %copy-start.14 = (f32[3,3,2048]{2,1,0:T(4,128)S(1)}, f32[3,3,2048]{2,1,0:T(4,128)}, u32[]{:S(2)}) copy-start(f32[3,3,2048]{2,1,0:T(4,128)} %param.8) | copy-start | bytes 221188
  5.6 5.9 %collective-permute-start = (bf16[3,2048,2]{1,2,0:T(2,128)(2,1)S(1)}, bf16[3,2048,2]{1,2,0:T(2,128)(2,1)S(1)}, u32[]{:S(2)}, u32[]{:S(2)}) collective-permute-start(bf16[3,2048,2]{1,2,0:T(2,128)(2,1)S(1)} %copy.63), channel_id=1, source_target_pairs={{0,2},{2,4},{4,6},{6,8},{8,10},{10,12},{12,14},{14,16},{16,18},{18... | collective-permute-start | bytes 73736 | tf_op jit(solution)/shard_map/ppermute | solution.py:18
  24.0 59.8 %all-to-all-start = ((bf16[32,64,256]{2,1,0:T(8,128)(2,1)}), bf16[32,64,256]{2,1,0:T(8,128)(2,1)}, u32[]{:S(2)}, u32[]{:S(2)}) async-start(bf16[32,64,256]{2,1,0:T(8,128)(2,1)} %bitcast.72), calls=%async_computation | async-start | bytes 2097152 | tf_op jit(solution)/shard_map/all_to_all | solution.py:361
  35.2 44.1 %collective-permute-start.1 = (bf16[2048,128]{1,0:T(8,128)(2,1)}, bf16[2048,128]{1,0:T(8,128)(2,1)}, u32[]{:S(2)}, u32[]{:S(2)}) collective-permute-start(bf16[2048,128]{1,0:T(8,128)(2,1)} %dynamic-slice_bitcast_fusion), channel_id=1, source_target_pairs={{0,1},{1,0},{2,3},{3,2},{4,5},{5,4},{6,7},{7,6},{8,9},{9,8},{10,11... | collective-permute-start | bytes 1572872 | tf_op jit(solution)/shard_map/ppermute | solution.py:340
  80.7 0.8 copy-start.7
  80.7 1.1 copy-start.8
  83.7 35.4 %all-to-all-start.2 = ((bf16[32,64,256]{2,1,0:T(8,128)(2,1)}), bf16[32,64,256]{2,1,0:T(8,128)(2,1)}, u32[]{:S(2)}, u32[]{:S(2)}) async-start(bf16[32,64,256]{2,1,0:T(8,128)(2,1)} %multiply_convert_fusion), calls=%async_computation.2 | async-start | bytes 2097152 | tf_op jit(solution)/shard_map/all_to_all | solution.py:362
  95.0 7.1 %copy-start.9 = (f32[64,16]{1,0:T(8,128)S(1)}, f32[64,16]{1,0:T(8,128)}, u32[]{:S(2)}) copy-start(f32[64,16]{1,0:T(8,128)} %get-tuple-element.39) | copy-start | bytes 12292
  95.0 7.1 %copy-start.10 = (f32[64,16]{1,0:T(8,128)S(1)}, f32[64,16]{1,0:T(8,128)}, u32[]{:S(2)}) copy-start(f32[64,16]{1,0:T(8,128)} %get-tuple-element.40) | copy-start | bytes 12292
  97.5 4.5 %copy-start.11 = (f32[64,16]{1,0:T(8,128)S(1)}, f32[64,16]{1,0:T(8,128)}, u32[]{:S(2)}) copy-start(f32[64,16]{1,0:T(8,128)} %get-tuple-element.41) | copy-start | bytes 12292
  97.5 4.5 %copy-start.12 = (f32[64,16]{1,0:T(8,128)S(1)}, f32[64,16]{1,0:T(8,128)}, u32[]{:S(2)}) copy-start(f32[64,16]{1,0:T(8,128)} %get-tuple-element.42) | copy-start | bytes 12292
  99.9 2.0 copy-start.13
  119.2 34.7 %all-to-all-start.1 = ((bf16[64,32,256]{2,0,1:T(8,128)(2,1)}), bf16[64,32,256]{2,0,1:T(8,128)(2,1)}, u32[]{:S(2)}, u32[]{:S(2)}) async-start(bf16[64,32,256]{2,0,1:T(8,128)(2,1)} %copy.75), calls=%async_computation.1 | async-start | bytes 2097152 | tf_op jit(solution)/shard_map/all_to_all | solution.py:387
  151.1 10.6 %copy-start.15 = (f32[64,1,16]{2,1,0:T(1,128)S(1)}, f32[64,1,16]{2,1,0:T(1,128)}, u32[]{:S(2)}) copy-start(f32[64,1,16]{2,1,0:T(1,128)} %get-tuple-element.16) | copy-start | bytes 12292
  151.1 10.7 %copy-start.16 = (f32[64,1,128]{2,1,0:T(1,128)S(1)}, f32[64,1,128]{2,1,0:T(1,128)}, u32[]{:S(2)}) copy-start(f32[64,1,128]{2,1,0:T(1,128)} %get-tuple-element.17) | copy-start | bytes 98308
  153.9 39.9 %all-to-all-start.3 = ((bf16[64,32,256]{2,0,1:T(8,128)(2,1)}), bf16[64,32,256]{2,0,1:T(8,128)(2,1)}, u32[]{:S(2)}, u32[]{:S(2)}) async-start(bf16[64,32,256]{2,0,1:T(8,128)(2,1)} %copy.77), calls=%async_computation.3 | async-start | bytes 2097152 | tf_op jit(solution)/shard_map/all_to_all | solution.py:388
  162.3 3.0 %collective-permute-start.3 = (f32[64,17]{0,1:T(8,128)S(1)}, f32[64,17]{0,1:T(8,128)S(1)}, u32[]{:S(2)}, u32[]{:S(2)}) collective-permute-start(f32[64,17]{0,1:T(8,128)S(1)} %pad_maximum_fusion.3), channel_id=1, source_target_pairs={{0,64},{64,0},{128,192},{192,128},{1,65},{65,1},{129,193},{193,129... | collective-permute-start | bytes 13064 | tf_op jit(solution)/shard_map/ppermute | solution.py:399
  165.3 4.3 %collective-permute-start.4 = (f32[64,17]{0,1:T(8,128)S(1)}, f32[64,17]{0,1:T(8,128)S(1)}, u32[]{:S(2)}, u32[]{:S(2)}) collective-permute-start(f32[64,17]{0,1:T(8,128)S(1)} %fusion.24), channel_id=1, source_target_pairs={{0,128},{64,192},{128,0},{192,64},{1,129},{65,193},{129,1},{193,65... | collective-permute-start | bytes 13064 | tf_op jit(solution)/shard_map/ppermute | solution.py:399
  169.6 2.8 %collective-permute-start.5 = (f32[64,17]{0,1:T(8,128)S(1)}, f32[64,17]{0,1:T(8,128)S(1)}, u32[]{:S(2)}, u32[]{:S(2)}) collective-permute-start(f32[64,17]{0,1:T(8,128)S(1)} %add.49), channel_id=1, source_target_pairs={{0,2},{2,0},{4,6},{6,4},{8,10},{10,8},{12,14},{14,12},{16,18},{18,... | collective-permute-start | bytes 13064 | tf_op jit(solution)/shard_map/ppermute | solution.py:409
  172.5 6.5 %collective-permute-start.6 = (f32[128,17]{0,1:T(8,128)S(1)}, f32[128,17]{0,1:T(8,128)S(1)}, u32[]{:S(2)}, u32[]{:S(2)}) collective-permute-start(f32[128,17]{0,1:T(8,128)S(1)} %maximum_select_fusion.4), channel_id=1, source_target_pairs={{0,4},{2,6},{4,0},{6,2},{8,12},{10,14},{12,8},{14,10},{16,20},{18,... | collective-permute-start | bytes 26120 | tf_op jit(solution)/shard_map/ppermute | solution.py:409
  179.0 8.9 %collective-permute-start.7 = (f32[256,17]{0,1:T(8,128)S(1)}, f32[256,17]{0,1:T(8,128)S(1)}, u32[]{:S(2)}, u32[]{:S(2)}) collective-permute-start(f32[256,17]{0,1:T(8,128)S(1)} %maximum_select_fusion.3), channel_id=1, source_target_pairs={{0,8},{2,10},{4,12},{6,14},{8,0},{10,2},{12,4},{14,6},{16,24},{18,... | collective-permute-start | bytes 52232 | tf_op jit(solution)/shard_map/ppermute | solution.py:409
  187.9 3.0 %collective-permute-start.8 = (f32[512,17]{0,1:T(8,128)S(1)}, f32[512,17]{0,1:T(8,128)S(1)}, u32[]{:S(2)}, u32[]{:S(2)}) collective-permute-start(f32[512,17]{0,1:T(8,128)S(1)} %maximum_select_fusion.2), channel_id=1, source_target_pairs={{0,16},{2,18},{4,20},{6,22},{8,24},{10,26},{12,28},{14,30},{16,0},... | collective-permute-start | bytes 104456 | tf_op jit(solution)/shard_map/ppermute | solution.py:409
  191.0 16.0 %collective-permute-start.9 = (f32[1024,17]{0,1:T(8,128)S(1)}, f32[1024,17]{0,1:T(8,128)S(1)}, u32[]{:S(2)}, u32[]{:S(2)}) collective-permute-start(f32[1024,17]{0,1:T(8,128)S(1)} %maximum_select_fusion.1), channel_id=1, source_target_pairs={{0,32},{2,34},{4,36},{6,38},{8,40},{10,42},{12,44},{14,46},{16,48}... | collective-permute-start | bytes 208904 | tf_op jit(solution)/shard_map/ppermute | solution.py:409
  197.5 1.0 copy-start
  197.5 1.3 copy-start.2
  197.5 1.6 copy-start.4
  200.5 9.3 %copy-start.1 = (bf16[1,2048,256]{2,1,0:T(8,128)(2,1)S(1)}, bf16[1,2048,256]{2,1,0:T(8,128)(2,1)}, u32[]{:S(2)}) copy-start(bf16[1,2048,256]{2,1,0:T(8,128)(2,1)} %copy-done) | copy-start | bytes 3145732
  200.5 9.3 %copy-start.3 = (bf16[1,2048,256]{2,1,0:T(8,128)(2,1)S(1)}, bf16[1,2048,256]{2,1,0:T(8,128)(2,1)}, u32[]{:S(2)}) copy-start(bf16[1,2048,256]{2,1,0:T(8,128)(2,1)} %copy-done.2) | copy-start | bytes 3145732
  200.6 9.3 %copy-start.5 = (bf16[1,2048,256]{2,1,0:T(8,128)(2,1)S(1)}, bf16[1,2048,256]{2,1,0:T(8,128)(2,1)}, u32[]{:S(2)}) copy-start(bf16[1,2048,256]{2,1,0:T(8,128)(2,1)} %copy-done.4) | copy-start | bytes 3145732
  202.4 5.8 %collective-permute-start.2 = (bf16[3,2048,2]{1,2,0:T(2,128)(2,1)S(1)}, bf16[3,2048,2]{1,2,0:T(2,128)(2,1)S(1)}, u32[]{:S(2)}, u32[]{:S(2)}) collective-permute-start(bf16[3,2048,2]{1,2,0:T(2,128)(2,1)S(1)} %copy.78), channel_id=1, source_target_pairs={{2,0},{4,2},{6,4},{8,6},{10,8},{12,10},{14,12},{16,14},{18,16},{20... | collective-permute-start | bytes 73736 | tf_op jit(solution)/shard_map/ppermute | solution.py:18

commit v11 on v9

--- a/solution.py
+++ b/solution.py
@@ -397,7 +397,7 @@
             hop *= 2
     else:
         local_grads = lax.psum(local_grads, "dp")
-    if ctx_count & (ctx_count - 1) == 0:
+    if False:
         ctx_index = lax.axis_index("ctx")
         gathered = local_grads
         hop = 1

time: 211 us -> 218 us (1.033); the launches traced: 210 us -> 214 us
  starting transfers between devices: 56.4 us -> 46.3 us
  waiting for transfers between devices: 46.8 us -> 53.7 us
  local copies, waits for them, and re-layouts: 30.4 us -> 36 us
    all_to_all x1, waiting for transfers between devices: 0.01 us -> 19 us  [on_device(): lax.all_to_all(back_rows, 'ctx', split_axis=1, concat_axis=0, tiled=True)]
    ppermute x5 -> x0, waiting for transfers between devices: 12.2 us -> none  [on_device(): theirs = lax.ppermute(gathered, 'ctx', partners)]
    ppermute x5 -> x0, starting transfers between devices: 11.9 us -> none  [on_device(): theirs = lax.ppermute(gathered, 'ctx', partners)]
    all_to_all x0 -> x1, starting transfers between devices: none -> 3.88 us  [on_device(): lax.all_to_all(spread, 'ctx', split_axis=0, concat_axis=0, tiled=True)]
    unnamed x27 -> x42, local copies, waits for them, and re-layouts: 2.85 us -> 4.76 us
  transfers between devices with their start and end apart: 14 -> 10, of which waited for: 8 -> 5; matrix products, arithmetic and copies ran while one was open for 26% -> 28% of each run, Pallas kernels for 16% -> 16%
where the time goes in v11:
time: 218 us; the launch traced here: 214 us
  waiting for transfers between devices  53.7 us (25%)
  starting transfers between devices  46.3 us (21%)
  other arithmetic  42.7 us (20%)
  local copies, waits for them, and re-layouts  36 us (17%)
  Pallas kernels  34.6 us (16%)
    pallas_call x1, Pallas kernels, long_conv(): pl.pallas_call(partial(long_conv_kernel, True), grid=(chan_count // step,...  23.3 us
    all_to_all x1, waiting for transfers between devices, on_device(): lax.all_to_all(product, 'ctx', split_axis=0, concat_axis=1, tiled=True)  20.6 us
    all_to_all x1, waiting for transfers between devices, on_device(): lax.all_to_all(back_rows, 'ctx', split_axis=1, concat_axis=0, tiled=True)  19 us
    pallas_call x1, Pallas kernels, long_conv(): pl.pallas_call(partial(long_conv_kernel, False), grid=(chan_count // step...  11.3 us
    all_to_all x1, waiting for transfers between devices, on_device(): lax.all_to_all(adjoint, 'ctx', split_axis=0, concat_axis=1, tiled=True)  11 us
    unnamed x7, other arithmetic  7.91 us
    all_to_all x1, starting transfers between devices, on_device(): lax.all_to_all(back_rows, 'ctx', split_axis=1, concat_axis=0, tiled=True)  7.86 us
    ppermute x2, starting transfers between devices, from_behind(): return lax.ppermute(shard, axis, pairs)  7.61 us
  transfers between devices with their start and end apart: 10, of which 5 were waited for; matrix products, arithmetic and copies ran while one was open for 28% of the time, Pallas kernels for 16%

profile of v11, /device:TPU:1, one launch (start us, length us, event | category | flops | bytes accessed | tf_op | source)
XLA Modules:
  0.0 214.3 jit_solution(9982667870592742414)
XLA Ops:
  0.6 1.9 slice.71
  3.9 5.2 %collective-permute-start = (bf16[3,2048,2]{1,2,0:T(2,128)(2,1)}, bf16[3,2048,2]{1,2,0:T(2,128)(2,1)}, u32[]{:S(2)}, u32[]{:S(2)}) collective-permute-start(bf16[3,2048,2]{1,2,0:T(2,128)(2,1)} %copy.102), channel_id=1, source_target_pairs={{0,2},{2,4},{4,6},{6,8},{8,10},{10,12},{12,14},{14,16},{16,18},{18... | collective-permute-start | bytes 73736 | tf_op jit(solution)/shard_map/ppermute | solution.py:18
  9.1 1.9 dynamic-slice_bitcast_fusion
  11.0 6.0 %collective-permute-start.1 = (bf16[2048,128]{1,0:T(8,128)(2,1)}, bf16[2048,128]{1,0:T(8,128)(2,1)}, u32[]{:S(2)}, u32[]{:S(2)}) collective-permute-start(bf16[2048,128]{1,0:T(8,128)(2,1)} %dynamic-slice_bitcast_fusion), channel_id=1, source_target_pairs={{0,1},{1,0},{2,3},{3,2},{4,5},{5,4},{6,7},{7,6},{8,9},{9,8},{10,11... | collective-permute-start | bytes 1572872 | tf_op jit(solution)/shard_map/ppermute | solution.py:340
  27.8 1.8 stack.62.refs_3_.refs_4_
  29.7 2.3 %copy.103 = bf16[3,2048,2]{2,1,0:T(8,128)(2,1)} copy(bf16[3,2048,2]{1,2,0:T(2,128)(2,1)} %collective-permute-done) | data formatting | bytes 49152 | tf_op jit(solution)/shard_map/ppermute | solution.py:18
  31.9 3.3 %maximum_convert_fusion = f32[3,2048,258]{2,1,0:T(8,128)S(1)} fusion(bf16[3,2048,256]{2,1,0:T(8,128)(2,1)S(1)} %bitcast.70, bf16[3,2048,2]{2,1,0:T(8,128)(2,1)} %copy.103), kind=kLoop, calls=%fused_computation.12 | loop fusion | flops 6340608 | bytes 9510912 | tf_op jit(solution)/shard_map/convert_element_type | solution.py:24
  35.3 6.4 %fusion.4 = bf16[3,2048,256]{2,1,0:T(8,128)(2,1)S(1)} fusion(f32[3,2048,258]{2,1,0:T(8,128)S(1)} %maximum_convert_fusion, f32[3,2048]{1,0:T(4,128)S(1)} %get-tuple-element.28, f32[3,2048]{1,0:T(4,128)S(1)} %get-tuple-element.29, f32[3,2048]{1,0:T(4,128)S(1)} %bitcast.81), kind=kLoop, calls=%fused_computation.8 | loop fusion | flops 9437184 | bytes 22093824 | tf_op jit(solution)/shard_map/convert_element_type | solution.py:350
  42.9 7.5 %all-to-all-start = ((bf16[32,64,256]{2,1,0:T(8,128)(2,1)}), bf16[32,64,256]{2,1,0:T(8,128)(2,1)}, u32[]{:S(2)}, u32[]{:S(2)}) async-start(bf16[32,64,256]{2,1,0:T(8,128)(2,1)} %bitcast.75), calls=%async_computation | async-start | bytes 2097152 | tf_op jit(solution)/shard_map/all_to_all | solution.py:361
  57.8 20.6 %all-to-all-done = bf16[32,64,256]{2,1,0:T(8,128)(2,1)} async-done(((bf16[32,64,256]{2,1,0:T(8,128)(2,1)}), bf16[32,64,256]{2,1,0:T(8,128)(2,1)}, u32[]{:S(2)}, u32[]{:S(2)}) %all-to-all-start) | async-done | bytes 1048608 | tf_op jit(solution)/shard_map/all_to_all | solution.py:361
  78.4 4.6 %all-to-all-start.2 = ((bf16[32,64,256]{2,1,0:T(8,128)(2,1)}), bf16[32,64,256]{2,1,0:T(8,128)(2,1)}, u32[]{:S(2)}, u32[]{:S(2)}) async-start(bf16[32,64,256]{2,1,0:T(8,128)(2,1)} %multiply_convert_fusion), calls=%async_computation.2 | async-start | bytes 2097152 | tf_op jit(solution)/shard_map/all_to_all | solution.py:362
  83.0 2.8 %copy.135 = bf16[32,64,256]{2,0,1:T(8,128)(2,1)} copy(bf16[32,64,256]{2,1,0:T(8,128)(2,1)} %all-to-all-done) | data formatting | bytes 2097152 | tf_op jit(solution)/shard_map/all_to_all | solution.py:361
  85.8 11.3 %shard_map.93 = bf16[64,32,256]{2,1,0:T(8,128)(2,1)} custom-call(bf16[64,32,256]{2,1,0:T(8,128)(2,1)} %bitcast.77, f32[64,2,256]{2,1,0:T(2,128)} %pad_maximum_fusion.2.refs_1_.refs_2_, bf16[64,8,16,256]{3,2,1,0:T(8,128)(2,1)} %fusion.16.refs_2_.refs_3_, f32[64,8,16]{2,1,0:T(8,128)} %stack.62.refs_3_.refs_4_), custom_call_target="tpu_custom_call" | custom-call | flops 40265318400 | bytes 6291456 | tf_op jit(solution)/shard_map/pallas_call | solution.py:283
  97.1 2.8 %copy.115 = bf16[64,32,256]{2,0,1:T(8,128)(2,1)} copy(bf16[64,32,256]{2,1,0:T(8,128)(2,1)} %shard_map.93) | data formatting | bytes 2097152 | tf_op jit(solution)/shard_map/pallas_call | solution.py:283
  99.9 11.0 %all-to-all-done.2 = bf16[32,64,256]{2,1,0:T(8,128)(2,1)} async-done(((bf16[32,64,256]{2,1,0:T(8,128)(2,1)}), bf16[32,64,256]{2,1,0:T(8,128)(2,1)}, u32[]{:S(2)}, u32[]{:S(2)}) %all-to-all-start.2) | async-done | bytes 1048608 | tf_op jit(solution)/shard_map/all_to_all | solution.py:362
  111.0 4.6 %all-to-all-start.1 = ((bf16[64,32,256]{2,0,1:T(8,128)(2,1)}), bf16[64,32,256]{2,0,1:T(8,128)(2,1)}, u32[]{:S(2)}, u32[]{:S(2)}) async-start(bf16[64,32,256]{2,0,1:T(8,128)(2,1)} %copy.115), calls=%async_computation.1 | async-start | bytes 2097152 | tf_op jit(solution)/shard_map/all_to_all | solution.py:384
  115.5 2.8 %copy.134 = bf16[32,64,256]{2,0,1:T(8,128)(2,1)} copy(bf16[32,64,256]{2,1,0:T(8,128)(2,1)} %all-to-all-done.2) | data formatting | bytes 2097152 | tf_op jit(solution)/shard_map/all_to_all | solution.py:362
  118.3 23.3 %shard_map.94 = (bf16[64,32,256]{2,1,0:T(8,128)(2,1)}, f32[64,1,16]{2,1,0:T(1,128)}, f32[64,1,128]{2,1,0:T(1,128)}) custom-call(bf16[64,32,256]{2,1,0:T(8,128)(2,1)} %bitcast.78, bf16[64,32,256]{2,1,0:T(8,128)(2,1)} %bitcast.79, f32[64,2,256]{2,1,0:T(2,128)} %pad_maximum_fusion.2.refs_1_.refs_2_, bf16[64,8,16,256]{3,2,1,0:T(8,128)(2,1)} %fusion.16.refs_2_.refs_3_, ...), custom_call_target="tpu_custom_call" | custom-call | flops 67108864000 | bytes 7340032 | tf_op jit(solution)/shard_map/pallas_call | solution.py:294
  141.6 2.8 %copy.117 = bf16[64,32,256]{2,0,1:T(8,128)(2,1)} copy(bf16[64,32,256]{2,1,0:T(8,128)(2,1)} %get-tuple-element.7) | data formatting | bytes 2097152 | tf_op jit(solution)/shard_map/pallas_call | solution.py:294
  144.4 7.9 %all-to-all-start.3 = ((bf16[64,32,256]{2,0,1:T(8,128)(2,1)}), bf16[64,32,256]{2,0,1:T(8,128)(2,1)}, u32[]{:S(2)}, u32[]{:S(2)}) async-start(bf16[64,32,256]{2,0,1:T(8,128)(2,1)} %copy.117), calls=%async_computation.3 | async-start | bytes 2097152 | tf_op jit(solution)/shard_map/all_to_all | solution.py:385
  154.3 1.6 collective-permute-done.3
  156.0 2.9 %collective-permute-start.4 = (f32[64,17]{0,1:T(8,128)S(1)}, f32[64,17]{0,1:T(8,128)S(1)}, u32[]{:S(2)}, u32[]{:S(2)}) collective-permute-start(f32[64,17]{0,1:T(8,128)S(1)} %fusion.24), channel_id=1, source_target_pairs={{0,128},{64,192},{128,0},{192,64},{1,129},{65,193},{129,1},{193,65... | collective-permute-start | bytes 13064 | tf_op jit(solution)/shard_map/ppermute | solution.py:396
  161.2 19.0 %all-to-all-done.3 = bf16[64,32,256]{2,0,1:T(8,128)(2,1)} async-done(((bf16[64,32,256]{2,0,1:T(8,128)(2,1)}), bf16[64,32,256]{2,0,1:T(8,128)(2,1)}, u32[]{:S(2)}, u32[]{:S(2)}) %all-to-all-start.3) | async-done | bytes 1048608 | tf_op jit(solution)/shard_map/all_to_all | solution.py:385
  180.2 3.9 %all-to-all-start.4 = ((f32[32,1,1088]{2,1,0:T(1,128)}), f32[32,1,1088]{2,1,0:T(1,128)S(1)}, u32[]{:S(2)}, u32[]{:S(2)}) async-start(f32[32,1,1088]{2,1,0:T(1,128)} %reshape.224), calls=%async_computation.4 | async-start | bytes 294912 | tf_op jit(solution)/shard_map/all_to_all | solution.py:416
  184.1 3.7 %fusion.9 = (bf16[1,2048,256]{2,1,0:T(8,128)(2,1)S(1)}, bf16[1,2048,256]{2,1,0:T(8,128)(2,1)S(1)}, bf16[1,2048,256]{2,1,0:T(8,128)(2,1)}, bf16[1,2048,256]{2,1,0:T(8,128)(2,1)S(1)}) fusion(bf16[64,32,256]{2,0,1:T(8,128)(2,1)} %all-to-all-done.3, bf16[3,2048,256]{2,1,0:T(8,128)(2,1)S(1)} %fusion.4, bf16[64,32,256]{2,0,1:T(8,128)(2,1)} %all-to-all-done.1, ...), kind=kLoop, calls=%fused_computation.20 | loop fusion | flops 8912896 | bytes 10485760 | tf_op jit(solution)/shard_map/convert.6
  189.4 1.4 pad_maximum_fusion
  190.9 2.5 %copy.118 = bf16[3,2048,2]{1,2,0:T(2,128)(2,1)} copy(bf16[3,2048,2]{2,1,0:T(8,128)(2,1)} %pad_maximum_fusion) | data formatting | bytes 49152 | tf_op jit(solution)/shard_map/slice | solution.py:426
  193.4 2.4 %collective-permute-start.2 = (bf16[3,2048,2]{1,2,0:T(2,128)(2,1)}, bf16[3,2048,2]{1,2,0:T(2,128)(2,1)}, u32[]{:S(2)}, u32[]{:S(2)}) collective-permute-start(bf16[3,2048,2]{1,2,0:T(2,128)(2,1)} %copy.118), channel_id=1, source_target_pairs={{2,0},{4,2},{6,4},{8,6},{10,8},{12,10},{14,12},{16,14},{18,16},{20... | collective-permute-start | bytes 73736 | tf_op jit(solution)/shard_map/ppermute | solution.py:18
  196.3 1.7 reduce.2
  202.1 2.3 %copy.119 = bf16[3,2048,2]{2,1,0:T(8,128)(2,1)} copy(bf16[3,2048,2]{1,2,0:T(2,128)(2,1)} %collective-permute-done.2) | data formatting | bytes 49152 | tf_op jit(solution)/shard_map/ppermute | solution.py:18
  204.4 2.6 %maximum_convert_fusion.1 = f32[3,2048,258]{2,1,0:T(8,128)S(1)} fusion(bf16[3,2048,2]{2,1,0:T(8,128)(2,1)} %copy.119, bf16[1,2048,256]{2,1,0:T(8,128)(2,1)S(1)} %copy-done.3, bf16[1,2048,256]{2,1,0:T(8,128)(2,1)S(1)} %copy-done.1, bf16[1,2048,256]{2,1,0:T(8,128)(2,1)S(1)} %copy-done.5), kind=kLoop, calls=%fused_computation.13 | loop fusion | flops 12681216 | bytes 9510912 | tf_op jit(solution)/shard_map/convert_element_type | solution.py:38
  207.0 7.3 %fusion.6 = bf16[1,3,2048,256]{3,2,1,0:T(8,128)(2,1)} fusion(f32[3,2048,258]{2,1,0:T(8,128)S(1)} %maximum_convert_fusion.1, f32[3,2048]{1,0:T(4,128)S(1)} %copy-done.11, f32[3,2048]{1,0:T(4,128)S(1)} %copy-done.13, f32[3,2048]{1,0:T(4,128)S(1)} %bitcast.82), kind=kLoop, calls=%fused_computation.14 | loop fusion | flops 9437184 | bytes 22093824 | tf_op jit(solution)/shard_map/broadcast_in_dim | solution.py:428
  (87 shorter events, 31.2 us)
Async XLA Ops:
  3.9 28.1 %copy-start.6 = (bf16[1,3,2048,256]{3,2,1,0:T(8,128)(2,1)S(1)}, bf16[1,3,2048,256]{3,2,1,0:T(8,128)(2,1)}, u32[]{:S(2)}) copy-start(bf16[1,3,2048,256]{3,2,1,0:T(8,128)(2,1)} %param.6) | copy-start | bytes 9437188
  3.9 25.8 %collective-permute-start = (bf16[3,2048,2]{1,2,0:T(2,128)(2,1)}, bf16[3,2048,2]{1,2,0:T(2,128)(2,1)}, u32[]{:S(2)}, u32[]{:S(2)}) collective-permute-start(bf16[3,2048,2]{1,2,0:T(2,128)(2,1)} %copy.102), channel_id=1, source_target_pairs={{0,2},{2,4},{4,6},{6,8},{8,10},{10,12},{12,14},{14,16},{16,18},{18... | collective-permute-start | bytes 73736 | tf_op jit(solution)/shard_map/ppermute | solution.py:18
  11.0 43.1 %collective-permute-start.1 = (bf16[2048,128]{1,0:T(8,128)(2,1)}, bf16[2048,128]{1,0:T(8,128)(2,1)}, u32[]{:S(2)}, u32[]{:S(2)}) collective-permute-start(bf16[2048,128]{1,0:T(8,128)(2,1)} %dynamic-slice_bitcast_fusion), channel_id=1, source_target_pairs={{0,1},{1,0},{2,3},{3,2},{4,5},{5,4},{6,7},{7,6},{8,9},{9,8},{10,11... | collective-permute-start | bytes 1572872 | tf_op jit(solution)/shard_map/ppermute | solution.py:340
  24.9 10.3 %copy-start.10 = (f32[3,2048]{1,0:T(4,128)}, f32[3,2048]{1,0:T(4,128)S(1)}, u32[]{:S(2)}) copy-start(f32[3,2048]{1,0:T(4,128)S(1)} %get-tuple-element.28) | copy-start | bytes 73732
  24.9 10.3 %copy-start.12 = (f32[3,2048]{1,0:T(4,128)}, f32[3,2048]{1,0:T(4,128)S(1)}, u32[]{:S(2)}) copy-start(f32[3,2048]{1,0:T(4,128)S(1)} %get-tuple-element.29) | copy-start | bytes 73732
  26.9 8.4 %copy-start.14 = (f32[3,1,2048]{2,0,1:T(4,128)}, f32[3,1,2048]{2,0,1:T(4,128)S(1)}, u32[]{:S(2)}) copy-start(f32[3,1,2048]{2,0,1:T(4,128)S(1)} %copy.136) | copy-start | bytes 73732
  42.9 35.4 %all-to-all-start = ((bf16[32,64,256]{2,1,0:T(8,128)(2,1)}), bf16[32,64,256]{2,1,0:T(8,128)(2,1)}, u32[]{:S(2)}, u32[]{:S(2)}) async-start(bf16[32,64,256]{2,1,0:T(8,128)(2,1)} %bitcast.75), calls=%async_computation | async-start | bytes 2097152 | tf_op jit(solution)/shard_map/all_to_all | solution.py:361
  50.4 3.7 %copy-start.9 = (bf16[1,4096,128]{2,1,0:T(8,128)(2,1)S(1)}, bf16[1,4096,128]{2,1,0:T(8,128)(2,1)}, u32[]{:S(2)}) copy-start(bf16[1,4096,128]{2,1,0:T(8,128)(2,1)} %param.7) | copy-start | bytes 3145732
  55.4 0.8 copy-start.7
  55.4 1.1 copy-start.8
  78.4 32.6 %all-to-all-start.2 = ((bf16[32,64,256]{2,1,0:T(8,128)(2,1)}), bf16[32,64,256]{2,1,0:T(8,128)(2,1)}, u32[]{:S(2)}, u32[]{:S(2)}) async-start(bf16[32,64,256]{2,1,0:T(8,128)(2,1)} %multiply_convert_fusion), calls=%async_computation.2 | async-start | bytes 2097152 | tf_op jit(solution)/shard_map/all_to_all | solution.py:362
  111.0 33.4 %all-to-all-start.1 = ((bf16[64,32,256]{2,0,1:T(8,128)(2,1)}), bf16[64,32,256]{2,0,1:T(8,128)(2,1)}, u32[]{:S(2)}, u32[]{:S(2)}) async-start(bf16[64,32,256]{2,0,1:T(8,128)(2,1)} %copy.115), calls=%async_computation.1 | async-start | bytes 2097152 | tf_op jit(solution)/shard_map/all_to_all | solution.py:384
  141.6 10.7 %copy-start.16 = (f32[64,1,16]{2,1,0:T(1,128)S(1)}, f32[64,1,16]{2,1,0:T(1,128)}, u32[]{:S(2)}) copy-start(f32[64,1,16]{2,1,0:T(1,128)} %get-tuple-element.8) | copy-start | bytes 12292
  141.6 10.8 %copy-start.17 = (f32[64,1,128]{2,1,0:T(1,128)S(1)}, f32[64,1,128]{2,1,0:T(1,128)}, u32[]{:S(2)}) copy-start(f32[64,1,128]{2,1,0:T(1,128)} %get-tuple-element.9) | copy-start | bytes 98308
  144.4 35.8 %all-to-all-start.3 = ((bf16[64,32,256]{2,0,1:T(8,128)(2,1)}), bf16[64,32,256]{2,0,1:T(8,128)(2,1)}, u32[]{:S(2)}, u32[]{:S(2)}) async-start(bf16[64,32,256]{2,0,1:T(8,128)(2,1)} %copy.117), calls=%async_computation.3 | async-start | bytes 2097152 | tf_op jit(solution)/shard_map/all_to_all | solution.py:385
  152.9 3.0 %collective-permute-start.3 = (f32[64,17]{0,1:T(8,128)S(1)}, f32[64,17]{0,1:T(8,128)S(1)}, u32[]{:S(2)}, u32[]{:S(2)}) collective-permute-start(f32[64,17]{0,1:T(8,128)S(1)} %pad_maximum_fusion.3), channel_id=1, source_target_pairs={{0,64},{64,0},{128,192},{192,128},{1,65},{65,1},{129,193},{193,129... | collective-permute-start | bytes 13064 | tf_op jit(solution)/shard_map/ppermute | solution.py:396
  156.0 4.3 %collective-permute-start.4 = (f32[64,17]{0,1:T(8,128)S(1)}, f32[64,17]{0,1:T(8,128)S(1)}, u32[]{:S(2)}, u32[]{:S(2)}) collective-permute-start(f32[64,17]{0,1:T(8,128)S(1)} %fusion.24), channel_id=1, source_target_pairs={{0,128},{64,192},{128,0},{192,64},{1,129},{65,193},{129,1},{193,65... | collective-permute-start | bytes 13064 | tf_op jit(solution)/shard_map/ppermute | solution.py:396
  180.2 15.6 %all-to-all-start.4 = ((f32[32,1,1088]{2,1,0:T(1,128)}), f32[32,1,1088]{2,1,0:T(1,128)S(1)}, u32[]{:S(2)}, u32[]{:S(2)}) async-start(f32[32,1,1088]{2,1,0:T(1,128)} %reshape.224), calls=%async_computation.4 | async-start | bytes 294912 | tf_op jit(solution)/shard_map/all_to_all | solution.py:416
  187.8 1.0 copy-start
  187.8 1.3 copy-start.2
  187.8 1.6 copy-start.4
  190.9 13.5 %copy-start.1 = (bf16[1,2048,256]{2,1,0:T(8,128)(2,1)S(1)}, bf16[1,2048,256]{2,1,0:T(8,128)(2,1)}, u32[]{:S(2)}) copy-start(bf16[1,2048,256]{2,1,0:T(8,128)(2,1)} %copy-done) | copy-start | bytes 3145732
  190.9 13.5 %copy-start.3 = (bf16[1,2048,256]{2,1,0:T(8,128)(2,1)S(1)}, bf16[1,2048,256]{2,1,0:T(8,128)(2,1)}, u32[]{:S(2)}) copy-start(bf16[1,2048,256]{2,1,0:T(8,128)(2,1)} %copy-done.2) | copy-start | bytes 3145732
  190.9 13.5 %copy-start.5 = (bf16[1,2048,256]{2,1,0:T(8,128)(2,1)S(1)}, bf16[1,2048,256]{2,1,0:T(8,128)(2,1)}, u32[]{:S(2)}) copy-start(bf16[1,2048,256]{2,1,0:T(8,128)(2,1)} %copy-done.4) | copy-start | bytes 3145732
  193.4 8.7 %collective-permute-start.2 = (bf16[3,2048,2]{1,2,0:T(2,128)(2,1)}, bf16[3,2048,2]{1,2,0:T(2,128)(2,1)}, u32[]{:S(2)}, u32[]{:S(2)}) collective-permute-start(bf16[3,2048,2]{1,2,0:T(2,128)(2,1)} %copy.118), channel_id=1, source_target_pairs={{2,0},{4,2},{6,4},{8,6},{10,8},{12,10},{14,12},{16,14},{18,16},{20... | collective-permute-start | bytes 73736 | tf_op jit(solution)/shard_map/ppermute | solution.py:18
  204.4 2.6 %copy-start.11 = (f32[3,2048]{1,0:T(4,128)S(1)}, f32[3,2048]{1,0:T(4,128)}, u32[]{:S(2)}) copy-start(f32[3,2048]{1,0:T(4,128)} %copy-done.10) | copy-start | bytes 73732
  204.4 2.6 %copy-start.13 = (f32[3,2048]{1,0:T(4,128)S(1)}, f32[3,2048]{1,0:T(4,128)}, u32[]{:S(2)}) copy-start(f32[3,2048]{1,0:T(4,128)} %copy-done.12) | copy-start | bytes 73732
  204.4 2.6 %copy-start.15 = (f32[3,1,2048]{2,0,1:T(4,128)S(1)}, f32[3,1,2048]{2,0,1:T(4,128)}, u32[]{:S(2)}) copy-start(f32[3,1,2048]{2,0,1:T(4,128)} %copy-done.14) | copy-start | bytes 73732
